TPU v7x, 128 devices: a whole 4x4x4 slice. The times are simulated.
128 devices in a mesh: row: 8 (over y, core), col: 16 (over x, z).
Axes of the slice: x: 4, y: 4, z: 4, core: 2. Of those that a mesh axis runs over, the one named last changes fastest.
Arguments:
- occ_coeffs: bfloat16 [49152, 20480], P('row', 'col'), may hold values from -0.21875 to 0.21875
- colloc: bfloat16 [1024, 1024, 512], P(('row', 'col')), may hold values from -6 to 6
- grid_points: float32 [1024, 3, 512], P(('row', 'col')), may hold values from -4 to 4
- grid_weights: float32 [1024, 512], P(('row', 'col')), may hold values from 0.01 to 0.1
- charge_sites: float32 [3, 512], replicated, may hold values from -4 to 4
- charge_proj: bfloat16 [512, 128], replicated, may hold values from -0.5 to 0.5
- shell_lists: int32 [1024, 16], P(('row', 'col')), may hold values from 0 to 767, as said below
- point_counts: int32 [1024], P(('row', 'col')), may hold values from 1 to 512, as said below
Outputs:
- exchange_slab: float32 [49152, 128], P(('row', 'col'))
Inputs may be any that keep to these rules, and one draw needn't show every extreme that they name: `shell_lists`: batches b * 8 to b * 8 + 7 belong to the b-th device in row+col order, and the blocks named by one device's batches are all different. Owner device o holds blocks o * 6 to o * 6 + 5; one device's batches name at most 2 blocks of one owner, and in every draw one owner gets exactly 2 from every device. `point_counts`: points of a batch beyond its count are not part of it.
All inputs are finite; a program needn't handle non-finite values.
Results may differ from a plain program's by a relative error of at most 0.0045.
Values may be sent and summed in bfloat16 or wider, within the bound.
No kernel may reach another device: no remote copies, remote signals or barrier semaphores. Data moves between devices by JAX's collectives and lax.ppermute only.
A program may use at most 128 MiB of HBM per device.

v0:
```python
import jax
import jax.numpy as jnp
from jax import lax
from jax.sharding import PartitionSpec as P

SH = 64
NSIG = 16


smear_sq = 0.25


def from_root(value, axis, source):
    kept = jnp.where(lax.axis_index(axis) == source, value, 0).astype(value.dtype)
    return lax.psum(kept, axis)


def potential(points, charge_sites):
    dist_sq = (points[0][None, :] - charge_sites[0][:, None]) ** 2
    dist_sq = dist_sq + (points[1][None, :] - charge_sites[1][:, None]) ** 2
    dist_sq = dist_sq + (points[2][None, :] - charge_sites[2][:, None]) ** 2
    return lax.rsqrt(dist_sq + smear_sq)


def batch_terms(
    dens_rows, colloc, grid_points, grid_weights, charge_sites, charge_proj, point_counts
):
    slab_width = charge_proj.shape[1]
    total_points = colloc.shape[2]
    block_points = min(256, total_points)
    func_rows = colloc.shape[1]

    def one_batch(carry, item):
        batch_rows, batch_colloc, batch_points, batch_weights, count = item
        blocks_used = (count + block_points - 1) // block_points

        def point_block(index, accumulated):
            start = index * block_points
            values = lax.dynamic_slice_in_dim(batch_colloc, start, block_points, 1)
            points = lax.dynamic_slice_in_dim(batch_points, start, block_points, 1)
            weights = lax.dynamic_slice_in_dim(batch_weights, start, block_points, 0)
            live = (start + jnp.arange(block_points) < count).astype(jnp.float32)
            field = lax.dot_general(
                batch_rows, values, (((0,), (0,)), ((), ())), preferred_element_type=jnp.float32
            ).astype(jnp.bfloat16)
            projected = jnp.dot(charge_proj, field, preferred_element_type=jnp.float32)
            charges = (
                projected * potential(points, charge_sites) * (weights * live)[None, :]
            ).astype(jnp.bfloat16)
            spread_back = lax.dot_general(
                charge_proj, charges, (((0,), (0,)), ((), ())), preferred_element_type=jnp.float32
            ).astype(jnp.bfloat16)
            return accumulated + lax.dot_general(
                values, spread_back, (((1,), (1,)), ((), ())), preferred_element_type=jnp.float32
            )

        start_value = jnp.zeros((func_rows, slab_width), jnp.float32)
        return (carry, lax.fori_loop(0, blocks_used, point_block, start_value))

    _, terms = lax.scan(one_batch, 0, (dens_rows, colloc, grid_points, grid_weights, point_counts))
    return terms


def on_device(
    occ_coeffs,
    colloc,
    grid_points,
    grid_weights,
    charge_sites,
    charge_proj,
    shell_lists,
    point_counts,
):
    row_count = lax.axis_size("row")
    col_count = lax.axis_size("col")
    owners = row_count * col_count
    group_rows = occ_coeffs.shape[0]
    slab_width = charge_proj.shape[1]
    own_rows = group_rows // col_count
    own_blocks = own_rows // SH
    window = from_root(occ_coeffs[:slab_width], "row", 0)
    requested = shell_lists.reshape(-1)
    request_count = requested.shape[0]
    capacity = 2 * request_count // owners
    owner = requested // own_blocks
    onehot = (owner[:, None] == jnp.arange(owners)[None, :]).astype(jnp.int32)
    before = jnp.cumsum(onehot, axis=0) - onehot
    rank = jnp.sum(before * onehot, axis=1)
    slot = owner * capacity + rank
    empty_ids = jnp.full((owners * capacity,), -1, jnp.int32)
    density = lax.psum_scatter(
        lax.dot_general(
            occ_coeffs, window, (((1,), (1,)), ((), ())), preferred_element_type=jnp.float32
        ),
        "col",
        scatter_dimension=0,
        tiled=True,
    ).astype(jnp.bfloat16)
    store = density.reshape(own_blocks, SH, slab_width)
    wanted = empty_ids.at[slot].set(requested % own_blocks).reshape(owners, capacity)
    received_ids = lax.all_to_all(wanted, ("row", "col"), split_axis=0, concat_axis=0, tiled=True)
    found = store[jnp.maximum(received_ids, 0)]
    replies, received_ids = (
        lax.all_to_all(found, ("row", "col"), split_axis=0, concat_axis=0, tiled=True),
        received_ids,
    )
    fetched = replies.reshape(owners * capacity, SH, slab_width)[slot]
    dens_rows = fetched.reshape(shell_lists.shape[0], NSIG * SH, slab_width)
    terms = batch_terms(
        dens_rows, colloc, grid_points, grid_weights, charge_sites, charge_proj, point_counts
    )
    tiles = (
        jnp.zeros((owners * capacity, SH, slab_width), jnp.float32)
        .at[slot]
        .set(terms.reshape(request_count, SH, slab_width))
    )
    tiles = tiles.reshape(wanted.shape + (SH, slab_width))
    arrived = lax.all_to_all(tiles, ("row", "col"), split_axis=0, concat_axis=0, tiled=True)
    flat_ids = received_ids.reshape(-1)
    selector = (jnp.arange(store.shape[0])[:, None] == flat_ids[None, :]).astype(jnp.float32)
    summed = jnp.dot(
        selector,
        arrived.reshape(flat_ids.shape[0], SH * slab_width),
        precision=lax.Precision.HIGHEST,
        preferred_element_type=jnp.float32,
    )
    return summed.reshape(own_rows, slab_width)


def solution(mesh):
    placed = (
        P("row", "col"),
        P(("row", "col"), None, None),
        P(("row", "col"), None, None),
        P(("row", "col"), None),
        P(),
        P(),
        P(("row", "col"), None),
        P(("row", "col")),
    )
    return jax.shard_map(
        on_device, mesh=mesh, in_specs=placed, out_specs=P(("row", "col"), None), check_vma=False
    )
```

profile of v0, /device:TPU:1, one launch (start us, length us, event | category | flops | bytes accessed | tf_op | source)
XLA Modules:
  0.0 452.6 jit_solution(184304201707396558)
XLA Ops:
  6.5 1.7 slice_select_fusion
  8.3 62.7 %all-reduce.2.cloned.1.call-done = bf16[128,1280]{1,0:T(8,128)(2,1)} async-done(((bf16[128,1280]{1,0:T(8,128)(2,1)}), bf16[128,1280]{1,0:T(8,128)(2,1)}) %all-reduce.2.cloned.1.call-update) | async-done | bytes 327696 | tf_op jit(solution)/shard_map/psum | solution.py:15
  71.0 12.4 %convolution_bitcast_fusion.1 = f32[6144,128]{0,1:T(8,128)} fusion(bf16[128,1280]{1,0:T(8,128)(2,1)} %all-reduce.2.cloned.1.call-done, bf16[6144,1280]{1,0:T(8,128)(2,1)} %param.12), kind=kOutput, calls=%fused_computation.46 | convolution fusion | flops 2013265920 | bytes 19202048 | tf_op jit(solution)/shard_map/dot_general | solution.py:92
  84.3 1.0 scatter_custom_fusion
  85.5 18.8 %all_to_all.19 = s32[128,1,2]{2,1,0:T(1,128)S(1)} all-to-all(s32[128,1,2]{2,1,0:T(1,128)S(1)} %bitcast.106), channel_id=1, replica_groups=mesh['row'=8,'col'=16] {'row','col'}, dimensions={0} | all-to-all | bytes 2048 | tf_op jit(solution)/shard_map/all_to_all | solution.py:101
  104.7 1.0 fusion.38
  105.9 53.0 %reduce-scatter.2.cloned.1.call-done = f32[384,128]{0,1:T(8,128)} async-done(((f32[6144,128]{0,1:T(8,128)}), f32[384,128]{0,1:T(8,128)}) %reduce-scatter.2.cloned.1.call-update) | async-done | bytes 196624 | tf_op jit(solution)/shard_map/reduce_scatter | solution.py:91
  158.9 0.9 convert_element_type.22
  160.0 3.1 gather_fusion
  163.0 9.6 %all-to-all-start.1 = ((bf16[128,2,64,128]{3,2,1,0:T(8,128)(2,1)}), bf16[128,2,64,128]{3,2,1,0:T(8,128)(2,1)}, u32[]{:S(2)}, u32[]{:S(2)}) async-start(bf16[128,2,64,128]{3,2,1,0:T(8,128)(2,1)} %bitcast.96), calls=%async_computation.2 | async-start | bytes 8388608 | tf_op jit(solution)/shard_map/all_to_all | solution.py:104
  172.7 52.0 %all-to-all-done.1 = bf16[128,2,64,128]{3,2,1,0:T(8,128)(2,1)} async-done(((bf16[128,2,64,128]{3,2,1,0:T(8,128)(2,1)}), bf16[128,2,64,128]{3,2,1,0:T(8,128)(2,1)}, u32[]{:S(2)}, u32[]{:S(2)}) %all-to-all-start.1) | async-done | bytes 4194336 | tf_op jit(solution)/shard_map/all_to_all | solution.py:104
  224.7 4.3 gather_fusion.1
  229.0 63.5 %while.47 = (s32[]{:T(128)}, f32[8,1024,128]{2,1,0:T(8,128)}, s32[8]{0:T(128)S(1)}, bf16[8,1024,512]{2,1,0:T(8,128)(2,1)}, f32[8,3,512]{2,0,1:T(8,128)}, /*index...) while((s32[]{:T(128)}, f32[8,1024,128]{2,1,0:T(8,128)}, ...), condition=%wide.region_8.9_spmd, body=%wide.region_5.8_spmd.sunk | while | flops 203096848 | bytes 7007006 | solution.py:60
  231.9 1.0 dynamic-slice_bitcast_fusion.5
  232.9 1.3 dynamic-slice_bitcast_fusion.4
  234.2 1.9 while.48
  236.1 0.9 bitcast_dynamic-update-slice_fusion.2
  239.8 1.0 dynamic-slice_bitcast_fusion.5
  240.8 1.3 dynamic-slice_bitcast_fusion.4
  242.2 1.9 while.48
  244.1 0.9 bitcast_dynamic-update-slice_fusion.2
  247.8 1.0 dynamic-slice_bitcast_fusion.5
  248.8 1.3 dynamic-slice_bitcast_fusion.4
  250.2 1.9 while.48
  252.1 0.8 bitcast_dynamic-update-slice_fusion.2
  255.7 1.0 dynamic-slice_bitcast_fusion.5
  256.7 1.3 dynamic-slice_bitcast_fusion.4
  258.1 1.9 while.48
  263.6 1.0 dynamic-slice_bitcast_fusion.5
  264.6 1.3 dynamic-slice_bitcast_fusion.4
  266.0 1.9 while.48
  267.9 0.9 bitcast_dynamic-update-slice_fusion.2
  271.6 1.0 dynamic-slice_bitcast_fusion.5
  272.6 1.3 dynamic-slice_bitcast_fusion.4
  273.9 1.9 while.48
  275.9 0.8 bitcast_dynamic-update-slice_fusion.2
  279.5 1.0 dynamic-slice_bitcast_fusion.5
  280.5 1.3 dynamic-slice_bitcast_fusion.4
  281.9 1.9 while.48
  287.4 1.0 dynamic-slice_bitcast_fusion.5
  288.4 1.3 dynamic-slice_bitcast_fusion.4
  289.8 1.9 while.48
  291.7 0.9 bitcast_dynamic-update-slice_fusion.2
  292.6 4.3 broadcast_in_dim.33
  296.8 19.7 %scatter_fusion = f32[256,64,128]{2,1,0:T(8,128)} fusion(f32[256,64,128]{2,1,0:T(8,128)} %broadcast_in_dim.33, s32[128]{0:T(128)S(1)} %fusion.35, f32[128,64,128]{2,1,0:T(8,128)} %bitcast.97), kind=kCustom, calls=%fused_computation.3 | custom fusion | bytes 12583424 | tf_op jit(solution)/shard_map/scatter | solution.py:115
  316.6 16.7 %all-to-all-start.2 = ((f32[128,2,64,128]{3,2,1,0:T(8,128)}), f32[128,2,64,128]{3,2,1,0:T(8,128)}, u32[]{:S(2)}, u32[]{:S(2)}) async-start(f32[128,2,64,128]{3,2,1,0:T(8,128)} %bitcast.95), calls=%async_computation.3 | async-start | bytes 16777216 | tf_op jit(solution)/shard_map/all_to_all | solution.py:118
  333.4 101.2 %all-to-all-done.2 = f32[128,2,64,128]{3,2,1,0:T(8,128)} async-done(((f32[128,2,64,128]{3,2,1,0:T(8,128)}), f32[128,2,64,128]{3,2,1,0:T(8,128)}, u32[]{:S(2)}, u32[]{:S(2)}) %all-to-all-start.2) | async-done | bytes 8388640 | tf_op jit(solution)/shard_map/all_to_all | solution.py:118
  434.6 10.4 %fusion.28 = f32[6,8192]{1,0:T(8,128)S(1)} fusion(f32[32,8,64,128]{3,2,1,0:T(8,128)} %bitcast.24, s32[256]{0:T(256)S(1)} %eq.37), kind=kOutput, calls=%fused_computation.43 | convolution fusion | flops 150996480 | bytes 8586240 | tf_op jit(solution)/shard_map/dot_general | solution.py:121
  (123 shorter events, 37.1 us)
Async XLA Ops:
  6.5 64.5 %all-reduce.2.cloned.1.call-start = ((), (), s32[]{:S(2)}) async-start(), calls=%async_computation.4 | async-start | bytes 655360 | tf_op jit(solution)/shard_map/psum | solution.py:15
  8.3 75.1 %copy-start.1 = (s32[8,16]{1,0:T(8,128)S(1)}, s32[8,16]{1,0:T(8,128)}, u32[]{:S(2)}) copy-start(s32[8,16]{1,0:T(8,128)} %param.18) | copy-start | bytes 1540
  8.3 150.6 %reduce-scatter.2.cloned.1.call-start = ((), (), s32[]{:S(2)}) async-start(), calls=%async_computation.5 | async-start | bytes 3342336 | tf_op jit(solution)/shard_map/reduce_scatter | solution.py:91
  163.0 61.7 %all-to-all-start.1 = ((bf16[128,2,64,128]{3,2,1,0:T(8,128)(2,1)}), bf16[128,2,64,128]{3,2,1,0:T(8,128)(2,1)}, u32[]{:S(2)}, u32[]{:S(2)}) async-start(bf16[128,2,64,128]{3,2,1,0:T(8,128)(2,1)} %bitcast.96), calls=%async_computation.2 | async-start | bytes 8388608 | tf_op jit(solution)/shard_map/all_to_all | solution.py:104
  172.6 56.4 %copy-start = (f32[3,512]{1,0:T(4,128)S(1)}, f32[3,512]{1,0:T(4,128)}, u32[]{:S(2)}) copy-start(f32[3,512]{1,0:T(4,128)} %param.16) | copy-start | bytes 18436
  172.6 56.4 %copy-start.2 = (bf16[512,128]{1,0:T(8,128)(2,1)S(1)}, bf16[512,128]{1,0:T(8,128)(2,1)}, u32[]{:S(2)}) copy-start(bf16[512,128]{1,0:T(8,128)(2,1)} %param.17) | copy-start | bytes 393220
  172.6 56.4 %copy-start.3 = (s32[8]{0:T(128)S(1)}, s32[8]{0:T(128)}, u32[]{:S(2)}) copy-start(s32[8]{0:T(128)} %param.19) | copy-start | bytes 100
  316.6 118.0 %all-to-all-start.2 = ((f32[128,2,64,128]{3,2,1,0:T(8,128)}), f32[128,2,64,128]{3,2,1,0:T(8,128)}, u32[]{:S(2)}, u32[]{:S(2)}) async-start(f32[128,2,64,128]{3,2,1,0:T(8,128)} %bitcast.95), calls=%async_computation.3 | async-start | bytes 16777216 | tf_op jit(solution)/shard_map/all_to_all | solution.py:118
Sparse Core Ops, SparseCore 0:
  9.7 61.2 all-reduce.1
  83.5 75.3 reduce-scatter.1
where the time goes:
time: 458 us; the launch traced here: 453 us
  waiting for transfers between devices  269 us (59%)
  local copies, waits for them, and re-layouts  77.8 us (17%)
  matrix products  31.6 us (7%)
  starting transfers between devices  26.3 us (6%)
  blocking collectives  18.8 us (4%)
  between operations  13.6 us (3%)
  other arithmetic  9.81 us (2%)
  loops' own time  5.88 us (1%)
    all_to_all x1, waiting for transfers between devices, on_device(): lax.all_to_all(tiles, ('row', 'col'), split_axis=0, concat_axis=0, tiled=...  101 us
    psum x1, waiting for transfers between devices, from_root(): return lax.psum(kept, axis)  62.7 us
    reduce_scatter x1, waiting for transfers between devices, on_device(): lax.psum_scatter(lax.dot_general(occ_coeffs, window, (((1,), (1,)), ((),...  53 us
    all_to_all x1, waiting for transfers between devices, on_device(): lax.all_to_all(found, ('row', 'col'), split_axis=0, concat_axis=0, tiled=...  52 us
    scatter x1, local copies, waits for them, and re-layouts, on_device(): tiles = jnp.zeros((owners * capacity, SH, slab_width), jnp.float32).at[sl...  19.7 us
    all_to_all x1, blocking collectives, on_device(): lax.all_to_all(wanted, ('row', 'col'), split_axis=0, concat_axis=0, tiled...  18.8 us
    squeeze x16, local copies, waits for them, and re-layouts, batch_terms(): lax.scan(one_batch, 0, (dens_rows, colloc, grid_points, grid_weights, poi...  18.2 us
    dynamic_slice x32, local copies, waits for them, and re-layouts, batch_terms(): lax.scan(one_batch, 0, (dens_rows, colloc, grid_points, grid_weights, poi...  17.2 us
  transfers between devices with their start and end apart: 4, of which 4 were waited for; matrix products, arithmetic and copies ran while one was open for 1% of the time, Pallas kernels for 0%

commit v1 on v0

v1 whole, which is shorter than its diff:
```python
import jax
import jax.numpy as jnp
from jax import lax
from jax.sharding import PartitionSpec as P

SH = 64
NSIG = 16


smear_sq = 0.25


def broadcast_from_first(value, axis):
    size = lax.axis_size(axis)
    index = lax.axis_index(axis)
    have = 1
    while have < size:
        pairs = [(src, src + have) for src in range(have) if src + have < size]
        moved = lax.ppermute(value, axis, pairs)
        value = jnp.where(index >= have, moved, value)
        have *= 2
    return value


def potential(points, charge_sites):
    dist_sq = (points[:, 0][:, None, :] - charge_sites[0][None, :, None]) ** 2
    dist_sq = dist_sq + (points[:, 1][:, None, :] - charge_sites[1][None, :, None]) ** 2
    dist_sq = dist_sq + (points[:, 2][:, None, :] - charge_sites[2][None, :, None]) ** 2
    return lax.rsqrt(dist_sq + smear_sq)


def batch_terms(dens_rows, colloc, grid_points, grid_weights, charge_sites, charge_proj, point_counts):
    total_points = colloc.shape[2]
    field = jnp.einsum(
        "bfs,bfp->bsp", dens_rows, colloc, preferred_element_type=jnp.float32
    ).astype(jnp.bfloat16)
    projected = jnp.einsum("ks,bsp->bkp", charge_proj, field, preferred_element_type=jnp.float32)
    live = (jnp.arange(total_points)[None, :] < point_counts[:, None]).astype(jnp.float32)
    charges = (
        projected * potential(grid_points, charge_sites) * (grid_weights * live)[:, None, :]
    ).astype(jnp.bfloat16)
    spread_back = jnp.einsum(
        "ks,bkp->bsp", charge_proj, charges, preferred_element_type=jnp.float32
    ).astype(jnp.bfloat16)
    return jnp.einsum("bfp,bsp->bfs", colloc, spread_back, preferred_element_type=jnp.float32)


def on_device(
    occ_coeffs,
    colloc,
    grid_points,
    grid_weights,
    charge_sites,
    charge_proj,
    shell_lists,
    point_counts,
):
    row_count = lax.axis_size("row")
    col_count = lax.axis_size("col")
    owners = row_count * col_count
    me = lax.axis_index("row") * col_count + lax.axis_index("col")
    group_rows = occ_coeffs.shape[0]
    slab_width = charge_proj.shape[1]
    own_rows = group_rows // col_count
    own_blocks = own_rows // SH
    tile = SH * slab_width

    all_lists = lax.all_gather(shell_lists, ("row", "col"), tiled=True)
    window = broadcast_from_first(occ_coeffs[:slab_width], "row")

    requested = shell_lists.reshape(-1)
    request_count = requested.shape[0]
    capacity = 2 * request_count // owners
    slots = owners * capacity
    owner = requested // own_blocks
    onehot = (owner[:, None] == jnp.arange(owners)[None, :]).astype(jnp.int32)
    before = jnp.cumsum(onehot, axis=0) - onehot
    rank = jnp.sum(before * onehot, axis=1)
    slot = owner * capacity + rank
    pick = (slot[:, None] == jnp.arange(slots)[None, :]).astype(jnp.bfloat16)

    lists = all_lists.reshape(owners, request_count)
    mine = (lists // own_blocks == me).astype(jnp.int32)
    order = jnp.cumsum(mine, axis=1)
    local = lists % own_blocks
    wanted_by = []
    for place in range(capacity):
        hit = mine * (order == place + 1)
        wanted_by.append(
            jnp.sum(hit * (local + 1), axis=1) - 1
        )
    received_ids = jnp.stack(wanted_by, axis=1).reshape(-1)
    serve = (received_ids[:, None] == jnp.arange(own_blocks)[None, :]).astype(jnp.bfloat16)

    density = lax.psum_scatter(
        lax.dot_general(
            occ_coeffs, window, (((1,), (1,)), ((), ())), preferred_element_type=jnp.float32
        ),
        "col",
        scatter_dimension=0,
        tiled=True,
    ).astype(jnp.bfloat16)
    store = density.reshape(own_blocks, tile)
    found = jnp.dot(serve, store, preferred_element_type=jnp.float32).astype(jnp.bfloat16)
    replies = lax.all_to_all(
        found.reshape(owners, capacity, tile), ("row", "col"), split_axis=0, concat_axis=0, tiled=True
    )
    fetched = jnp.dot(
        pick, replies.reshape(slots, tile), preferred_element_type=jnp.float32
    ).astype(jnp.bfloat16)
    dens_rows = fetched.reshape(shell_lists.shape[0], NSIG * SH, slab_width)
    terms = batch_terms(
        dens_rows, colloc, grid_points, grid_weights, charge_sites, charge_proj, point_counts
    )
    terms = terms.astype(jnp.bfloat16).reshape(request_count, tile)
    tiles = lax.dot_general(
        pick, terms, (((0,), (0,)), ((), ())), preferred_element_type=jnp.float32
    ).astype(jnp.bfloat16)
    arrived = lax.all_to_all(
        tiles.reshape(owners, capacity, tile), ("row", "col"), split_axis=0, concat_axis=0, tiled=True
    )
    summed = lax.dot_general(
        serve, arrived.reshape(slots, tile), (((0,), (0,)), ((), ())), preferred_element_type=jnp.float32
    )
    return summed.reshape(own_rows, slab_width)


def solution(mesh):
    placed = (
        P("row", "col"),
        P(("row", "col"), None, None),
        P(("row", "col"), None, None),
        P(("row", "col"), None),
        P(),
        P(),
        P(("row", "col"), None),
        P(("row", "col")),
    )
    return jax.shard_map(
        on_device, mesh=mesh, in_specs=placed, out_specs=P(("row", "col"), None), check_vma=False
    )
```

time: 458 us -> 321 us (0.70)
  waiting for transfers between devices: 269 us -> 83.9 us
  blocking collectives: 18.8 us -> 119 us
  local copies, waits for them, and re-layouts: 77.8 us -> 41.7 us
  starting transfers between devices: 26.3 us -> 13.5 us
  matrix products: 31.6 us -> 43.3 us
  loops' own time: 5.88 us -> 0 us
  other arithmetic: 9.81 us -> 4.28 us
    all_to_all x2 -> x1, waiting for transfers between devices: 153 us -> 51.3 us  [on_device(): lax.all_to_all(found.reshape(owners, capacity, tile), ('row', 'col'), spl...]
    psum x1 -> x0, waiting for transfers between devices: 62.7 us -> none  [from_root(): return lax.psum(kept, axis)]
    all_gather x0 -> x1, blocking collectives: none -> 61.2 us  [on_device(): all_lists = lax.all_gather(shell_lists, ('row', 'col'), tiled=True)]
    all_to_all x1, blocking collectives: 18.8 us -> 57.6 us  [on_device(): lax.all_to_all(tiles.reshape(owners, capacity, tile), ('row', 'col'), spl...]
    reduce_scatter x1, waiting for transfers between devices: 53 us -> 17.2 us  [on_device(): lax.psum_scatter(lax.dot_general(occ_coeffs, window, (((1,), (1,)), ((),...]
    reshape x0 -> x7, local copies, waits for them, and re-layouts: none -> 35.5 us  [the longest x1 7.62 us: on_device(): found.reshape(owners, capacity, tile)]
    scatter x2 -> x0, local copies, waits for them, and re-layouts: 20.7 us -> none  [the longest x1 19.7 us: on_device(): tiles = jnp.zeros((owners * capacity, SH, slab_width), jnp.float32).at[sl...]
    squeeze x16 -> x0, local copies, waits for them, and re-layouts: 18.2 us -> none  [batch_terms(): lax.scan(one_batch, 0, (dens_rows, colloc, grid_points, grid_weights, poi...]
  transfers between devices with their start and end apart: 4 -> 5, of which waited for: 4 -> 5; matrix products, arithmetic and copies ran while one was open for 1% -> 1% of each run, Pallas kernels for 0% -> 0%
where the time goes in v1:
time: 321 us; the launch traced here: 319 us
  blocking collectives  119 us (37%)
  waiting for transfers between devices  83.9 us (26%)
  matrix products  43.3 us (13%)
  local copies, waits for them, and re-layouts  41.7 us (13%)
  between operations  13.7 us (4%)
  starting transfers between devices  13.5 us (4%)
  other arithmetic  4.28 us (1%)
    all_gather x1, blocking collectives, on_device(): all_lists = lax.all_gather(shell_lists, ('row', 'col'), tiled=True)  61.2 us
    all_to_all x1, blocking collectives, on_device(): lax.all_to_all(tiles.reshape(owners, capacity, tile), ('row', 'col'), spl...  57.6 us
    all_to_all x1, waiting for transfers between devices, on_device(): lax.all_to_all(found.reshape(owners, capacity, tile), ('row', 'col'), spl...  51.3 us
    reduce_scatter x1, waiting for transfers between devices, on_device(): lax.psum_scatter(lax.dot_general(occ_coeffs, window, (((1,), (1,)), ((),...  17.2 us
    ppermute x3, waiting for transfers between devices, broadcast_from_first(): moved = lax.ppermute(value, axis, pairs)  15.4 us
    dot_general x1, matrix products, on_device(): lax.dot_general(occ_coeffs, window, (((1,), (1,)), ((), ())), preferred_e...  12.3 us
    all_to_all x1, starting transfers between devices, on_device(): lax.all_to_all(found.reshape(owners, capacity, tile), ('row', 'col'), spl...  9.57 us
    reshape x1, local copies, waits for them, and re-layouts, on_device(): found.reshape(owners, capacity, tile)  7.62 us
  transfers between devices with their start and end apart: 5, of which 5 were waited for; matrix products, arithmetic and copies ran while one was open for 1% of the time, Pallas kernels for 0%

profile of v1, /device:TPU:1, one launch (start us, length us, event | category | flops | bytes accessed | tf_op | source)
XLA Modules:
  0.0 319.2 jit_solution(13722545505886730577)
XLA Ops:
  6.5 1.0 slice.21
  7.6 1.3 collective-permute-start
  8.9 2.5 collective-permute-done
  11.4 1.0 broadcast_select_fusion
  12.4 1.3 collective-permute-start.1
  13.7 6.8 %collective-permute-done.1 = bf16[128,1280]{1,0:T(8,128)(2,1)S(1)} collective-permute-done((bf16[128,1280]{1,0:T(8,128)(2,1)S(1)}, bf16[128,1280]{1,0:T(8,128)(2,1)S(1)}, u32[]{:S(2)}, u32[]{:S(2)}) %collective-permute-start.1) | collective-permute-done | bytes 327712 | tf_op jit(solution)/shard_map/ppermute | solution.py:19
  20.5 1.3 collective-permute-start.2
  21.9 6.1 %collective-permute-done.2 = bf16[128,1280]{1,0:T(8,128)(2,1)S(1)} collective-permute-done((bf16[128,1280]{1,0:T(8,128)(2,1)S(1)}, bf16[128,1280]{1,0:T(8,128)(2,1)S(1)}, u32[]{:S(2)}, u32[]{:S(2)}) %collective-permute-start.2) | collective-permute-done | bytes 327712 | tf_op jit(solution)/shard_map/ppermute | solution.py:19
  28.0 12.3 %convolution_bitcast_fusion = f32[6144,128]{0,1:T(8,128)} fusion(bf16[6144,1280]{1,0:T(8,128)(2,1)} %param.8, bf16[128,1280]{1,0:T(8,128)(2,1)S(1)} %collective-permute-done.2, bf16[128,1280]{1,0:T(8,128)(2,1)S(1)} %broadcast_select_fusion.1, pred[]{:T(512)S(6)} %ge.9), kind=kOutput, calls=%fused_computation.6 | convolution fusion | flops 2013429760 | bytes 19529728 | tf_op jit(solution)/shard_map/dot_general | solution.py:96
  40.3 61.2 %all_gather.3 = s32[1024,16]{1,0:T(8,128)S(1)} all-gather(s32[8,16]{1,0:T(8,128)S(1)} %copy-done.3), channel_id=1, replica_groups=mesh['row'=8,'col'=16] {'row','col'}, dimensions={0}, use_global_device_ids=true | all-gather | bytes 66048 | tf_op jit(solution)/shard_map/all_gather | solution.py:68
  101.5 0.1 broadcast_divide_fusion
  101.7 0.2 div.28
  101.9 0.3 fusion.15
  102.2 0.2 and.32
  102.6 0.2 reduce_window_sum.22
  102.8 0.1 copy.13
  102.9 0.2 eq.75
  103.1 0.1 copy.14
  103.3 0.2 eq.80
  103.5 0.9 fusion.10
  104.5 0.1 reduce_sum.36
  104.7 0.1 reduce_sum.46
  104.8 0.1 copy.15
  104.9 0.1 eq.81
  105.1 17.2 %reduce-scatter.2.cloned.1.call-done = f32[384,128]{0,1:T(8,128)} async-done(((f32[6144,128]{0,1:T(8,128)}), f32[384,128]{0,1:T(8,128)}) %reduce-scatter.2.cloned.1.call-update) | async-done | bytes 196624 | tf_op jit(solution)/shard_map/reduce_scatter | solution.py:95
  122.2 0.9 convert_element_type.46
  123.2 0.1 copy.16
  123.3 0.1 reshape.107
  123.4 3.2 %convolution_convert_fusion.1 = bf16[256,8192]{1,0:T(8,128)(2,1)} fusion(bf16[6,8192]{1,0:T(8,128)(2,1)S(1)} %reshape.107, s32[256]{0:T(256)S(1)} %eq.81), kind=kOutput, calls=%fused_computation.1 | convolution fusion | flops 27264512 | bytes 4293632 | tf_op jit(solution)/shard_map/dot_general | solution.py:104
  126.7 7.6 %reshape.108 = bf16[128,2,8192]{2,1,0:T(2,128)(2,1)} reshape(bf16[256,8192]{1,0:T(8,128)(2,1)} %convolution_convert_fusion.1) | data formatting | bytes 8388608 | tf_op jit(solution)/shard_map/reshape | solution.py:106
  134.3 9.6 %all-to-all-start = ((bf16[128,2,8192]{2,1,0:T(2,128)(2,1)}), bf16[128,2,8192]{2,1,0:T(2,128)(2,1)}, u32[]{:S(2)}, u32[]{:S(2)}) async-start(bf16[128,2,8192]{2,1,0:T(2,128)(2,1)} %reshape.108), calls=%async_computation.1 | async-start | bytes 8388608 | tf_op jit(solution)/shard_map/all_to_all | solution.py:105
  144.2 0.2 reduce_window_sum.23
  144.4 0.2 select_reduce_fusion
  144.7 51.3 %all-to-all-done = bf16[128,2,8192]{2,1,0:T(2,128)(2,1)} async-done(((bf16[128,2,8192]{2,1,0:T(2,128)(2,1)}), bf16[128,2,8192]{2,1,0:T(2,128)(2,1)}, u32[]{:S(2)}, u32[]{:S(2)}) %all-to-all-start) | async-done | bytes 4194336 | tf_op jit(solution)/shard_map/all_to_all | solution.py:105
  196.0 7.2 %reshape.109 = bf16[256,8192]{1,0:T(8,128)(2,1)} reshape(bf16[128,2,8192]{2,1,0:T(2,128)(2,1)} %all-to-all-done) | data formatting | bytes 8388608 | tf_op jit(solution)/shard_map/reshape | solution.py:109
  203.2 4.3 %convolution_convert_fusion.2 = bf16[128,8192]{1,0:T(8,128)(2,1)} fusion(bf16[256,8192]{1,0:T(8,128)(2,1)} %reshape.109, s32[128]{0:T(128)S(1)} %multiply_add_fusion), kind=kOutput, calls=%fused_computation.2 | convolution fusion | flops 537952256 | bytes 6291968 | tf_op jit(solution)/shard_map/dot_general | solution.py:108
  207.5 2.9 reshape.110
  210.4 4.8 %convolution_convert_fusion.3 = bf16[8,128,512]{2,1,0:T(8,128)(2,1)S(1)} fusion(bf16[8,1024,128]{2,1,0:T(8,128)(2,1)S(1)} %reshape.110, bf16[8,1024,512]{2,1,0:T(8,128)(2,1)} %param.9), kind=kOutput, calls=%fused_computation.11 | convolution fusion | flops 1074266112 | bytes 11534336 | tf_op jit(solution)/shard_map/bfs,bfp->bsp/dot_general | solution.py:34
  215.2 5.9 %fusion.6 = bf16[8,512,128]{1,2,0:T(8,128)(2,1)} fusion(f32[8,512]{1,0:T(8,128)S(1)} %fusion.28, f32[512]{0:T(512)S(1)} %bitcast.41, f32[8,512]{1,0:T(8,128)S(1)} %get-tuple-element.10, f32[512]{0:T(512)S(1)} %bitcast.42, f32[8,512]{1,0:T(8,128)S(1)} %get-tuple-element.11, f32[512]{0:T(512)S(1)} %bitcast.40, f32[8,512]{1,0:T(8,128)S(1)} %get-tuple-element.9, ...), kind=kOutput, calls=%fused_computation.10 | convolution fusion | flops 1099431936 | bytes 2299904 | tf_op jit(solution)/shard_map/ks,bkp->bsp/dot_general | solution.py:42
  221.1 6.5 %convert_bitcast_fusion = bf16[8,1024,128]{1,2,0:T(8,128)(2,1)S(1)} fusion(bf16[8,512,128]{1,2,0:T(8,128)(2,1)} %fusion.6, bf16[8,1024,512]{2,1,0:T(8,128)(2,1)} %param.9), kind=kOutput, calls=%fused_computation.9 | convolution fusion | flops 1074790400 | bytes 11534336 | tf_op jit(solution)/shard_map/bfp,bsp->bfs/dot_general | solution.py:45
  227.6 2.4 copy.17
  230.0 2.8 reshape.111
  232.8 3.3 %convolution_convert_fusion = bf16[256,8192]{1,0:T(8,128)(2,1)} fusion(bf16[128,8192]{1,0:T(8,128)(2,1)S(1)} %reshape.111, s32[128]{0:T(128)S(1)} %multiply_add_fusion), kind=kOutput, calls=%fused_computation | convolution fusion | flops 539000832 | bytes 6291968 | tf_op jit(solution)/shard_map/dot_general | solution.py:116
  236.2 7.6 %reshape.112 = bf16[128,2,8192]{2,1,0:T(2,128)(2,1)} reshape(bf16[256,8192]{1,0:T(8,128)(2,1)} %convolution_convert_fusion) | data formatting | bytes 8388608 | tf_op jit(solution)/shard_map/reshape | solution.py:120
  243.8 57.6 %all_to_all.10 = bf16[128,2,8192]{2,1,0:T(2,128)(2,1)} all-to-all(bf16[128,2,8192]{2,1,0:T(2,128)(2,1)} %reshape.112), channel_id=1, replica_groups=mesh['row'=8,'col'=16] {'row','col'}, dimensions={0} | all-to-all | bytes 8388608 | tf_op jit(solution)/shard_map/all_to_all | solution.py:119
  301.4 7.2 %reshape.113 = bf16[256,8192]{1,0:T(8,128)(2,1)} reshape(bf16[128,2,8192]{2,1,0:T(2,128)(2,1)} %all_to_all.10) | data formatting | bytes 8388608 | tf_op jit(solution)/shard_map/reshape | solution.py:123
  308.6 2.9 fusion.20
  311.5 0.8 reshape.114
  (34 shorter events, 0.8 us)
Async XLA Ops:
  6.5 208.6 %copy-start = (bf16[512,128]{1,0:T(8,128)(2,1)S(1)}, bf16[512,128]{1,0:T(8,128)(2,1)}, u32[]{:S(2)}) copy-start(bf16[512,128]{1,0:T(8,128)(2,1)} %param.13) | copy-start | bytes 393220
  6.5 115.7 %reduce-scatter.2.cloned.1.call-start = ((), (), s32[]{:S(2)}) async-start(), calls=%async_computation.3 | async-start | bytes 3342336 | tf_op jit(solution)/shard_map/reduce_scatter | solution.py:95
  7.6 3.8 %collective-permute-start = (bf16[128,1280]{1,0:T(8,128)(2,1)S(1)}, bf16[128,1280]{1,0:T(8,128)(2,1)S(1)}, u32[]{:S(2)}, u32[]{:S(2)}) collective-permute-start(bf16[128,1280]{1,0:T(8,128)(2,1)S(1)} %slice.21), channel_id=1, source_target_pairs={{0,16},{1,17},{2,18},{3,19},{4,20},{5,21},{6,22},{7,23},{8,24},{9,... | collective-permute-start | bytes 983048 | tf_op jit(solution)/shard_map/ppermute | solution.py:19
  12.4 8.1 %collective-permute-start.1 = (bf16[128,1280]{1,0:T(8,128)(2,1)S(1)}, bf16[128,1280]{1,0:T(8,128)(2,1)S(1)}, u32[]{:S(2)}, u32[]{:S(2)}) collective-permute-start(bf16[128,1280]{1,0:T(8,128)(2,1)S(1)} %broadcast_select_fusion), channel_id=1, source_target_pairs={{0,32},{16,48},{1,33},{17,49},{2,34},{18,50},{3,35},{19,51},{4,36}... | collective-permute-start | bytes 983048 | tf_op jit(solution)/shard_map/ppermute | solution.py:19
  20.5 7.5 %collective-permute-start.2 = (bf16[128,1280]{1,0:T(8,128)(2,1)S(1)}, bf16[128,1280]{1,0:T(8,128)(2,1)S(1)}, u32[]{:S(2)}, u32[]{:S(2)}) collective-permute-start(bf16[128,1280]{1,0:T(8,128)(2,1)S(1)} %broadcast_select_fusion.1), channel_id=1, source_target_pairs={{0,64},{16,80},{32,96},{48,112},{1,65},{17,81},{33,97},{49,113},{2... | collective-permute-start | bytes 983048 | tf_op jit(solution)/shard_map/ppermute | solution.py:19
  21.8 18.5 %copy-start.3 = (s32[8,16]{1,0:T(8,128)S(1)}, s32[8,16]{1,0:T(8,128)}, u32[]{:S(2)}) copy-start(s32[8,16]{1,0:T(8,128)} %param.14) | copy-start | bytes 1540
  134.3 10.3 %copy-start.5 = (f32[3,512]{1,0:T(4,128)S(1)}, f32[3,512]{1,0:T(4,128)}, u32[]{:S(2)}) copy-start(f32[3,512]{1,0:T(4,128)} %param.12) | copy-start | bytes 18436
  134.3 10.3 %copy-start.4 = (f32[8,512]{1,0:T(8,128)S(1)}, f32[8,512]{1,0:T(8,128)}, u32[]{:S(2)}) copy-start(f32[8,512]{1,0:T(8,128)} %param.11) | copy-start | bytes 49156
  134.3 10.3 %copy-start.6 = (s32[8]{0:T(128)S(1)}, s32[8]{0:T(128)}, u32[]{:S(2)}) copy-start(s32[8]{0:T(128)} %param.15) | copy-start | bytes 100
  134.3 10.4 %copy-start.2 = (f32[8,3,512]{2,0,1:T(8,128)S(1)}, f32[8,3,512]{2,0,1:T(8,128)}, u32[]{:S(2)}) copy-start(f32[8,3,512]{2,0,1:T(8,128)} %param.10) | copy-start | bytes 147460
  134.3 61.7 %all-to-all-start = ((bf16[128,2,8192]{2,1,0:T(2,128)(2,1)}), bf16[128,2,8192]{2,1,0:T(2,128)(2,1)}, u32[]{:S(2)}, u32[]{:S(2)}) async-start(bf16[128,2,8192]{2,1,0:T(2,128)(2,1)} %reshape.108), calls=%async_computation.1 | async-start | bytes 8388608 | tf_op jit(solution)/shard_map/all_to_all | solution.py:105
  301.4 11.0 %copy-start.1 = (bf16[512,128]{1,0:T(8,128)(2,1)S(1)}, bf16[512,128]{1,0:T(8,128)(2,1)}, u32[]{:S(2)}) copy-start(bf16[512,128]{1,0:T(8,128)(2,1)} %param.13) | copy-start | bytes 393220
Sparse Core Ops, SparseCore 0:
  40.4 81.7 reduce-scatter.1

commit v2 on v1

--- a/solution.py
+++ b/solution.py
@@ -63,9 +63,7 @@
     slab_width = charge_proj.shape[1]
     own_rows = group_rows // col_count
     own_blocks = own_rows // SH
-    tile = SH * slab_width
 
-    all_lists = lax.all_gather(shell_lists, ("row", "col"), tiled=True)
     window = broadcast_from_first(occ_coeffs[:slab_width], "row")
 
     requested = shell_lists.reshape(-1)
@@ -77,20 +75,14 @@
     before = jnp.cumsum(onehot, axis=0) - onehot
     rank = jnp.sum(before * onehot, axis=1)
     slot = owner * capacity + rank
-    pick = (slot[:, None] == jnp.arange(slots)[None, :]).astype(jnp.bfloat16)
-
-    lists = all_lists.reshape(owners, request_count)
-    mine = (lists // own_blocks == me).astype(jnp.int32)
-    order = jnp.cumsum(mine, axis=1)
-    local = lists % own_blocks
-    wanted_by = []
-    for place in range(capacity):
-        hit = mine * (order == place + 1)
-        wanted_by.append(
-            jnp.sum(hit * (local + 1), axis=1) - 1
-        )
-    received_ids = jnp.stack(wanted_by, axis=1).reshape(-1)
-    serve = (received_ids[:, None] == jnp.arange(own_blocks)[None, :]).astype(jnp.bfloat16)
+    hit = slot[None, :] == jnp.arange(slots)[:, None]
+    source_of = jnp.sum(
+        jnp.where(hit, jnp.arange(request_count)[None, :] - request_count, 0), axis=1
+    ) + request_count
+    wanted = jnp.full((slots,), -1, jnp.int32).at[slot].set(requested % own_blocks)
+    received_ids = lax.all_to_all(
+        wanted.reshape(owners, capacity), ("row", "col"), split_axis=0, concat_axis=0, tiled=True
+    ).reshape(-1)
 
     density = lax.psum_scatter(
         lax.dot_general(
@@ -100,27 +92,32 @@
         scatter_dimension=0,
         tiled=True,
     ).astype(jnp.bfloat16)
-    store = density.reshape(own_blocks, tile)
-    found = jnp.dot(serve, store, preferred_element_type=jnp.float32).astype(jnp.bfloat16)
+    store = density.reshape(own_blocks, SH, slab_width)
+    found = store[jnp.maximum(received_ids, 0)]
     replies = lax.all_to_all(
-        found.reshape(owners, capacity, tile), ("row", "col"), split_axis=0, concat_axis=0, tiled=True
+        found.reshape(owners, capacity * SH, slab_width),
+        ("row", "col"),
+        split_axis=0,
+        concat_axis=0,
+        tiled=True,
     )
-    fetched = jnp.dot(
-        pick, replies.reshape(slots, tile), preferred_element_type=jnp.float32
-    ).astype(jnp.bfloat16)
+    fetched = replies.reshape(slots, SH, slab_width)[slot]
     dens_rows = fetched.reshape(shell_lists.shape[0], NSIG * SH, slab_width)
     terms = batch_terms(
         dens_rows, colloc, grid_points, grid_weights, charge_sites, charge_proj, point_counts
     )
-    terms = terms.astype(jnp.bfloat16).reshape(request_count, tile)
-    tiles = lax.dot_general(
-        pick, terms, (((0,), (0,)), ((), ())), preferred_element_type=jnp.float32
-    ).astype(jnp.bfloat16)
+    terms = terms.astype(jnp.bfloat16).reshape(request_count, SH, slab_width)
+    tiles = jnp.take(terms, source_of, axis=0, mode="fill", fill_value=0)
     arrived = lax.all_to_all(
-        tiles.reshape(owners, capacity, tile), ("row", "col"), split_axis=0, concat_axis=0, tiled=True
+        tiles.reshape(owners, capacity * SH, slab_width),
+        ("row", "col"),
+        split_axis=0,
+        concat_axis=0,
+        tiled=True,
     )
-    summed = lax.dot_general(
-        serve, arrived.reshape(slots, tile), (((0,), (0,)), ((), ())), preferred_element_type=jnp.float32
+    serve = (jnp.arange(own_blocks)[:, None] == received_ids[None, :]).astype(jnp.bfloat16)
+    summed = jnp.einsum(
+        "js,sfc->jfc", serve, arrived.reshape(slots, SH, slab_width), preferred_element_type=jnp.float32
     )
     return summed.reshape(own_rows, slab_width)
 

time: 321 us -> 292 us (0.910)
  blocking collectives: 119 us -> 24.4 us
  waiting for transfers between devices: 83.9 us -> 172 us
  local copies, waits for them, and re-layouts: 41.7 us -> 17 us
  matrix products: 43.3 us -> 33.9 us
  other arithmetic: 4.28 us -> 11.3 us
  starting transfers between devices: 13.5 us -> 18.6 us
    all_gather x1 -> x0, blocking collectives: 61.2 us -> none  [on_device(): all_lists = lax.all_gather(shell_lists, ('row', 'col'), tiled=True)]
    all_to_all x1 -> x2, waiting for transfers between devices: 51.3 us -> 103 us  [the longest x1 52.1 us: on_device(): lax.all_to_all(tiles.reshape(owners, capacity * SH, slab_width), ('row',...]
    reshape x8 -> x0, local copies, waits for them, and re-layouts: 36.3 us -> none  [the longest x1 7.62 us: on_device(): found.reshape(owners, capacity, tile)]
    reduce_scatter x1, waiting for transfers between devices: 17.2 us -> 53.1 us  [on_device(): lax.psum_scatter(lax.dot_general(occ_coeffs, window, (((1,), (1,)), ((),...]
    all_to_all x1, blocking collectives: 57.6 us -> 24.4 us  [on_device(): lax.all_to_all(wanted.reshape(owners, capacity), ('row', 'col'), split_ax...]
    dot_general x4 -> x1, matrix products: 13.8 us -> 4.47 us  [on_device(): jnp.einsum('js,sfc->jfc', serve, arrived.reshape(slots, SH, slab_width),...]
    gather x0 -> x3, local copies, waits for them, and re-layouts: none -> 9.25 us  [the longest x1 3.14 us: on_device(): fetched = replies.reshape(slots, SH, slab_width)[slot]]
    select_n x1 -> x4, other arithmetic: 0.01 us -> 7.65 us  [the longest x2 7.63 us: on_device(): tiles = jnp.take(terms, source_of, axis=0, mode='fill', fill_value=0)]
  transfers between devices with their start and end apart: 5 -> 6, of which waited for: 5 -> 6; matrix products, arithmetic and copies ran while one was open for 1% -> 2% of each run, Pallas kernels for 0% -> 0%
where the time goes in v2:
time: 292 us; the launch traced here: 291 us
  waiting for transfers between devices  172 us (59%)
  matrix products  33.9 us (12%)
  blocking collectives  24.4 us (8%)
  starting transfers between devices  18.6 us (6%)
  local copies, waits for them, and re-layouts  17 us (6%)
  between operations  13.7 us (5%)
  other arithmetic  11.3 us (4%)
    reduce_scatter x1, waiting for transfers between devices, on_device(): lax.psum_scatter(lax.dot_general(occ_coeffs, window, (((1,), (1,)), ((),...  53.1 us
    all_to_all x1, waiting for transfers between devices, on_device(): lax.all_to_all(tiles.reshape(owners, capacity * SH, slab_width), ('row',...  52.1 us
    all_to_all x1, waiting for transfers between devices, on_device(): lax.all_to_all(found.reshape(owners, capacity * SH, slab_width), ('row',...  51.2 us
    all_to_all x1, blocking collectives, on_device(): lax.all_to_all(wanted.reshape(owners, capacity), ('row', 'col'), split_ax...  24.4 us
    ppermute x3, waiting for transfers between devices, broadcast_from_first(): moved = lax.ppermute(value, axis, pairs)  15.4 us
    dot_general x1, matrix products, on_device(): lax.dot_general(occ_coeffs, window, (((1,), (1,)), ((), ())), preferred_e...  12.3 us
    all_to_all x1, starting transfers between devices, on_device(): lax.all_to_all(found.reshape(owners, capacity * SH, slab_width), ('row',...  9.57 us
    select_n x2, other arithmetic, on_device(): tiles = jnp.take(terms, source_of, axis=0, mode='fill', fill_value=0)  7.63 us
  transfers between devices with their start and end apart: 6, of which 6 were waited for; matrix products, arithmetic and copies ran while one was open for 2% of the time, Pallas kernels for 0%

profile of v2, /device:TPU:1, one launch (start us, length us, event | category | flops | bytes accessed | tf_op | source)
XLA Modules:
  0.0 290.7 jit_solution(829347685592586417)
XLA Ops:
  6.5 1.0 slice.21
  7.6 1.3 collective-permute-start
  8.9 2.5 collective-permute-done
  11.4 1.0 broadcast_select_fusion
  12.4 1.3 collective-permute-start.1
  13.7 6.8 %collective-permute-done.1 = bf16[128,1280]{1,0:T(8,128)(2,1)S(1)} collective-permute-done((bf16[128,1280]{1,0:T(8,128)(2,1)S(1)}, bf16[128,1280]{1,0:T(8,128)(2,1)S(1)}, u32[]{:S(2)}, u32[]{:S(2)}) %collective-permute-start.1) | collective-permute-done | bytes 327712 | tf_op jit(solution)/shard_map/ppermute | solution.py:19
  20.5 1.3 collective-permute-start.2
  21.9 6.1 %collective-permute-done.2 = bf16[128,1280]{1,0:T(8,128)(2,1)S(1)} collective-permute-done((bf16[128,1280]{1,0:T(8,128)(2,1)S(1)}, bf16[128,1280]{1,0:T(8,128)(2,1)S(1)}, u32[]{:S(2)}, u32[]{:S(2)}) %collective-permute-start.2) | collective-permute-done | bytes 327712 | tf_op jit(solution)/shard_map/ppermute | solution.py:19
  28.0 12.3 %convolution_bitcast_fusion = f32[6144,128]{0,1:T(8,128)} fusion(bf16[6144,1280]{1,0:T(8,128)(2,1)} %param.8, bf16[128,1280]{1,0:T(8,128)(2,1)S(1)} %collective-permute-done.2, bf16[128,1280]{1,0:T(8,128)(2,1)S(1)} %broadcast_select_fusion.1, pred[]{:T(512)S(6)} %ge.20), kind=kOutput, calls=%fused_computation.7 | convolution fusion | flops 2013429760 | bytes 19529728 | tf_op jit(solution)/shard_map/dot_general | solution.py:88
  40.2 0.0 reduce-scatter.2.cloned.1.call-update
  40.3 0.1 div.28
  40.4 0.1 div.27
  40.5 0.1 rem.34
  40.6 0.1 ne.65
  40.6 0.1 and.37
  40.7 0.1 fusion.15
  40.8 0.2 reduce_window_sum.11
  41.0 0.2 select_reduce_fusion.1
  41.2 1.0 scatter_custom_fusion
  42.2 0.1 all_to_all.12
  42.3 24.4 %all_to_all.19 = s32[128,1,2]{2,1,0:T(1,128)S(1)} all-to-all(s32[128,1,2]{2,1,0:T(1,128)S(1)} %bitcast.61), channel_id=1, replica_groups=mesh['row'=8,'col'=16] {'row','col'}, dimensions={0} | all-to-all | bytes 2048 | tf_op jit(solution)/shard_map/all_to_all | solution.py:83
  66.8 0.5 broadcast.226
  67.3 1.0 fusion.26
  68.3 0.1 reshape.204
  68.4 53.1 %reduce-scatter.2.cloned.1.call-done = f32[384,128]{0,1:T(8,128)} async-done(((f32[6144,128]{0,1:T(8,128)}), f32[384,128]{0,1:T(8,128)}) %reduce-scatter.2.cloned.1.call-update) | async-done | bytes 196624 | tf_op jit(solution)/shard_map/reduce_scatter | solution.py:87
  121.5 0.9 convert_element_type.25
  122.5 0.1 copy.28
  122.6 3.1 %gather_fusion = bf16[256,64,128]{2,1,0:T(8,128)(2,1)} fusion(bf16[6,64,128]{2,1,0:T(8,128)(2,1)S(1)} %bitcast.56, s32[1024]{0:T(1024)S(1)} %pad_clamp_fusion.2), kind=kCustom, calls=%fused_computation | custom fusion | bytes 8389632 | tf_op jit(solution)/shard_map/gather | solution.py:96
  125.7 9.6 %all-to-all-start.1 = ((bf16[128,128,128]{2,1,0:T(8,128)(2,1)}), bf16[128,128,128]{2,1,0:T(8,128)(2,1)}, u32[]{:S(2)}, u32[]{:S(2)}) async-start(bf16[128,128,128]{2,1,0:T(8,128)(2,1)} %bitcast.58), calls=%async_computation.2 | async-start | bytes 8388608 | tf_op jit(solution)/shard_map/all_to_all | solution.py:97
  135.3 0.1 select_reduce_fusion
  135.4 0.1 add.124
  135.5 0.1 add.127
  135.7 0.1 copy.26
  135.8 0.1 copy.27
  136.0 0.1 fusion.16
  136.1 51.2 %all-to-all-done.1 = bf16[128,128,128]{2,1,0:T(8,128)(2,1)} async-done(((bf16[128,128,128]{2,1,0:T(8,128)(2,1)}), bf16[128,128,128]{2,1,0:T(8,128)(2,1)}, u32[]{:S(2)}, u32[]{:S(2)}) %all-to-all-start.1) | async-done | bytes 4194336 | tf_op jit(solution)/shard_map/all_to_all | solution.py:97
  187.3 3.1 %gather_fusion.1 = bf16[128,64,128]{2,1,0:T(8,128)(2,1)S(1)} fusion(bf16[256,64,128]{2,1,0:T(8,128)(2,1)} %bitcast.8, s32[1024]{0:T(1024)S(1)} %pad_clamp_fusion.1), kind=kCustom, calls=%fused_computation.1 | custom fusion | bytes 4194816 | tf_op jit(solution)/shard_map/gather | solution.py:104
  190.5 4.8 %convolution_convert_fusion = bf16[8,128,512]{2,1,0:T(8,128)(2,1)S(1)} fusion(bf16[8,1024,128]{2,1,0:T(8,128)(2,1)S(1)} %bitcast.60, bf16[8,1024,512]{2,1,0:T(8,128)(2,1)} %param.9), kind=kOutput, calls=%fused_computation.15 | convolution fusion | flops 1074266112 | bytes 11534336 | tf_op jit(solution)/shard_map/bfs,bfp->bsp/dot_general | solution.py:34
  195.3 4.7 %fusion.8 = bf16[8,512,128]{2,1,0:T(8,128)(2,1)S(1)} fusion(f32[8,512]{1,0:T(8,128)S(1)} %fusion.16, f32[512]{0:T(512)S(1)} %bitcast.67, f32[8,512]{1,0:T(8,128)S(1)} %get-tuple-element.10, f32[512]{0:T(512)S(1)} %bitcast.68, f32[8,512]{1,0:T(8,128)S(1)} %get-tuple-element.11, f32[512]{0:T(512)S(1)} %bitcast.66, f32[8,512]{1,0:T(8,128)S(1)} %get-tuple-element.9, ...), kind=kOutput, calls=%fused_computation.14 | convolution fusion | flops 1099431936 | bytes 2299904 | tf_op jit(solution)/shard_map/ks,bkp->bsp/dot_general | solution.py:42
  200.0 7.6 %convert_bitcast_fusion = bf16[8,1024,128]{1,2,0:T(8,128)(2,1)} fusion(bf16[8,512,128]{2,1,0:T(8,128)(2,1)S(1)} %fusion.8, bf16[8,1024,512]{2,1,0:T(8,128)(2,1)} %param.9), kind=kOutput, calls=%fused_computation.13 | convolution fusion | flops 1074790400 | bytes 11534336 | tf_op jit(solution)/shard_map/bfp,bsp->bfs/dot_general | solution.py:45
  207.6 3.0 %copy.32 = bf16[8,1024,128]{2,1,0:T(8,128)(2,1)S(1)} copy(bf16[8,1024,128]{1,2,0:T(8,128)(2,1)} %convert_bitcast_fusion) | data formatting | bytes 4194304 | tf_op jit(solution)/shard_map/convert_element_type | solution.py:109
  210.6 3.1 %gather_fusion.2 = bf16[256,64,128]{2,1,0:T(8,128)(2,1)} fusion(bf16[128,64,128]{2,1,0:T(8,128)(2,1)S(1)} %bitcast.57, s32[1024]{0:T(1024)S(1)} %pad_clamp_fusion), kind=kCustom, calls=%fused_computation.2 | custom fusion | bytes 8389632 | tf_op jit(solution)/shard_map/jit(_take)/gather | solution.py:110
  213.7 7.6 %bitcast_select_fusion = bf16[128,128,128]{2,1,0:T(8,128)(2,1)} fusion(pred[128,128]{1,0:T(8,128)(4,1)S(1)} %copy.27, bf16[128,128,128]{2,1,0:T(8,128)(2,1)} %bitcast.59), kind=kLoop, calls=%fused_computation.8 | loop fusion | flops 2097152 | bytes 8404992 | tf_op jit(solution)/shard_map/jit(_take)/select_n | solution.py:110
  221.3 5.1 %all-to-all-start.2 = ((bf16[128,128,128]{2,1,0:T(8,128)(2,1)}), bf16[128,128,128]{2,1,0:T(8,128)(2,1)}, u32[]{:S(2)}, u32[]{:S(2)}) async-start(bf16[128,128,128]{2,1,0:T(8,128)(2,1)} %bitcast_select_fusion), calls=%async_computation.3 | async-start | bytes 8388608 | tf_op jit(solution)/shard_map/all_to_all | solution.py:111
  226.4 0.1 eq.47
  226.6 52.1 %all-to-all-done.2 = bf16[128,128,128]{2,1,0:T(8,128)(2,1)} async-done(((bf16[128,128,128]{2,1,0:T(8,128)(2,1)}), bf16[128,128,128]{2,1,0:T(8,128)(2,1)}, u32[]{:S(2)}, u32[]{:S(2)}) %all-to-all-start.2) | async-done | bytes 4194336 | tf_op jit(solution)/shard_map/all_to_all | solution.py:111
  278.7 4.5 %fusion.2 = f32[6,64,128]{2,0,1:T(8,128)S(1)} fusion(bf16[256,64,128]{2,1,0:T(8,128)(2,1)} %bitcast.24, s32[256]{0:T(256)S(1)} %eq.47), kind=kOutput, calls=%fused_computation.9 | convolution fusion | flops 25167360 | bytes 4391936 | tf_op jit(solution)/shard_map/js,sfc->jfc/dot_general | solution.py:119
  283.1 0.7 copy.34
  (28 shorter events, 0.2 us)
Async XLA Ops:
  6.5 188.7 %copy-start = (bf16[512,128]{1,0:T(8,128)(2,1)S(1)}, bf16[512,128]{1,0:T(8,128)(2,1)}, u32[]{:S(2)}) copy-start(bf16[512,128]{1,0:T(8,128)(2,1)} %param.13) | copy-start | bytes 393220
  6.5 115.0 %reduce-scatter.2.cloned.1.call-start = ((), (), s32[]{:S(2)}) async-start(), calls=%async_computation.4 | async-start | bytes 3342336 | tf_op jit(solution)/shard_map/reduce_scatter | solution.py:87
  7.6 3.8 %collective-permute-start = (bf16[128,1280]{1,0:T(8,128)(2,1)S(1)}, bf16[128,1280]{1,0:T(8,128)(2,1)S(1)}, u32[]{:S(2)}, u32[]{:S(2)}) collective-permute-start(bf16[128,1280]{1,0:T(8,128)(2,1)S(1)} %slice.21), channel_id=1, source_target_pairs={{0,16},{1,17},{2,18},{3,19},{4,20},{5,21},{6,22},{7,23},{8,24},{9,... | collective-permute-start | bytes 983048 | tf_op jit(solution)/shard_map/ppermute | solution.py:19
  12.4 8.1 %collective-permute-start.1 = (bf16[128,1280]{1,0:T(8,128)(2,1)S(1)}, bf16[128,1280]{1,0:T(8,128)(2,1)S(1)}, u32[]{:S(2)}, u32[]{:S(2)}) collective-permute-start(bf16[128,1280]{1,0:T(8,128)(2,1)S(1)} %broadcast_select_fusion), channel_id=1, source_target_pairs={{0,32},{16,48},{1,33},{17,49},{2,34},{18,50},{3,35},{19,51},{4,36}... | collective-permute-start | bytes 983048 | tf_op jit(solution)/shard_map/ppermute | solution.py:19
  20.5 7.5 %collective-permute-start.2 = (bf16[128,1280]{1,0:T(8,128)(2,1)S(1)}, bf16[128,1280]{1,0:T(8,128)(2,1)S(1)}, u32[]{:S(2)}, u32[]{:S(2)}) collective-permute-start(bf16[128,1280]{1,0:T(8,128)(2,1)S(1)} %broadcast_select_fusion.1), channel_id=1, source_target_pairs={{0,64},{16,80},{32,96},{48,112},{1,65},{17,81},{33,97},{49,113},{2... | collective-permute-start | bytes 983048 | tf_op jit(solution)/shard_map/ppermute | solution.py:19
  21.8 18.4 %copy-start.2 = (s32[8,16]{1,0:T(8,128)S(1)}, s32[8,16]{1,0:T(8,128)}, u32[]{:S(2)}) copy-start(s32[8,16]{1,0:T(8,128)} %param.14) | copy-start | bytes 1540
  125.7 10.3 %copy-start.4 = (f32[3,512]{1,0:T(4,128)S(1)}, f32[3,512]{1,0:T(4,128)}, u32[]{:S(2)}) copy-start(f32[3,512]{1,0:T(4,128)} %param.12) | copy-start | bytes 18436
  125.7 10.3 %copy-start.3 = (f32[8,512]{1,0:T(8,128)S(1)}, f32[8,512]{1,0:T(8,128)}, u32[]{:S(2)}) copy-start(f32[8,512]{1,0:T(8,128)} %param.11) | copy-start | bytes 49156
  125.7 10.3 %copy-start.5 = (s32[8]{0:T(128)S(1)}, s32[8]{0:T(128)}, u32[]{:S(2)}) copy-start(s32[8]{0:T(128)} %param.15) | copy-start | bytes 100
  125.7 10.4 %copy-start.1 = (f32[8,3,512]{2,0,1:T(8,128)S(1)}, f32[8,3,512]{2,0,1:T(8,128)}, u32[]{:S(2)}) copy-start(f32[8,3,512]{2,0,1:T(8,128)} %param.10) | copy-start | bytes 147460
  125.7 61.7 %all-to-all-start.1 = ((bf16[128,128,128]{2,1,0:T(8,128)(2,1)}), bf16[128,128,128]{2,1,0:T(8,128)(2,1)}, u32[]{:S(2)}, u32[]{:S(2)}) async-start(bf16[128,128,128]{2,1,0:T(8,128)(2,1)} %bitcast.58), calls=%async_computation.2 | async-start | bytes 8388608 | tf_op jit(solution)/shard_map/all_to_all | solution.py:97
  221.3 57.3 %all-to-all-start.2 = ((bf16[128,128,128]{2,1,0:T(8,128)(2,1)}), bf16[128,128,128]{2,1,0:T(8,128)(2,1)}, u32[]{:S(2)}, u32[]{:S(2)}) async-start(bf16[128,128,128]{2,1,0:T(8,128)(2,1)} %bitcast_select_fusion), calls=%async_computation.3 | async-start | bytes 8388608 | tf_op jit(solution)/shard_map/all_to_all | solution.py:111
Sparse Core Ops, SparseCore 0:
  40.4 81.0 reduce-scatter.1

commit v3 on v2

--- a/solution.py
+++ b/solution.py
@@ -84,14 +84,13 @@
         wanted.reshape(owners, capacity), ("row", "col"), split_axis=0, concat_axis=0, tiled=True
     ).reshape(-1)
 
-    density = lax.psum_scatter(
-        lax.dot_general(
-            occ_coeffs, window, (((1,), (1,)), ((), ())), preferred_element_type=jnp.float32
-        ),
-        "col",
-        scatter_dimension=0,
-        tiled=True,
-    ).astype(jnp.bfloat16)
+    partial = lax.dot_general(
+        occ_coeffs, window, (((1,), (1,)), ((), ())), preferred_element_type=jnp.float32
+    )
+    pieces = lax.all_to_all(
+        partial.reshape(col_count, own_rows, slab_width), "col", split_axis=0, concat_axis=0, tiled=True
+    )
+    density = jnp.sum(pieces, axis=0).astype(jnp.bfloat16)
     store = density.reshape(own_blocks, SH, slab_width)
     found = store[jnp.maximum(received_ids, 0)]
     replies = lax.all_to_all(

time: 292 us -> 258 us (0.88)
  starting transfers between devices: 18.6 us -> 43.5 us
  blocking collectives: 24.4 us -> 0 us
  waiting for transfers between devices: 172 us -> 149 us
  between operations: 13.7 us -> 0.31 us
    reduce_scatter x1 -> x0, waiting for transfers between devices: 53.1 us -> none  [on_device(): lax.psum_scatter(lax.dot_general(occ_coeffs, window, (((1,), (1,)), ((),...]
    all_to_all x0 -> x2, waiting for transfers between devices: none -> 38.9 us  [the longest x1 38.9 us: on_device(): lax.all_to_all(partial.reshape(col_count, own_rows, slab_width), 'col', s...]
    all_to_all x1 -> x0, blocking collectives: 24.4 us -> none  [on_device(): lax.all_to_all(wanted.reshape(owners, capacity), ('row', 'col'), split_ax...]
    all_to_all x0 -> x2, starting transfers between devices: none -> 17.9 us  [the longest x1 10.8 us: on_device(): lax.all_to_all(wanted.reshape(owners, capacity), ('row', 'col'), split_ax...]
    ppermute x3, waiting for transfers between devices: 15.4 us -> 6.76 us  [broadcast_from_first(): moved = lax.ppermute(value, axis, pairs)]
    all_to_all x1, starting transfers between devices: 9.57 us -> 15.4 us  [on_device(): lax.all_to_all(found.reshape(owners, capacity * SH, slab_width), ('row',...]
  transfers between devices with their start and end apart: 6 -> 7, of which waited for: 6 -> 5; matrix products, arithmetic and copies ran while one was open for 2% -> 7% of each run, Pallas kernels for 0% -> 0%
where the time goes in v3:
time: 258 us; the launch traced here: 257 us
  waiting for transfers between devices  149 us (58%)
  starting transfers between devices  43.5 us (17%)
  matrix products  32.2 us (12%)
  local copies, waits for them, and re-layouts  19.6 us (8%)
  other arithmetic  11.9 us (5%)
    all_to_all x1, waiting for transfers between devices, on_device(): lax.all_to_all(tiles.reshape(owners, capacity * SH, slab_width), ('row',...  52.1 us
    all_to_all x1, waiting for transfers between devices, on_device(): lax.all_to_all(found.reshape(owners, capacity * SH, slab_width), ('row',...  51.2 us
    all_to_all x1, waiting for transfers between devices, on_device(): lax.all_to_all(partial.reshape(col_count, own_rows, slab_width), 'col', s...  38.9 us
    all_to_all x1, starting transfers between devices, on_device(): lax.all_to_all(found.reshape(owners, capacity * SH, slab_width), ('row',...  15.4 us
    all_to_all x1, starting transfers between devices, on_device(): lax.all_to_all(wanted.reshape(owners, capacity), ('row', 'col'), split_ax...  10.8 us
    dot_general x1, matrix products, on_device(): lax.dot_general(occ_coeffs, window, (((1,), (1,)), ((), ())), preferred_e...  10.6 us
    select_n x2, other arithmetic, on_device(): tiles = jnp.take(terms, source_of, axis=0, mode='fill', fill_value=0)  7.63 us
    dot_general x1, matrix products, batch_terms(): jnp.einsum('bfp,bsp->bfs', colloc, spread_back, preferred_element_type=jn...  7.6 us
  transfers between devices with their start and end apart: 7, of which 5 were waited for; matrix products, arithmetic and copies ran while one was open for 7% of the time, Pallas kernels for 0%

profile of v3, /device:TPU:1, one launch (start us, length us, event | category | flops | bytes accessed | tf_op | source)
XLA Modules:
  0.0 256.5 jit_solution(10833963624608286687)
XLA Ops:
  0.0 1.0 slice.21
  1.0 1.3 collective-permute-start
  2.3 0.7 broadcast_remainder_fusion
  3.0 0.1 div.28
  3.1 0.1 rem.34
  3.2 0.7 compare_and_fusion.1
  3.9 0.1 ne.65
  4.0 0.9 collective-permute-done
  4.9 1.0 broadcast_select_fusion
  5.9 2.6 %collective-permute-start.1 = (bf16[128,1280]{1,0:T(8,128)(2,1)S(1)}, bf16[128,1280]{1,0:T(8,128)(2,1)S(1)}, u32[]{:S(2)}, u32[]{:S(2)}) collective-permute-start(bf16[128,1280]{1,0:T(8,128)(2,1)S(1)} %broadcast_select_fusion), channel_id=1, source_target_pairs={{0,32},{16,48},{1,33},{17,49},{2,34},{18,50},{3,35},{19,51},{4,36}... | collective-permute-start | bytes 983048 | tf_op jit(solution)/shard_map/ppermute | solution.py:19
  8.5 0.1 div.27
  8.5 0.1 and.37
  8.6 0.1 fusion.16
  8.7 0.2 reduce_window_sum.11
  8.9 5.9 %collective-permute-done.1 = bf16[128,1280]{1,0:T(8,128)(2,1)S(1)} collective-permute-done((bf16[128,1280]{1,0:T(8,128)(2,1)S(1)}, bf16[128,1280]{1,0:T(8,128)(2,1)S(1)}, u32[]{:S(2)}, u32[]{:S(2)}) %collective-permute-start.1) | collective-permute-done | bytes 327712 | tf_op jit(solution)/shard_map/ppermute | solution.py:19
  14.8 1.3 collective-permute-start.2
  16.2 0.2 select_reduce_fusion.1
  16.3 1.0 scatter_custom_fusion
  17.3 0.8 all_to_all.15
  18.1 10.8 %all-to-all-start = ((s32[128,1,2]{2,1,0:T(1,128)}), s32[128,1,2]{2,1,0:T(1,128)S(1)}, u32[]{:S(2)}, u32[]{:S(2)}) async-start(s32[128,1,2]{2,1,0:T(1,128)} %bitcast.2), calls=%async_computation | async-start | bytes 131072 | tf_op jit(solution)/shard_map/all_to_all | solution.py:83
  28.9 10.6 %fusion.11 = f32[128,6144]{1,0:T(8,128)S(1)} fusion(bf16[6144,1280]{1,0:T(8,128)(2,1)} %param.8, bf16[128,1280]{1,0:T(8,128)(2,1)S(1)} %collective-permute-done.2, bf16[128,1280]{1,0:T(8,128)(2,1)S(1)} %broadcast_select_fusion.1, pred[]{:T(512)S(6)} %ge.20), kind=kOutput, calls=%fused_computation.16 | convolution fusion | flops 2013429760 | bytes 19529728 | tf_op jit(solution)/shard_map/dot_general | solution.py:87
  39.5 2.0 copy.56
  41.5 7.1 %all-to-all-start.1 = ((f32[16,384,128]{1,2,0:T(8,128)}), f32[16,384,128]{1,2,0:T(8,128)S(1)}, u32[]{:S(2)}, u32[]{:S(2)}) async-start(f32[16,384,128]{1,2,0:T(8,128)} %bitcast.57), calls=%async_computation.1 | async-start | bytes 6291456 | tf_op jit(solution)/shard_map/all_to_all | solution.py:90
  48.6 0.5 broadcast.226
  49.1 1.0 fusion.27
  50.1 0.1 reshape.207
  50.3 38.9 %all-to-all-done.1 = f32[16,384,128]{1,2,0:T(8,128)S(1)} async-done(((f32[16,384,128]{1,2,0:T(8,128)}), f32[16,384,128]{1,2,0:T(8,128)S(1)}, u32[]{:S(2)}, u32[]{:S(2)}) %all-to-all-start.1) | async-done | bytes 3145760 | tf_op jit(solution)/shard_map/all_to_all | solution.py:90
  89.2 0.1 reduce_sum.32
  89.4 0.1 copy.41
  89.5 3.1 %gather_fusion = bf16[256,64,128]{2,1,0:T(8,128)(2,1)} fusion(bf16[6,64,128]{2,1,0:T(8,128)(2,1)S(1)} %bitcast.59, s32[1024]{0:T(1024)S(1)} %pad_clamp_fusion.2), kind=kCustom, calls=%fused_computation | custom fusion | bytes 8389632 | tf_op jit(solution)/shard_map/gather | solution.py:95
  92.6 15.4 %all-to-all-start.2 = ((bf16[128,128,128]{2,1,0:T(8,128)(2,1)}), bf16[128,128,128]{2,1,0:T(8,128)(2,1)}, u32[]{:S(2)}, u32[]{:S(2)}) async-start(bf16[128,128,128]{2,1,0:T(8,128)(2,1)} %bitcast.61), calls=%async_computation.2 | async-start | bytes 8388608 | tf_op jit(solution)/shard_map/all_to_all | solution.py:96
  107.9 0.1 select_reduce_fusion
  108.1 0.1 add.122
  108.2 0.1 add.125
  108.5 0.1 copy.38
  108.8 51.2 %all-to-all-done.2 = bf16[128,128,128]{2,1,0:T(8,128)(2,1)} async-done(((bf16[128,128,128]{2,1,0:T(8,128)(2,1)}), bf16[128,128,128]{2,1,0:T(8,128)(2,1)}, u32[]{:S(2)}, u32[]{:S(2)}) %all-to-all-start.2) | async-done | bytes 4194336 | tf_op jit(solution)/shard_map/all_to_all | solution.py:96
  160.0 3.1 %gather_fusion.1 = bf16[128,64,128]{2,1,0:T(8,128)(2,1)S(1)} fusion(bf16[256,64,128]{2,1,0:T(8,128)(2,1)} %bitcast.8, s32[1024]{0:T(1024)S(1)} %pad_clamp_fusion.1), kind=kCustom, calls=%fused_computation.1 | custom fusion | bytes 4194816 | tf_op jit(solution)/shard_map/gather | solution.py:103
  163.2 4.8 %convolution_convert_fusion = bf16[8,128,512]{2,1,0:T(8,128)(2,1)S(1)} fusion(bf16[8,1024,128]{2,1,0:T(8,128)(2,1)S(1)} %bitcast.63, bf16[8,1024,512]{2,1,0:T(8,128)(2,1)} %param.9), kind=kOutput, calls=%fused_computation.15 | convolution fusion | flops 1074266112 | bytes 11534336 | tf_op jit(solution)/shard_map/bfs,bfp->bsp/dot_general | solution.py:34
  168.0 4.7 %fusion.8 = bf16[8,512,128]{2,1,0:T(8,128)(2,1)S(1)} fusion(f32[8,512]{1,0:T(8,128)S(1)} %fusion.17, f32[512]{0:T(512)S(1)} %bitcast.70, f32[8,512]{1,0:T(8,128)S(1)} %get-tuple-element.10, f32[512]{0:T(512)S(1)} %bitcast.71, f32[8,512]{1,0:T(8,128)S(1)} %get-tuple-element.11, f32[512]{0:T(512)S(1)} %bitcast.69, f32[8,512]{1,0:T(8,128)S(1)} %get-tuple-element.9, ...), kind=kOutput, calls=%fused_computation.14 | convolution fusion | flops 1099431936 | bytes 2299904 | tf_op jit(solution)/shard_map/ks,bkp->bsp/dot_general | solution.py:42
  172.7 7.6 %convert_bitcast_fusion = bf16[8,1024,128]{1,2,0:T(8,128)(2,1)} fusion(bf16[8,512,128]{2,1,0:T(8,128)(2,1)S(1)} %fusion.8, bf16[8,1024,512]{2,1,0:T(8,128)(2,1)} %param.9), kind=kOutput, calls=%fused_computation.13 | convolution fusion | flops 1074790400 | bytes 11534336 | tf_op jit(solution)/shard_map/bfp,bsp->bfs/dot_general | solution.py:45
  180.3 3.0 %copy.45 = bf16[8,1024,128]{2,1,0:T(8,128)(2,1)S(1)} copy(bf16[8,1024,128]{1,2,0:T(8,128)(2,1)} %convert_bitcast_fusion) | data formatting | bytes 4194304 | tf_op jit(solution)/shard_map/convert_element_type | solution.py:108
  183.3 3.1 %gather_fusion.2 = bf16[256,64,128]{2,1,0:T(8,128)(2,1)} fusion(bf16[128,64,128]{2,1,0:T(8,128)(2,1)S(1)} %bitcast.60, s32[1024]{0:T(1024)S(1)} %pad_clamp_fusion), kind=kCustom, calls=%fused_computation.2 | custom fusion | bytes 8389632 | tf_op jit(solution)/shard_map/jit(_take)/gather | solution.py:109
  186.4 7.6 %bitcast_select_fusion = bf16[128,128,128]{2,1,0:T(8,128)(2,1)} fusion(pred[128,128]{1,0:T(8,128)(4,1)S(1)} %copy.38, bf16[128,128,128]{2,1,0:T(8,128)(2,1)} %bitcast.62), kind=kLoop, calls=%fused_computation.7 | loop fusion | flops 2097152 | bytes 8404992 | tf_op jit(solution)/shard_map/jit(_take)/select_n | solution.py:109
  194.0 5.1 %all-to-all-start.3 = ((bf16[128,128,128]{2,1,0:T(8,128)(2,1)}), bf16[128,128,128]{2,1,0:T(8,128)(2,1)}, u32[]{:S(2)}, u32[]{:S(2)}) async-start(bf16[128,128,128]{2,1,0:T(8,128)(2,1)} %bitcast_select_fusion), calls=%async_computation.3 | async-start | bytes 8388608 | tf_op jit(solution)/shard_map/all_to_all | solution.py:110
  199.1 0.1 eq.47
  199.2 52.1 %all-to-all-done.3 = bf16[128,128,128]{2,1,0:T(8,128)(2,1)} async-done(((bf16[128,128,128]{2,1,0:T(8,128)(2,1)}), bf16[128,128,128]{2,1,0:T(8,128)(2,1)}, u32[]{:S(2)}, u32[]{:S(2)}) %all-to-all-start.3) | async-done | bytes 4194336 | tf_op jit(solution)/shard_map/all_to_all | solution.py:110
  251.3 4.5 %fusion.2 = f32[6,64,128]{2,0,1:T(8,128)S(1)} fusion(bf16[256,64,128]{2,1,0:T(8,128)(2,1)} %bitcast.24, s32[256]{0:T(256)S(1)} %eq.47), kind=kOutput, calls=%fused_computation.8 | convolution fusion | flops 25167360 | bytes 4391936 | tf_op jit(solution)/shard_map/js,sfc->jfc/dot_general | solution.py:118
  255.8 0.7 copy.47
  (27 shorter events, 0.3 us)
Async XLA Ops:
  0.0 168.0 %copy-start = (bf16[512,128]{1,0:T(8,128)(2,1)S(1)}, bf16[512,128]{1,0:T(8,128)(2,1)}, u32[]{:S(2)}) copy-start(bf16[512,128]{1,0:T(8,128)(2,1)} %param.13) | copy-start | bytes 393220
  1.0 3.8 %collective-permute-start = (bf16[128,1280]{1,0:T(8,128)(2,1)S(1)}, bf16[128,1280]{1,0:T(8,128)(2,1)S(1)}, u32[]{:S(2)}, u32[]{:S(2)}) collective-permute-start(bf16[128,1280]{1,0:T(8,128)(2,1)S(1)} %slice.21), channel_id=1, source_target_pairs={{0,16},{1,17},{2,18},{3,19},{4,20},{5,21},{6,22},{7,23},{8,24},{9,... | collective-permute-start | bytes 983048 | tf_op jit(solution)/shard_map/ppermute | solution.py:19
  5.9 8.9 %collective-permute-start.1 = (bf16[128,1280]{1,0:T(8,128)(2,1)S(1)}, bf16[128,1280]{1,0:T(8,128)(2,1)S(1)}, u32[]{:S(2)}, u32[]{:S(2)}) collective-permute-start(bf16[128,1280]{1,0:T(8,128)(2,1)S(1)} %broadcast_select_fusion), channel_id=1, source_target_pairs={{0,32},{16,48},{1,33},{17,49},{2,34},{18,50},{3,35},{19,51},{4,36}... | collective-permute-start | bytes 983048 | tf_op jit(solution)/shard_map/ppermute | solution.py:19
  14.8 14.1 %collective-permute-start.2 = (bf16[128,1280]{1,0:T(8,128)(2,1)S(1)}, bf16[128,1280]{1,0:T(8,128)(2,1)S(1)}, u32[]{:S(2)}, u32[]{:S(2)}) collective-permute-start(bf16[128,1280]{1,0:T(8,128)(2,1)S(1)} %broadcast_select_fusion.1), channel_id=1, source_target_pairs={{0,64},{16,80},{32,96},{48,112},{1,65},{17,81},{33,97},{49,113},{2... | collective-permute-start | bytes 983048 | tf_op jit(solution)/shard_map/ppermute | solution.py:19
  18.1 23.4 %all-to-all-start = ((s32[128,1,2]{2,1,0:T(1,128)}), s32[128,1,2]{2,1,0:T(1,128)S(1)}, u32[]{:S(2)}, u32[]{:S(2)}) async-start(s32[128,1,2]{2,1,0:T(1,128)} %bitcast.2), calls=%async_computation | async-start | bytes 131072 | tf_op jit(solution)/shard_map/all_to_all | solution.py:83
  41.5 47.7 %all-to-all-start.1 = ((f32[16,384,128]{1,2,0:T(8,128)}), f32[16,384,128]{1,2,0:T(8,128)S(1)}, u32[]{:S(2)}, u32[]{:S(2)}) async-start(f32[16,384,128]{1,2,0:T(8,128)} %bitcast.57), calls=%async_computation.1 | async-start | bytes 6291456 | tf_op jit(solution)/shard_map/all_to_all | solution.py:90
  92.5 16.1 %copy-start.3 = (f32[3,512]{1,0:T(4,128)S(1)}, f32[3,512]{1,0:T(4,128)}, u32[]{:S(2)}) copy-start(f32[3,512]{1,0:T(4,128)} %param.12) | copy-start | bytes 18436
  92.5 16.1 %copy-start.2 = (f32[8,512]{1,0:T(8,128)S(1)}, f32[8,512]{1,0:T(8,128)}, u32[]{:S(2)}) copy-start(f32[8,512]{1,0:T(8,128)} %param.11) | copy-start | bytes 49156
  92.5 16.1 %copy-start.4 = (s32[8]{0:T(128)S(1)}, s32[8]{0:T(128)}, u32[]{:S(2)}) copy-start(s32[8]{0:T(128)} %param.15) | copy-start | bytes 100
  92.6 16.2 %copy-start.1 = (f32[8,3,512]{2,0,1:T(8,128)S(1)}, f32[8,3,512]{2,0,1:T(8,128)}, u32[]{:S(2)}) copy-start(f32[8,3,512]{2,0,1:T(8,128)} %param.10) | copy-start | bytes 147460
  92.6 67.5 %all-to-all-start.2 = ((bf16[128,128,128]{2,1,0:T(8,128)(2,1)}), bf16[128,128,128]{2,1,0:T(8,128)(2,1)}, u32[]{:S(2)}, u32[]{:S(2)}) async-start(bf16[128,128,128]{2,1,0:T(8,128)(2,1)} %bitcast.61), calls=%async_computation.2 | async-start | bytes 8388608 | tf_op jit(solution)/shard_map/all_to_all | solution.py:96
  194.0 57.3 %all-to-all-start.3 = ((bf16[128,128,128]{2,1,0:T(8,128)(2,1)}), bf16[128,128,128]{2,1,0:T(8,128)(2,1)}, u32[]{:S(2)}, u32[]{:S(2)}) async-start(bf16[128,128,128]{2,1,0:T(8,128)(2,1)} %bitcast_select_fusion), calls=%async_computation.3 | async-start | bytes 8388608 | tf_op jit(solution)/shard_map/all_to_all | solution.py:110

commit v4 on v3

--- a/solution.py
+++ b/solution.py
@@ -76,9 +76,7 @@
     rank = jnp.sum(before * onehot, axis=1)
     slot = owner * capacity + rank
     hit = slot[None, :] == jnp.arange(slots)[:, None]
-    source_of = jnp.sum(
-        jnp.where(hit, jnp.arange(request_count)[None, :] - request_count, 0), axis=1
-    ) + request_count
+    source_of = jnp.sum(jnp.where(hit, jnp.arange(request_count)[None, :], 0), axis=1)
     wanted = jnp.full((slots,), -1, jnp.int32).at[slot].set(requested % own_blocks)
     received_ids = lax.all_to_all(
         wanted.reshape(owners, capacity), ("row", "col"), split_axis=0, concat_axis=0, tiled=True
@@ -88,9 +86,13 @@
         occ_coeffs, window, (((1,), (1,)), ((), ())), preferred_element_type=jnp.float32
     )
     pieces = lax.all_to_all(
-        partial.reshape(col_count, own_rows, slab_width), "col", split_axis=0, concat_axis=0, tiled=True
+        partial.astype(jnp.bfloat16).reshape(col_count, own_rows, slab_width),
+        "col",
+        split_axis=0,
+        concat_axis=0,
+        tiled=True,
     )
-    density = jnp.sum(pieces, axis=0).astype(jnp.bfloat16)
+    density = jnp.sum(pieces.astype(jnp.float32), axis=0).astype(jnp.bfloat16)
     store = density.reshape(own_blocks, SH, slab_width)
     found = store[jnp.maximum(received_ids, 0)]
     replies = lax.all_to_all(
@@ -106,7 +108,7 @@
         dens_rows, colloc, grid_points, grid_weights, charge_sites, charge_proj, point_counts
     )
     terms = terms.astype(jnp.bfloat16).reshape(request_count, SH, slab_width)
-    tiles = jnp.take(terms, source_of, axis=0, mode="fill", fill_value=0)
+    tiles = terms[source_of]
     arrived = lax.all_to_all(
         tiles.reshape(owners, capacity * SH, slab_width),
         ("row", "col"),

time: 258 us -> 224 us (0.87)
  waiting for transfers between devices: 149 us -> 131 us
  other arithmetic: 11.9 us -> 4.32 us
  starting transfers between devices: 43.5 us -> 37 us
    all_to_all x1, waiting for transfers between devices: 38.9 us -> 20.6 us  [on_device(): lax.all_to_all(partial.astype(jnp.bfloat16).reshape(col_count, own_rows,...]
    select_n x2 -> x1, other arithmetic: 7.63 us -> 0.01 us  [on_device(): tiles = terms[source_of]]
    all_to_all x1, starting transfers between devices: 15.4 us -> 8.82 us  [on_device(): lax.all_to_all(found.reshape(owners, capacity * SH, slab_width), ('row',...]
  transfers between devices with their start and end apart: 7 -> 7, of which waited for: 5 -> 5; matrix products, arithmetic and copies ran while one was open for 7% -> 8% of each run, Pallas kernels for 0% -> 0%
where the time goes in v4:
time: 224 us
  waiting for transfers between devices  131 us (58%)
  starting transfers between devices  37 us (17%)
  matrix products  32.2 us (14%)
  local copies, waits for them, and re-layouts  18.6 us (8%)
  other arithmetic  4.32 us (2%)
    all_to_all x1, waiting for transfers between devices, on_device(): lax.all_to_all(tiles.reshape(owners, capacity * SH, slab_width), ('row',...  52.1 us
    all_to_all x1, waiting for transfers between devices, on_device(): lax.all_to_all(found.reshape(owners, capacity * SH, slab_width), ('row',...  51.8 us
    all_to_all x1, waiting for transfers between devices, on_device(): lax.all_to_all(partial.astype(jnp.bfloat16).reshape(col_count, own_rows,...  20.6 us
    all_to_all x1, starting transfers between devices, on_device(): lax.all_to_all(wanted.reshape(owners, capacity), ('row', 'col'), split_ax...  10.8 us
    dot_general x1, matrix products, on_device(): lax.dot_general(occ_coeffs, window, (((1,), (1,)), ((), ())), preferred_e...  10.6 us
    all_to_all x1, starting transfers between devices, on_device(): lax.all_to_all(found.reshape(owners, capacity * SH, slab_width), ('row',...  8.82 us
    dot_general x1, matrix products, batch_terms(): jnp.einsum('bfp,bsp->bfs', colloc, spread_back, preferred_element_type=jn...  7.61 us
    all_to_all x1, starting transfers between devices, on_device(): lax.all_to_all(partial.astype(jnp.bfloat16).reshape(col_count, own_rows,...  7.1 us
  transfers between devices with their start and end apart: 7, of which 5 were waited for; matrix products, arithmetic and copies ran while one was open for 8% of the time, Pallas kernels for 0%

profile of v4, /device:TPU:1, one launch (start us, length us, event | category | flops | bytes accessed | tf_op | source)
XLA Modules:
  0.0 223.6 jit_solution(9202306129481852917)
XLA Ops:
  0.0 0.0 copy-start
  0.0 1.0 slice.21
  1.0 1.3 collective-permute-start
  2.3 0.7 broadcast_remainder_fusion
  3.0 0.1 div.28
  3.1 0.1 rem.34
  3.2 0.7 compare_and_fusion
  3.9 0.1 ne.65
  4.0 0.9 collective-permute-done
  4.9 1.0 broadcast_select_fusion
  5.9 2.6 %collective-permute-start.1 = (bf16[128,1280]{1,0:T(8,128)(2,1)S(1)}, bf16[128,1280]{1,0:T(8,128)(2,1)S(1)}, u32[]{:S(2)}, u32[]{:S(2)}) collective-permute-start(bf16[128,1280]{1,0:T(8,128)(2,1)S(1)} %broadcast_select_fusion), channel_id=1, source_target_pairs={{0,32},{16,48},{1,33},{17,49},{2,34},{18,50},{3,35},{19,51},{4,36}... | collective-permute-start | bytes 983048 | tf_op jit(solution)/shard_map/ppermute | solution.py:19
  8.5 0.1 div.27
  8.5 0.1 and.29
  8.6 0.1 fusion.15
  8.7 0.2 reduce_window_sum.11
  8.9 5.9 %collective-permute-done.1 = bf16[128,1280]{1,0:T(8,128)(2,1)S(1)} collective-permute-done((bf16[128,1280]{1,0:T(8,128)(2,1)S(1)}, bf16[128,1280]{1,0:T(8,128)(2,1)S(1)}, u32[]{:S(2)}, u32[]{:S(2)}) %collective-permute-start.1) | collective-permute-done | bytes 327712 | tf_op jit(solution)/shard_map/ppermute | solution.py:19
  14.8 1.3 collective-permute-start.2
  16.2 0.2 select_reduce_fusion.1
  16.3 1.0 scatter_custom_fusion
  17.3 0.8 all_to_all.15
  18.1 10.8 %all-to-all-start = ((s32[128,1,2]{2,1,0:T(1,128)}), s32[128,1,2]{2,1,0:T(1,128)S(1)}, u32[]{:S(2)}, u32[]{:S(2)}) async-start(s32[128,1,2]{2,1,0:T(1,128)} %bitcast.2), calls=%async_computation | async-start | bytes 131072 | tf_op jit(solution)/shard_map/all_to_all | solution.py:81
  28.9 0.0 collective-permute-done.2
  28.9 10.6 %convolution_convert_fusion = bf16[128,6144]{1,0:T(8,128)(2,1)S(1)} fusion(bf16[6144,1280]{1,0:T(8,128)(2,1)} %param.8, bf16[128,1280]{1,0:T(8,128)(2,1)S(1)} %collective-permute-done.2, bf16[128,1280]{1,0:T(8,128)(2,1)S(1)} %broadcast_select_fusion.1, pred[]{:T(512)S(6)} %ge.9), kind=kOutput, calls=%fused_computation.7 | convolution fusion | flops 2014216192 | bytes 17956864 | tf_op jit(solution)/shard_map/dot_general | solution.py:85
  39.6 1.4 copy.48
  41.0 0.0 all-to-all-done
  41.0 7.1 %all-to-all-start.1 = ((bf16[16,384,128]{1,2,0:T(8,128)(2,1)}), bf16[16,384,128]{1,2,0:T(8,128)(2,1)S(1)}, u32[]{:S(2)}, u32[]{:S(2)}) async-start(bf16[16,384,128]{1,2,0:T(8,128)(2,1)} %bitcast.54), calls=%async_computation.1 | async-start | bytes 3145728 | tf_op jit(solution)/shard_map/all_to_all | solution.py:88
  48.1 0.5 broadcast.187
  48.6 1.0 fusion.26
  49.6 0.1 reshape.185
  49.7 20.6 %all-to-all-done.1 = bf16[16,384,128]{1,2,0:T(8,128)(2,1)S(1)} async-done(((bf16[16,384,128]{1,2,0:T(8,128)(2,1)}), bf16[16,384,128]{1,2,0:T(8,128)(2,1)S(1)}, u32[]{:S(2)}, u32[]{:S(2)}) %all-to-all-start.1) | async-done | bytes 1572896 | tf_op jit(solution)/shard_map/all_to_all | solution.py:88
  70.4 0.2 reduce_sum.36
  70.6 0.1 copy.33
  70.7 3.1 %gather_fusion = bf16[256,64,128]{2,1,0:T(8,128)(2,1)} fusion(bf16[6,64,128]{2,1,0:T(8,128)(2,1)S(1)} %bitcast.55, s32[1024]{0:T(1024)S(1)} %pad_clamp_fusion.2), kind=kCustom, calls=%fused_computation | custom fusion | bytes 8389632 | tf_op jit(solution)/shard_map/gather | solution.py:97
  73.8 8.8 %all-to-all-start.2 = ((bf16[128,128,128]{2,1,0:T(8,128)(2,1)}), bf16[128,128,128]{2,1,0:T(8,128)(2,1)}, u32[]{:S(2)}, u32[]{:S(2)}) async-start(bf16[128,128,128]{2,1,0:T(8,128)(2,1)} %bitcast.57), calls=%async_computation.2 | async-start | bytes 8388608 | tf_op jit(solution)/shard_map/all_to_all | solution.py:98
  82.7 0.1 select_reduce_fusion
  82.9 0.1 fusion.16
  82.9 51.8 %all-to-all-done.2 = bf16[128,128,128]{2,1,0:T(8,128)(2,1)} async-done(((bf16[128,128,128]{2,1,0:T(8,128)(2,1)}), bf16[128,128,128]{2,1,0:T(8,128)(2,1)}, u32[]{:S(2)}, u32[]{:S(2)}) %all-to-all-start.2) | async-done | bytes 4194336 | tf_op jit(solution)/shard_map/all_to_all | solution.py:98
  134.7 3.1 %gather_fusion.1 = bf16[128,64,128]{2,1,0:T(8,128)(2,1)S(1)} fusion(bf16[256,64,128]{2,1,0:T(8,128)(2,1)} %bitcast.7, s32[1024]{0:T(1024)S(1)} %pad_clamp_fusion.1), kind=kCustom, calls=%fused_computation.1 | custom fusion | bytes 4194816 | tf_op jit(solution)/shard_map/gather | solution.py:105
  137.9 4.8 %convolution_convert_fusion.1 = bf16[8,128,512]{2,1,0:T(8,128)(2,1)S(1)} fusion(bf16[8,1024,128]{2,1,0:T(8,128)(2,1)S(1)} %bitcast.59, bf16[8,1024,512]{2,1,0:T(8,128)(2,1)} %param.9), kind=kOutput, calls=%fused_computation.15 | convolution fusion | flops 1074266112 | bytes 11534336 | tf_op jit(solution)/shard_map/bfs,bfp->bsp/dot_general | solution.py:34
  142.7 4.7 %fusion.8 = bf16[8,512,128]{2,1,0:T(8,128)(2,1)S(1)} fusion(f32[8,512]{1,0:T(8,128)S(1)} %fusion.16, f32[512]{0:T(512)S(1)} %bitcast.63, f32[8,512]{1,0:T(8,128)S(1)} %get-tuple-element.10, f32[512]{0:T(512)S(1)} %bitcast.64, f32[8,512]{1,0:T(8,128)S(1)} %get-tuple-element.11, f32[512]{0:T(512)S(1)} %bitcast.62, f32[8,512]{1,0:T(8,128)S(1)} %get-tuple-element.9, ...), kind=kOutput, calls=%fused_computation.14 | convolution fusion | flops 1099431936 | bytes 2299904 | tf_op jit(solution)/shard_map/ks,bkp->bsp/dot_general | solution.py:42
  147.4 7.6 %convert_bitcast_fusion = bf16[8,1024,128]{1,2,0:T(8,128)(2,1)} fusion(bf16[8,512,128]{2,1,0:T(8,128)(2,1)S(1)} %fusion.8, bf16[8,1024,512]{2,1,0:T(8,128)(2,1)} %param.9), kind=kOutput, calls=%fused_computation.12 | convolution fusion | flops 1074790400 | bytes 11534336 | tf_op jit(solution)/shard_map/bfp,bsp->bfs/dot_general | solution.py:45
  155.0 3.0 %copy.37 = bf16[8,1024,128]{2,1,0:T(8,128)(2,1)S(1)} copy(bf16[8,1024,128]{1,2,0:T(8,128)(2,1)} %convert_bitcast_fusion) | data formatting | bytes 4194304 | tf_op jit(solution)/shard_map/convert_element_type | solution.py:110
  158.1 3.1 %gather_fusion.2 = bf16[256,64,128]{2,1,0:T(8,128)(2,1)} fusion(bf16[128,64,128]{2,1,0:T(8,128)(2,1)S(1)} %bitcast.56, s32[1024]{0:T(1024)S(1)} %pad_clamp_fusion), kind=kCustom, calls=%fused_computation.2 | custom fusion | bytes 8389632 | tf_op jit(solution)/shard_map/gather | solution.py:111
  161.1 5.1 %all-to-all-start.3 = ((bf16[128,128,128]{2,1,0:T(8,128)(2,1)}), bf16[128,128,128]{2,1,0:T(8,128)(2,1)}, u32[]{:S(2)}, u32[]{:S(2)}) async-start(bf16[128,128,128]{2,1,0:T(8,128)(2,1)} %bitcast.58), calls=%async_computation.3 | async-start | bytes 8388608 | tf_op jit(solution)/shard_map/all_to_all | solution.py:112
  166.2 0.1 eq.47
  166.4 52.1 %all-to-all-done.3 = bf16[128,128,128]{2,1,0:T(8,128)(2,1)} async-done(((bf16[128,128,128]{2,1,0:T(8,128)(2,1)}), bf16[128,128,128]{2,1,0:T(8,128)(2,1)}, u32[]{:S(2)}, u32[]{:S(2)}) %all-to-all-start.3) | async-done | bytes 4194336 | tf_op jit(solution)/shard_map/all_to_all | solution.py:112
  218.5 4.5 %fusion.2 = f32[6,64,128]{2,0,1:T(8,128)S(1)} fusion(bf16[256,64,128]{2,1,0:T(8,128)(2,1)} %bitcast.22, s32[256]{0:T(256)S(1)} %eq.47), kind=kOutput, calls=%fused_computation.8 | convolution fusion | flops 25167360 | bytes 4391936 | tf_op jit(solution)/shard_map/js,sfc->jfc/dot_general | solution.py:120
  222.9 0.7 copy.39
  (19 shorter events, 0.1 us)
Async XLA Ops:
  0.0 142.7 %copy-start = (bf16[512,128]{1,0:T(8,128)(2,1)S(1)}, bf16[512,128]{1,0:T(8,128)(2,1)}, u32[]{:S(2)}) copy-start(bf16[512,128]{1,0:T(8,128)(2,1)} %param.13) | copy-start | bytes 393220
  1.0 3.8 %collective-permute-start = (bf16[128,1280]{1,0:T(8,128)(2,1)S(1)}, bf16[128,1280]{1,0:T(8,128)(2,1)S(1)}, u32[]{:S(2)}, u32[]{:S(2)}) collective-permute-start(bf16[128,1280]{1,0:T(8,128)(2,1)S(1)} %slice.21), channel_id=1, source_target_pairs={{0,16},{1,17},{2,18},{3,19},{4,20},{5,21},{6,22},{7,23},{8,24},{9,... | collective-permute-start | bytes 983048 | tf_op jit(solution)/shard_map/ppermute | solution.py:19
  5.9 8.9 %collective-permute-start.1 = (bf16[128,1280]{1,0:T(8,128)(2,1)S(1)}, bf16[128,1280]{1,0:T(8,128)(2,1)S(1)}, u32[]{:S(2)}, u32[]{:S(2)}) collective-permute-start(bf16[128,1280]{1,0:T(8,128)(2,1)S(1)} %broadcast_select_fusion), channel_id=1, source_target_pairs={{0,32},{16,48},{1,33},{17,49},{2,34},{18,50},{3,35},{19,51},{4,36}... | collective-permute-start | bytes 983048 | tf_op jit(solution)/shard_map/ppermute | solution.py:19
  14.8 14.1 %collective-permute-start.2 = (bf16[128,1280]{1,0:T(8,128)(2,1)S(1)}, bf16[128,1280]{1,0:T(8,128)(2,1)S(1)}, u32[]{:S(2)}, u32[]{:S(2)}) collective-permute-start(bf16[128,1280]{1,0:T(8,128)(2,1)S(1)} %broadcast_select_fusion.1), channel_id=1, source_target_pairs={{0,64},{16,80},{32,96},{48,112},{1,65},{17,81},{33,97},{49,113},{2... | collective-permute-start | bytes 983048 | tf_op jit(solution)/shard_map/ppermute | solution.py:19
  18.1 22.9 %all-to-all-start = ((s32[128,1,2]{2,1,0:T(1,128)}), s32[128,1,2]{2,1,0:T(1,128)S(1)}, u32[]{:S(2)}, u32[]{:S(2)}) async-start(s32[128,1,2]{2,1,0:T(1,128)} %bitcast.2), calls=%async_computation | async-start | bytes 131072 | tf_op jit(solution)/shard_map/all_to_all | solution.py:81
  41.0 29.4 %all-to-all-start.1 = ((bf16[16,384,128]{1,2,0:T(8,128)(2,1)}), bf16[16,384,128]{1,2,0:T(8,128)(2,1)S(1)}, u32[]{:S(2)}, u32[]{:S(2)}) async-start(bf16[16,384,128]{1,2,0:T(8,128)(2,1)} %bitcast.54), calls=%async_computation.1 | async-start | bytes 3145728 | tf_op jit(solution)/shard_map/all_to_all | solution.py:88
  73.8 9.0 %copy-start.3 = (f32[3,512]{1,0:T(4,128)S(1)}, f32[3,512]{1,0:T(4,128)}, u32[]{:S(2)}) copy-start(f32[3,512]{1,0:T(4,128)} %param.12) | copy-start | bytes 18436
  73.8 9.0 %copy-start.2 = (f32[8,512]{1,0:T(8,128)S(1)}, f32[8,512]{1,0:T(8,128)}, u32[]{:S(2)}) copy-start(f32[8,512]{1,0:T(8,128)} %param.11) | copy-start | bytes 49156
  73.8 9.0 %copy-start.4 = (s32[8]{0:T(128)S(1)}, s32[8]{0:T(128)}, u32[]{:S(2)}) copy-start(s32[8]{0:T(128)} %param.15) | copy-start | bytes 100
  73.8 9.1 %copy-start.1 = (f32[8,3,512]{2,0,1:T(8,128)S(1)}, f32[8,3,512]{2,0,1:T(8,128)}, u32[]{:S(2)}) copy-start(f32[8,3,512]{2,0,1:T(8,128)} %param.10) | copy-start | bytes 147460
  73.8 60.9 %all-to-all-start.2 = ((bf16[128,128,128]{2,1,0:T(8,128)(2,1)}), bf16[128,128,128]{2,1,0:T(8,128)(2,1)}, u32[]{:S(2)}, u32[]{:S(2)}) async-start(bf16[128,128,128]{2,1,0:T(8,128)(2,1)} %bitcast.57), calls=%async_computation.2 | async-start | bytes 8388608 | tf_op jit(solution)/shard_map/all_to_all | solution.py:98
  161.1 57.3 %all-to-all-start.3 = ((bf16[128,128,128]{2,1,0:T(8,128)(2,1)}), bf16[128,128,128]{2,1,0:T(8,128)(2,1)}, u32[]{:S(2)}, u32[]{:S(2)}) async-start(bf16[128,128,128]{2,1,0:T(8,128)(2,1)} %bitcast.58), calls=%async_computation.3 | async-start | bytes 8388608 | tf_op jit(solution)/shard_map/all_to_all | solution.py:112

commit v5 on v3

--- a/solution.py
+++ b/solution.py
@@ -40,9 +40,9 @@
         projected * potential(grid_points, charge_sites) * (grid_weights * live)[:, None, :]
     ).astype(jnp.bfloat16)
     spread_back = jnp.einsum(
-        "ks,bkp->bsp", charge_proj, charges, preferred_element_type=jnp.float32
+        "bkp,ks->bps", charges, charge_proj, preferred_element_type=jnp.float32
     ).astype(jnp.bfloat16)
-    return jnp.einsum("bfp,bsp->bfs", colloc, spread_back, preferred_element_type=jnp.float32)
+    return jnp.einsum("bfp,bps->bfs", colloc, spread_back, preferred_element_type=jnp.float32)
 
 
 def on_device(
@@ -76,9 +76,7 @@
     rank = jnp.sum(before * onehot, axis=1)
     slot = owner * capacity + rank
     hit = slot[None, :] == jnp.arange(slots)[:, None]
-    source_of = jnp.sum(
-        jnp.where(hit, jnp.arange(request_count)[None, :] - request_count, 0), axis=1
-    ) + request_count
+    source_of = jnp.sum(jnp.where(hit, jnp.arange(request_count)[None, :], 0), axis=1)
     wanted = jnp.full((slots,), -1, jnp.int32).at[slot].set(requested % own_blocks)
     received_ids = lax.all_to_all(
         wanted.reshape(owners, capacity), ("row", "col"), split_axis=0, concat_axis=0, tiled=True
@@ -106,7 +104,7 @@
         dens_rows, colloc, grid_points, grid_weights, charge_sites, charge_proj, point_counts
     )
     terms = terms.astype(jnp.bfloat16).reshape(request_count, SH, slab_width)
-    tiles = jnp.take(terms, source_of, axis=0, mode="fill", fill_value=0)
+    tiles = terms[source_of]
     arrived = lax.all_to_all(
         tiles.reshape(owners, capacity * SH, slab_width),
         ("row", "col"),

time: 258 us -> 250 us (0.969)
  other arithmetic: 11.9 us -> 4.25 us
    select_n x2 -> x1, other arithmetic: 7.63 us -> 0.01 us  [on_device(): tiles = terms[source_of]]
where the time goes in v5:
time: 250 us; the launch traced here: 249 us
  waiting for transfers between devices  150 us (60%)
  starting transfers between devices  43.6 us (17%)
  matrix products  32.2 us (13%)
  local copies, waits for them, and re-layouts  19.1 us (8%)
  other arithmetic  4.25 us (2%)
    all_to_all x1, waiting for transfers between devices, on_device(): lax.all_to_all(tiles.reshape(owners, capacity * SH, slab_width), ('row',...  52.1 us
    all_to_all x1, waiting for transfers between devices, on_device(): lax.all_to_all(found.reshape(owners, capacity * SH, slab_width), ('row',...  51.8 us
    all_to_all x1, waiting for transfers between devices, on_device(): lax.all_to_all(partial.reshape(col_count, own_rows, slab_width), 'col', s...  38.9 us
    all_to_all x1, starting transfers between devices, on_device(): lax.all_to_all(found.reshape(owners, capacity * SH, slab_width), ('row',...  15.4 us
    all_to_all x1, starting transfers between devices, on_device(): lax.all_to_all(wanted.reshape(owners, capacity), ('row', 'col'), split_ax...  10.8 us
    dot_general x1, matrix products, on_device(): lax.dot_general(occ_coeffs, window, (((1,), (1,)), ((), ())), preferred_e...  10.6 us
    dot_general x1, matrix products, batch_terms(): jnp.einsum('bfp,bps->bfs', colloc, spread_back, preferred_element_type=jn...  7.61 us
    all_to_all x1, starting transfers between devices, on_device(): lax.all_to_all(partial.reshape(col_count, own_rows, slab_width), 'col', s...  7.1 us
  transfers between devices with their start and end apart: 7, of which 5 were waited for; matrix products, arithmetic and copies ran while one was open for 7% of the time, Pallas kernels for 0%

profile of v5, /device:TPU:1, one launch (start us, length us, event | category | flops | bytes accessed | tf_op | source)
XLA Modules:
  0.0 248.9 jit_solution(16854771163022042622)
XLA Ops:
  0.0 0.0 copy-start
  0.0 1.0 slice.21
  1.0 1.3 collective-permute-start
  2.3 0.7 broadcast_remainder_fusion
  3.0 0.1 div.28
  3.1 0.1 rem.34
  3.2 0.7 compare_and_fusion
  3.9 0.1 ne.65
  4.0 0.9 collective-permute-done
  4.9 1.0 broadcast_select_fusion
  5.9 2.6 %collective-permute-start.1 = (bf16[128,1280]{1,0:T(8,128)(2,1)S(1)}, bf16[128,1280]{1,0:T(8,128)(2,1)S(1)}, u32[]{:S(2)}, u32[]{:S(2)}) collective-permute-start(bf16[128,1280]{1,0:T(8,128)(2,1)S(1)} %broadcast_select_fusion), channel_id=1, source_target_pairs={{0,32},{16,48},{1,33},{17,49},{2,34},{18,50},{3,35},{19,51},{4,36}... | collective-permute-start | bytes 983048 | tf_op jit(solution)/shard_map/ppermute | solution.py:19
  8.5 0.1 div.27
  8.5 0.1 and.29
  8.6 0.1 fusion.16
  8.7 0.2 reduce_window_sum.11
  8.9 5.9 %collective-permute-done.1 = bf16[128,1280]{1,0:T(8,128)(2,1)S(1)} collective-permute-done((bf16[128,1280]{1,0:T(8,128)(2,1)S(1)}, bf16[128,1280]{1,0:T(8,128)(2,1)S(1)}, u32[]{:S(2)}, u32[]{:S(2)}) %collective-permute-start.1) | collective-permute-done | bytes 327712 | tf_op jit(solution)/shard_map/ppermute | solution.py:19
  14.8 1.3 collective-permute-start.2
  16.2 0.2 select_reduce_fusion.1
  16.3 1.0 scatter_custom_fusion
  17.3 0.8 all_to_all.15
  18.1 10.8 %all-to-all-start = ((s32[128,1,2]{2,1,0:T(1,128)}), s32[128,1,2]{2,1,0:T(1,128)S(1)}, u32[]{:S(2)}, u32[]{:S(2)}) async-start(s32[128,1,2]{2,1,0:T(1,128)} %bitcast.2), calls=%async_computation | async-start | bytes 131072 | tf_op jit(solution)/shard_map/all_to_all | solution.py:81
  28.9 0.0 collective-permute-done.2
  28.9 10.6 %fusion.11 = f32[128,6144]{1,0:T(8,128)S(1)} fusion(bf16[6144,1280]{1,0:T(8,128)(2,1)} %param.8, bf16[128,1280]{1,0:T(8,128)(2,1)S(1)} %collective-permute-done.2, bf16[128,1280]{1,0:T(8,128)(2,1)S(1)} %broadcast_select_fusion.1, pred[]{:T(512)S(6)} %ge.9), kind=kOutput, calls=%fused_computation.15 | convolution fusion | flops 2013429760 | bytes 19529728 | tf_op jit(solution)/shard_map/dot_general | solution.py:85
  39.5 2.0 copy.48
  41.5 0.0 all-to-all-done
  41.5 7.1 %all-to-all-start.1 = ((f32[16,384,128]{1,2,0:T(8,128)}), f32[16,384,128]{1,2,0:T(8,128)S(1)}, u32[]{:S(2)}, u32[]{:S(2)}) async-start(f32[16,384,128]{1,2,0:T(8,128)} %bitcast.54), calls=%async_computation.1 | async-start | bytes 6291456 | tf_op jit(solution)/shard_map/all_to_all | solution.py:88
  48.6 0.5 broadcast.187
  49.1 1.0 fusion.27
  50.1 0.1 reshape.184
  50.3 38.9 %all-to-all-done.1 = f32[16,384,128]{1,2,0:T(8,128)S(1)} async-done(((f32[16,384,128]{1,2,0:T(8,128)}), f32[16,384,128]{1,2,0:T(8,128)S(1)}, u32[]{:S(2)}, u32[]{:S(2)}) %all-to-all-start.1) | async-done | bytes 3145760 | tf_op jit(solution)/shard_map/all_to_all | solution.py:88
  89.2 0.1 reduce_sum.33
  89.4 0.1 copy.33
  89.5 3.1 %gather_fusion = bf16[256,64,128]{2,1,0:T(8,128)(2,1)} fusion(bf16[6,64,128]{2,1,0:T(8,128)(2,1)S(1)} %bitcast.55, s32[1024]{0:T(1024)S(1)} %pad_clamp_fusion.2), kind=kCustom, calls=%fused_computation | custom fusion | bytes 8389632 | tf_op jit(solution)/shard_map/gather | solution.py:93
  92.6 15.4 %all-to-all-start.2 = ((bf16[128,128,128]{2,1,0:T(8,128)(2,1)}), bf16[128,128,128]{2,1,0:T(8,128)(2,1)}, u32[]{:S(2)}, u32[]{:S(2)}) async-start(bf16[128,128,128]{2,1,0:T(8,128)(2,1)} %bitcast.57), calls=%async_computation.2 | async-start | bytes 8388608 | tf_op jit(solution)/shard_map/all_to_all | solution.py:94
  108.0 0.1 select_reduce_fusion
  108.1 0.1 fusion.17
  108.2 51.8 %all-to-all-done.2 = bf16[128,128,128]{2,1,0:T(8,128)(2,1)} async-done(((bf16[128,128,128]{2,1,0:T(8,128)(2,1)}), bf16[128,128,128]{2,1,0:T(8,128)(2,1)}, u32[]{:S(2)}, u32[]{:S(2)}) %all-to-all-start.2) | async-done | bytes 4194336 | tf_op jit(solution)/shard_map/all_to_all | solution.py:94
  160.0 3.1 %gather_fusion.1 = bf16[128,64,128]{2,1,0:T(8,128)(2,1)S(1)} fusion(bf16[256,64,128]{2,1,0:T(8,128)(2,1)} %bitcast.7, s32[1024]{0:T(1024)S(1)} %pad_clamp_fusion.1), kind=kCustom, calls=%fused_computation.1 | custom fusion | bytes 4194816 | tf_op jit(solution)/shard_map/gather | solution.py:101
  163.2 4.8 %convolution_convert_fusion = bf16[8,128,512]{2,1,0:T(8,128)(2,1)S(1)} fusion(bf16[8,1024,128]{2,1,0:T(8,128)(2,1)S(1)} %bitcast.59, bf16[8,1024,512]{2,1,0:T(8,128)(2,1)} %param.9), kind=kOutput, calls=%fused_computation.14 | convolution fusion | flops 1074266112 | bytes 11534336 | tf_op jit(solution)/shard_map/bfs,bfp->bsp/dot_general | solution.py:34
  168.0 4.7 %fusion.8 = bf16[8,512,128]{2,1,0:T(8,128)(2,1)S(1)} fusion(f32[8,512]{1,0:T(8,128)S(1)} %fusion.17, f32[512]{0:T(512)S(1)} %bitcast.63, f32[8,512]{1,0:T(8,128)S(1)} %get-tuple-element.10, f32[512]{0:T(512)S(1)} %bitcast.64, f32[8,512]{1,0:T(8,128)S(1)} %get-tuple-element.11, f32[512]{0:T(512)S(1)} %bitcast.62, f32[8,512]{1,0:T(8,128)S(1)} %get-tuple-element.9, ...), kind=kOutput, calls=%fused_computation.13 | convolution fusion | flops 1099431936 | bytes 2299904 | tf_op jit(solution)/shard_map/bkp,ks->bps/dot_general | solution.py:42
  172.7 7.6 %convert_bitcast_fusion = bf16[8,1024,128]{1,2,0:T(8,128)(2,1)} fusion(bf16[8,512,128]{2,1,0:T(8,128)(2,1)S(1)} %fusion.8, bf16[8,1024,512]{2,1,0:T(8,128)(2,1)} %param.9), kind=kOutput, calls=%fused_computation.12 | convolution fusion | flops 1074790400 | bytes 11534336 | tf_op jit(solution)/shard_map/bfp,bps->bfs/dot_general | solution.py:45
  180.3 3.0 %copy.37 = bf16[8,1024,128]{2,1,0:T(8,128)(2,1)S(1)} copy(bf16[8,1024,128]{1,2,0:T(8,128)(2,1)} %convert_bitcast_fusion) | data formatting | bytes 4194304 | tf_op jit(solution)/shard_map/convert_element_type | solution.py:106
  183.3 3.1 %gather_fusion.2 = bf16[256,64,128]{2,1,0:T(8,128)(2,1)} fusion(bf16[128,64,128]{2,1,0:T(8,128)(2,1)S(1)} %bitcast.56, s32[1024]{0:T(1024)S(1)} %pad_clamp_fusion), kind=kCustom, calls=%fused_computation.2 | custom fusion | bytes 8389632 | tf_op jit(solution)/shard_map/gather | solution.py:107
  186.4 5.1 %all-to-all-start.3 = ((bf16[128,128,128]{2,1,0:T(8,128)(2,1)}), bf16[128,128,128]{2,1,0:T(8,128)(2,1)}, u32[]{:S(2)}, u32[]{:S(2)}) async-start(bf16[128,128,128]{2,1,0:T(8,128)(2,1)} %bitcast.58), calls=%async_computation.3 | async-start | bytes 8388608 | tf_op jit(solution)/shard_map/all_to_all | solution.py:108
  191.5 0.1 eq.47
  191.6 52.1 %all-to-all-done.3 = bf16[128,128,128]{2,1,0:T(8,128)(2,1)} async-done(((bf16[128,128,128]{2,1,0:T(8,128)(2,1)}), bf16[128,128,128]{2,1,0:T(8,128)(2,1)}, u32[]{:S(2)}, u32[]{:S(2)}) %all-to-all-start.3) | async-done | bytes 4194336 | tf_op jit(solution)/shard_map/all_to_all | solution.py:108
  243.7 4.5 %fusion.2 = f32[6,64,128]{2,0,1:T(8,128)S(1)} fusion(bf16[256,64,128]{2,1,0:T(8,128)(2,1)} %bitcast.22, s32[256]{0:T(256)S(1)} %eq.47), kind=kOutput, calls=%fused_computation.7 | convolution fusion | flops 25167360 | bytes 4391936 | tf_op jit(solution)/shard_map/js,sfc->jfc/dot_general | solution.py:116
  248.2 0.7 copy.39
  (19 shorter events, 0.1 us)
Async XLA Ops:
  0.0 168.0 %copy-start = (bf16[512,128]{1,0:T(8,128)(2,1)S(1)}, bf16[512,128]{1,0:T(8,128)(2,1)}, u32[]{:S(2)}) copy-start(bf16[512,128]{1,0:T(8,128)(2,1)} %param.13) | copy-start | bytes 393220
  1.0 3.8 %collective-permute-start = (bf16[128,1280]{1,0:T(8,128)(2,1)S(1)}, bf16[128,1280]{1,0:T(8,128)(2,1)S(1)}, u32[]{:S(2)}, u32[]{:S(2)}) collective-permute-start(bf16[128,1280]{1,0:T(8,128)(2,1)S(1)} %slice.21), channel_id=1, source_target_pairs={{0,16},{1,17},{2,18},{3,19},{4,20},{5,21},{6,22},{7,23},{8,24},{9,... | collective-permute-start | bytes 983048 | tf_op jit(solution)/shard_map/ppermute | solution.py:19
  5.9 8.9 %collective-permute-start.1 = (bf16[128,1280]{1,0:T(8,128)(2,1)S(1)}, bf16[128,1280]{1,0:T(8,128)(2,1)S(1)}, u32[]{:S(2)}, u32[]{:S(2)}) collective-permute-start(bf16[128,1280]{1,0:T(8,128)(2,1)S(1)} %broadcast_select_fusion), channel_id=1, source_target_pairs={{0,32},{16,48},{1,33},{17,49},{2,34},{18,50},{3,35},{19,51},{4,36}... | collective-permute-start | bytes 983048 | tf_op jit(solution)/shard_map/ppermute | solution.py:19
  14.8 14.1 %collective-permute-start.2 = (bf16[128,1280]{1,0:T(8,128)(2,1)S(1)}, bf16[128,1280]{1,0:T(8,128)(2,1)S(1)}, u32[]{:S(2)}, u32[]{:S(2)}) collective-permute-start(bf16[128,1280]{1,0:T(8,128)(2,1)S(1)} %broadcast_select_fusion.1), channel_id=1, source_target_pairs={{0,64},{16,80},{32,96},{48,112},{1,65},{17,81},{33,97},{49,113},{2... | collective-permute-start | bytes 983048 | tf_op jit(solution)/shard_map/ppermute | solution.py:19
  18.1 23.4 %all-to-all-start = ((s32[128,1,2]{2,1,0:T(1,128)}), s32[128,1,2]{2,1,0:T(1,128)S(1)}, u32[]{:S(2)}, u32[]{:S(2)}) async-start(s32[128,1,2]{2,1,0:T(1,128)} %bitcast.2), calls=%async_computation | async-start | bytes 131072 | tf_op jit(solution)/shard_map/all_to_all | solution.py:81
  41.5 47.7 %all-to-all-start.1 = ((f32[16,384,128]{1,2,0:T(8,128)}), f32[16,384,128]{1,2,0:T(8,128)S(1)}, u32[]{:S(2)}, u32[]{:S(2)}) async-start(f32[16,384,128]{1,2,0:T(8,128)} %bitcast.54), calls=%async_computation.1 | async-start | bytes 6291456 | tf_op jit(solution)/shard_map/all_to_all | solution.py:88
  92.6 15.5 %copy-start.3 = (f32[3,512]{1,0:T(4,128)S(1)}, f32[3,512]{1,0:T(4,128)}, u32[]{:S(2)}) copy-start(f32[3,512]{1,0:T(4,128)} %param.12) | copy-start | bytes 18436
  92.6 15.6 %copy-start.2 = (f32[8,512]{1,0:T(8,128)S(1)}, f32[8,512]{1,0:T(8,128)}, u32[]{:S(2)}) copy-start(f32[8,512]{1,0:T(8,128)} %param.11) | copy-start | bytes 49156
  92.6 15.6 %copy-start.4 = (s32[8]{0:T(128)S(1)}, s32[8]{0:T(128)}, u32[]{:S(2)}) copy-start(s32[8]{0:T(128)} %param.15) | copy-start | bytes 100
  92.6 15.7 %copy-start.1 = (f32[8,3,512]{2,0,1:T(8,128)S(1)}, f32[8,3,512]{2,0,1:T(8,128)}, u32[]{:S(2)}) copy-start(f32[8,3,512]{2,0,1:T(8,128)} %param.10) | copy-start | bytes 147460
  92.6 67.5 %all-to-all-start.2 = ((bf16[128,128,128]{2,1,0:T(8,128)(2,1)}), bf16[128,128,128]{2,1,0:T(8,128)(2,1)}, u32[]{:S(2)}, u32[]{:S(2)}) async-start(bf16[128,128,128]{2,1,0:T(8,128)(2,1)} %bitcast.57), calls=%async_computation.2 | async-start | bytes 8388608 | tf_op jit(solution)/shard_map/all_to_all | solution.py:94
  186.4 57.3 %all-to-all-start.3 = ((bf16[128,128,128]{2,1,0:T(8,128)(2,1)}), bf16[128,128,128]{2,1,0:T(8,128)(2,1)}, u32[]{:S(2)}, u32[]{:S(2)}) async-start(bf16[128,128,128]{2,1,0:T(8,128)(2,1)} %bitcast.58), calls=%async_computation.3 | async-start | bytes 8388608 | tf_op jit(solution)/shard_map/all_to_all | solution.py:108

commit v6 on v5

--- a/solution.py
+++ b/solution.py
@@ -13,13 +13,20 @@
 def broadcast_from_first(value, axis):
     size = lax.axis_size(axis)
     index = lax.axis_index(axis)
-    have = 1
-    while have < size:
-        pairs = [(src, src + have) for src in range(have) if src + have < size]
-        moved = lax.ppermute(value, axis, pairs)
-        value = jnp.where(index >= have, moved, value)
-        have *= 2
-    return value
+    if size != 8:
+        have = 1
+        while have < size:
+            pairs = [(src, src + have) for src in range(have) if src + have < size]
+            moved = lax.ppermute(value, axis, pairs)
+            value = jnp.where(index >= have, moved, value)
+            have *= 2
+        return value
+    first = [lax.ppermute(value, axis, [(0, dst)]) for dst in (1, 2, 6)]
+    value = jnp.where(index == 1, first[0], value)
+    value = jnp.where(index == 2, first[1], value)
+    value = jnp.where(index == 6, first[2], value)
+    second = lax.ppermute(value, axis, [(1, 3), (2, 4), (6, 7), (0, 5)])
+    return jnp.where((index == 3) | (index == 4) | (index == 5) | (index == 7), second, value)
 
 
 def potential(points, charge_sites):

time: 250 us -> 248 us (level)
    ppermute x3 -> x4, waiting for transfers between devices: 6.76 us -> 5.39 us  [the longest x3 5.39 us: broadcast_from_first(): first = [lax.ppermute(value, axis, [(0, dst)]) for dst in (1, 2, 6)]]
    ppermute x3 -> x4, starting transfers between devices: 5.18 us -> 3.97 us  [the longest x3 2.66 us: broadcast_from_first(): first = [lax.ppermute(value, axis, [(0, dst)]) for dst in (1, 2, 6)]]
  transfers between devices with their start and end apart: 7 -> 8, of which waited for: 5 -> 4; matrix products, arithmetic and copies ran while one was open for 7% -> 7% of each run, Pallas kernels for 0% -> 0%
where the time goes in v6:
time: 248 us; the launch traced here: 247 us
  waiting for transfers between devices  148 us (60%)
  starting transfers between devices  43 us (17%)
  matrix products  32.1 us (13%)
  local copies, waits for them, and re-layouts  19.1 us (8%)
  other arithmetic  4.23 us (2%)
    all_to_all x1, waiting for transfers between devices, on_device(): lax.all_to_all(tiles.reshape(owners, capacity * SH, slab_width), ('row',...  52.1 us
    all_to_all x1, waiting for transfers between devices, on_device(): lax.all_to_all(found.reshape(owners, capacity * SH, slab_width), ('row',...  51.8 us
    all_to_all x1, waiting for transfers between devices, on_device(): lax.all_to_all(partial.reshape(col_count, own_rows, slab_width), 'col', s...  38.9 us
    all_to_all x1, starting transfers between devices, on_device(): lax.all_to_all(found.reshape(owners, capacity * SH, slab_width), ('row',...  15.4 us
    all_to_all x1, starting transfers between devices, on_device(): lax.all_to_all(wanted.reshape(owners, capacity), ('row', 'col'), split_ax...  11.4 us
    dot_general x1, matrix products, on_device(): lax.dot_general(occ_coeffs, window, (((1,), (1,)), ((), ())), preferred_e...  10.6 us
    dot_general x1, matrix products, batch_terms(): jnp.einsum('bfp,bps->bfs', colloc, spread_back, preferred_element_type=jn...  7.6 us
    all_to_all x1, starting transfers between devices, on_device(): lax.all_to_all(partial.reshape(col_count, own_rows, slab_width), 'col', s...  7.1 us
  transfers between devices with their start and end apart: 8, of which 4 were waited for; matrix products, arithmetic and copies ran while one was open for 7% of the time, Pallas kernels for 0%

profile of v6, /device:TPU:1, one launch (start us, length us, event | category | flops | bytes accessed | tf_op | source)
XLA Modules:
  0.0 246.9 jit_solution(13918662976258914914)
XLA Ops:
  0.0 1.0 slice.21
  1.0 0.7 collective-permute-start
  1.7 0.7 collective-permute-start.1
  2.4 1.3 collective-permute-start.2
  3.7 0.7 broadcast_remainder_fusion
  4.4 0.7 compare_and_fusion
  5.1 0.1 div.28
  5.2 0.1 rem.34
  5.3 0.1 ne.65
  5.4 0.1 div.27
  5.5 0.1 and.29
  5.5 0.1 fusion.16
  5.6 0.2 reduce_window_sum.11
  5.8 0.0 collective-permute-done
  5.8 0.0 collective-permute-done.1
  5.8 5.4 %collective-permute-done.2 = bf16[128,1280]{1,0:T(8,128)(2,1)S(1)} collective-permute-done((bf16[128,1280]{1,0:T(8,128)(2,1)S(1)}, bf16[128,1280]{1,0:T(8,128)(2,1)S(1)}, u32[]{:S(2)}, u32[]{:S(2)}) %collective-permute-start.2) | collective-permute-done | bytes 327712 | tf_op jit(solution)/shard_map/ppermute | solution.py:24
  11.2 1.0 select_select_fusion
  12.2 1.3 collective-permute-start.3
  13.6 0.2 select_reduce_fusion.1
  13.7 1.0 scatter_custom_fusion
  14.7 0.8 all_to_all.15
  15.5 11.4 %all-to-all-start = ((s32[128,1,2]{2,1,0:T(1,128)}), s32[128,1,2]{2,1,0:T(1,128)S(1)}, u32[]{:S(2)}, u32[]{:S(2)}) async-start(s32[128,1,2]{2,1,0:T(1,128)} %bitcast.2), calls=%async_computation | async-start | bytes 131072 | tf_op jit(solution)/shard_map/all_to_all | solution.py:88
  27.0 10.6 %fusion.11 = f32[128,6144]{1,0:T(8,128)S(1)} fusion(bf16[6144,1280]{1,0:T(8,128)(2,1)} %param.8, bf16[128,1280]{1,0:T(8,128)(2,1)S(1)} %collective-permute-done.3, bf16[128,1280]{1,0:T(8,128)(2,1)S(1)} %select_select_fusion, pred[]{:T(512)S(6)} %or.11), kind=kOutput, calls=%fused_computation.15 | convolution fusion | flops 2013429760 | bytes 19529728 | tf_op jit(solution)/shard_map/dot_general | solution.py:92
  37.6 2.0 copy.48
  39.5 0.0 all-to-all-done
  39.5 7.1 %all-to-all-start.1 = ((f32[16,384,128]{1,2,0:T(8,128)}), f32[16,384,128]{1,2,0:T(8,128)S(1)}, u32[]{:S(2)}, u32[]{:S(2)}) async-start(f32[16,384,128]{1,2,0:T(8,128)} %bitcast.54), calls=%async_computation.1 | async-start | bytes 6291456 | tf_op jit(solution)/shard_map/all_to_all | solution.py:95
  46.6 0.5 broadcast.187
  47.2 1.0 fusion.27
  48.2 0.1 reshape.184
  48.3 38.9 %all-to-all-done.1 = f32[16,384,128]{1,2,0:T(8,128)S(1)} async-done(((f32[16,384,128]{1,2,0:T(8,128)}), f32[16,384,128]{1,2,0:T(8,128)S(1)}, u32[]{:S(2)}, u32[]{:S(2)}) %all-to-all-start.1) | async-done | bytes 3145760 | tf_op jit(solution)/shard_map/all_to_all | solution.py:95
  87.2 0.1 reduce_sum.33
  87.4 0.1 copy.33
  87.5 3.1 %gather_fusion = bf16[256,64,128]{2,1,0:T(8,128)(2,1)} fusion(bf16[6,64,128]{2,1,0:T(8,128)(2,1)S(1)} %bitcast.55, s32[1024]{0:T(1024)S(1)} %pad_clamp_fusion.2), kind=kCustom, calls=%fused_computation | custom fusion | bytes 8389632 | tf_op jit(solution)/shard_map/gather | solution.py:100
  90.6 15.4 %all-to-all-start.2 = ((bf16[128,128,128]{2,1,0:T(8,128)(2,1)}), bf16[128,128,128]{2,1,0:T(8,128)(2,1)}, u32[]{:S(2)}, u32[]{:S(2)}) async-start(bf16[128,128,128]{2,1,0:T(8,128)(2,1)} %bitcast.57), calls=%async_computation.2 | async-start | bytes 8388608 | tf_op jit(solution)/shard_map/all_to_all | solution.py:101
  106.0 0.1 select_reduce_fusion
  106.2 0.1 fusion.17
  106.3 51.8 %all-to-all-done.2 = bf16[128,128,128]{2,1,0:T(8,128)(2,1)} async-done(((bf16[128,128,128]{2,1,0:T(8,128)(2,1)}), bf16[128,128,128]{2,1,0:T(8,128)(2,1)}, u32[]{:S(2)}, u32[]{:S(2)}) %all-to-all-start.2) | async-done | bytes 4194336 | tf_op jit(solution)/shard_map/all_to_all | solution.py:101
  158.1 3.1 %gather_fusion.1 = bf16[128,64,128]{2,1,0:T(8,128)(2,1)S(1)} fusion(bf16[256,64,128]{2,1,0:T(8,128)(2,1)} %bitcast.7, s32[1024]{0:T(1024)S(1)} %pad_clamp_fusion.1), kind=kCustom, calls=%fused_computation.1 | custom fusion | bytes 4194816 | tf_op jit(solution)/shard_map/gather | solution.py:108
  161.2 4.8 %convolution_convert_fusion = bf16[8,128,512]{2,1,0:T(8,128)(2,1)S(1)} fusion(bf16[8,1024,128]{2,1,0:T(8,128)(2,1)S(1)} %bitcast.59, bf16[8,1024,512]{2,1,0:T(8,128)(2,1)} %param.9), kind=kOutput, calls=%fused_computation.14 | convolution fusion | flops 1074266112 | bytes 11534336 | tf_op jit(solution)/shard_map/bfs,bfp->bsp/dot_general | solution.py:41
  166.0 4.7 %fusion.8 = bf16[8,512,128]{2,1,0:T(8,128)(2,1)S(1)} fusion(f32[8,512]{1,0:T(8,128)S(1)} %fusion.17, f32[512]{0:T(512)S(1)} %bitcast.63, f32[8,512]{1,0:T(8,128)S(1)} %get-tuple-element.10, f32[512]{0:T(512)S(1)} %bitcast.64, f32[8,512]{1,0:T(8,128)S(1)} %get-tuple-element.11, f32[512]{0:T(512)S(1)} %bitcast.62, f32[8,512]{1,0:T(8,128)S(1)} %get-tuple-element.9, ...), kind=kOutput, calls=%fused_computation.13 | convolution fusion | flops 1099431936 | bytes 2299904 | tf_op jit(solution)/shard_map/bkp,ks->bps/dot_general | solution.py:49
  170.7 7.6 %convert_bitcast_fusion = bf16[8,1024,128]{1,2,0:T(8,128)(2,1)} fusion(bf16[8,512,128]{2,1,0:T(8,128)(2,1)S(1)} %fusion.8, bf16[8,1024,512]{2,1,0:T(8,128)(2,1)} %param.9), kind=kOutput, calls=%fused_computation.12 | convolution fusion | flops 1074790400 | bytes 11534336 | tf_op jit(solution)/shard_map/bfp,bps->bfs/dot_general | solution.py:52
  178.3 3.0 %copy.37 = bf16[8,1024,128]{2,1,0:T(8,128)(2,1)S(1)} copy(bf16[8,1024,128]{1,2,0:T(8,128)(2,1)} %convert_bitcast_fusion) | data formatting | bytes 4194304 | tf_op jit(solution)/shard_map/convert_element_type | solution.py:113
  181.3 3.1 %gather_fusion.2 = bf16[256,64,128]{2,1,0:T(8,128)(2,1)} fusion(bf16[128,64,128]{2,1,0:T(8,128)(2,1)S(1)} %bitcast.56, s32[1024]{0:T(1024)S(1)} %pad_clamp_fusion), kind=kCustom, calls=%fused_computation.2 | custom fusion | bytes 8389632 | tf_op jit(solution)/shard_map/gather | solution.py:114
  184.4 5.1 %all-to-all-start.3 = ((bf16[128,128,128]{2,1,0:T(8,128)(2,1)}), bf16[128,128,128]{2,1,0:T(8,128)(2,1)}, u32[]{:S(2)}, u32[]{:S(2)}) async-start(bf16[128,128,128]{2,1,0:T(8,128)(2,1)} %bitcast.58), calls=%async_computation.3 | async-start | bytes 8388608 | tf_op jit(solution)/shard_map/all_to_all | solution.py:115
  189.5 0.1 eq.68
  189.6 52.1 %all-to-all-done.3 = bf16[128,128,128]{2,1,0:T(8,128)(2,1)} async-done(((bf16[128,128,128]{2,1,0:T(8,128)(2,1)}), bf16[128,128,128]{2,1,0:T(8,128)(2,1)}, u32[]{:S(2)}, u32[]{:S(2)}) %all-to-all-start.3) | async-done | bytes 4194336 | tf_op jit(solution)/shard_map/all_to_all | solution.py:115
  241.7 4.5 %fusion.2 = f32[6,64,128]{2,0,1:T(8,128)S(1)} fusion(bf16[256,64,128]{2,1,0:T(8,128)(2,1)} %bitcast.22, s32[256]{0:T(256)S(1)} %eq.68), kind=kOutput, calls=%fused_computation.7 | convolution fusion | flops 25167360 | bytes 4391936 | tf_op jit(solution)/shard_map/js,sfc->jfc/dot_general | solution.py:123
  246.2 0.7 copy.39
  (20 shorter events, 0.1 us)
Async XLA Ops:
  0.0 166.0 %copy-start = (bf16[512,128]{1,0:T(8,128)(2,1)S(1)}, bf16[512,128]{1,0:T(8,128)(2,1)}, u32[]{:S(2)}) copy-start(bf16[512,128]{1,0:T(8,128)(2,1)} %param.13) | copy-start | bytes 393220
  1.0 4.8 %collective-permute-start = (bf16[128,1280]{1,0:T(8,128)(2,1)S(1)}, bf16[128,1280]{1,0:T(8,128)(2,1)S(1)}, u32[]{:S(2)}, u32[]{:S(2)}) collective-permute-start(bf16[128,1280]{1,0:T(8,128)(2,1)S(1)} %slice.21), channel_id=1, source_target_pairs={{0,96},{1,97},{2,98},{3,99},{4,100},{5,101},{6,102},{7,103},{8,104... | collective-permute-start | bytes 983048 | tf_op jit(solution)/shard_map/ppermute | solution.py:24
  1.7 4.1 %collective-permute-start.1 = (bf16[128,1280]{1,0:T(8,128)(2,1)S(1)}, bf16[128,1280]{1,0:T(8,128)(2,1)S(1)}, u32[]{:S(2)}, u32[]{:S(2)}) collective-permute-start(bf16[128,1280]{1,0:T(8,128)(2,1)S(1)} %slice.21), channel_id=1, source_target_pairs={{0,32},{1,33},{2,34},{3,35},{4,36},{5,37},{6,38},{7,39},{8,40},{9,... | collective-permute-start | bytes 983048 | tf_op jit(solution)/shard_map/ppermute | solution.py:24
  2.4 8.8 %collective-permute-start.2 = (bf16[128,1280]{1,0:T(8,128)(2,1)S(1)}, bf16[128,1280]{1,0:T(8,128)(2,1)S(1)}, u32[]{:S(2)}, u32[]{:S(2)}) collective-permute-start(bf16[128,1280]{1,0:T(8,128)(2,1)S(1)} %slice.21), channel_id=1, source_target_pairs={{0,16},{1,17},{2,18},{3,19},{4,20},{5,21},{6,22},{7,23},{8,24},{9,... | collective-permute-start | bytes 983048 | tf_op jit(solution)/shard_map/ppermute | solution.py:24
  12.2 14.7 %collective-permute-start.3 = (bf16[128,1280]{1,0:T(8,128)(2,1)S(1)}, bf16[128,1280]{1,0:T(8,128)(2,1)S(1)}, u32[]{:S(2)}, u32[]{:S(2)}) collective-permute-start(bf16[128,1280]{1,0:T(8,128)(2,1)S(1)} %select_select_fusion), channel_id=1, source_target_pairs={{16,48},{32,64},{96,112},{0,80},{17,49},{33,65},{97,113},{1,81},{1... | collective-permute-start | bytes 983048 | tf_op jit(solution)/shard_map/ppermute | solution.py:28
  15.5 24.0 %all-to-all-start = ((s32[128,1,2]{2,1,0:T(1,128)}), s32[128,1,2]{2,1,0:T(1,128)S(1)}, u32[]{:S(2)}, u32[]{:S(2)}) async-start(s32[128,1,2]{2,1,0:T(1,128)} %bitcast.2), calls=%async_computation | async-start | bytes 131072 | tf_op jit(solution)/shard_map/all_to_all | solution.py:88
  39.5 47.7 %all-to-all-start.1 = ((f32[16,384,128]{1,2,0:T(8,128)}), f32[16,384,128]{1,2,0:T(8,128)S(1)}, u32[]{:S(2)}, u32[]{:S(2)}) async-start(f32[16,384,128]{1,2,0:T(8,128)} %bitcast.54), calls=%async_computation.1 | async-start | bytes 6291456 | tf_op jit(solution)/shard_map/all_to_all | solution.py:95
  90.6 15.5 %copy-start.3 = (f32[3,512]{1,0:T(4,128)S(1)}, f32[3,512]{1,0:T(4,128)}, u32[]{:S(2)}) copy-start(f32[3,512]{1,0:T(4,128)} %param.12) | copy-start | bytes 18436
  90.6 15.6 %copy-start.2 = (f32[8,512]{1,0:T(8,128)S(1)}, f32[8,512]{1,0:T(8,128)}, u32[]{:S(2)}) copy-start(f32[8,512]{1,0:T(8,128)} %param.11) | copy-start | bytes 49156
  90.6 15.6 %copy-start.4 = (s32[8]{0:T(128)S(1)}, s32[8]{0:T(128)}, u32[]{:S(2)}) copy-start(s32[8]{0:T(128)} %param.15) | copy-start | bytes 100
  90.6 15.7 %copy-start.1 = (f32[8,3,512]{2,0,1:T(8,128)S(1)}, f32[8,3,512]{2,0,1:T(8,128)}, u32[]{:S(2)}) copy-start(f32[8,3,512]{2,0,1:T(8,128)} %param.10) | copy-start | bytes 147460
  90.6 67.5 %all-to-all-start.2 = ((bf16[128,128,128]{2,1,0:T(8,128)(2,1)}), bf16[128,128,128]{2,1,0:T(8,128)(2,1)}, u32[]{:S(2)}, u32[]{:S(2)}) async-start(bf16[128,128,128]{2,1,0:T(8,128)(2,1)} %bitcast.57), calls=%async_computation.2 | async-start | bytes 8388608 | tf_op jit(solution)/shard_map/all_to_all | solution.py:101
  184.4 57.3 %all-to-all-start.3 = ((bf16[128,128,128]{2,1,0:T(8,128)(2,1)}), bf16[128,128,128]{2,1,0:T(8,128)(2,1)}, u32[]{:S(2)}, u32[]{:S(2)}) async-start(bf16[128,128,128]{2,1,0:T(8,128)(2,1)} %bitcast.58), calls=%async_computation.3 | async-start | bytes 8388608 | tf_op jit(solution)/shard_map/all_to_all | solution.py:115

commit v7 on v6

--- a/solution.py
+++ b/solution.py
@@ -2,6 +2,7 @@
 import jax.numpy as jnp
 from jax import lax
 from jax.sharding import PartitionSpec as P
+from jax.experimental import pallas as pl
 
 SH = 64
 NSIG = 16
@@ -36,20 +37,50 @@
     return lax.rsqrt(dist_sq + smear_sq)
 
 
+def batch_kernel(dens_ref, colloc_ref, points_ref, scale_ref, sites_ref, proj_ref, out_ref):
+    rows = dens_ref[0]
+    values = colloc_ref[0]
+    weights = proj_ref[...]
+    field = lax.dot_general(
+        rows, values, (((0,), (0,)), ((), ())), preferred_element_type=jnp.float32
+    ).astype(jnp.bfloat16)
+    projected = jnp.dot(weights, field, preferred_element_type=jnp.float32)
+    points = points_ref[0]
+    sites = sites_ref[...]
+    dist_sq = (points[0:1, :] - sites[:, 0:1]) ** 2
+    dist_sq = dist_sq + (points[1:2, :] - sites[:, 1:2]) ** 2
+    dist_sq = dist_sq + (points[2:3, :] - sites[:, 2:3]) ** 2
+    charges = (projected * lax.rsqrt(dist_sq + smear_sq) * scale_ref[0]).astype(jnp.bfloat16)
+    spread_back = lax.dot_general(
+        weights, charges, (((0,), (0,)), ((), ())), preferred_element_type=jnp.float32
+    ).astype(jnp.bfloat16)
+    term = lax.dot_general(
+        values, spread_back, (((1,), (1,)), ((), ())), preferred_element_type=jnp.float32
+    )
+    out_ref[0] = term.astype(out_ref.dtype)
+
+
 def batch_terms(dens_rows, colloc, grid_points, grid_weights, charge_sites, charge_proj, point_counts):
-    total_points = colloc.shape[2]
-    field = jnp.einsum(
-        "bfs,bfp->bsp", dens_rows, colloc, preferred_element_type=jnp.float32
-    ).astype(jnp.bfloat16)
-    projected = jnp.einsum("ks,bsp->bkp", charge_proj, field, preferred_element_type=jnp.float32)
+    batches, func_rows, total_points = colloc.shape
+    slab_width = charge_proj.shape[1]
+    aux = charge_proj.shape[0]
     live = (jnp.arange(total_points)[None, :] < point_counts[:, None]).astype(jnp.float32)
-    charges = (
-        projected * potential(grid_points, charge_sites) * (grid_weights * live)[:, None, :]
-    ).astype(jnp.bfloat16)
-    spread_back = jnp.einsum(
-        "bkp,ks->bps", charges, charge_proj, preferred_element_type=jnp.float32
-    ).astype(jnp.bfloat16)
-    return jnp.einsum("bfp,bps->bfs", colloc, spread_back, preferred_element_type=jnp.float32)
+    scale = (grid_weights * live).reshape(batches, 1, total_points)
+    sites = jnp.transpose(charge_sites)
+    return pl.pallas_call(
+        batch_kernel,
+        grid=(batches,),
+        in_specs=[
+            pl.BlockSpec((1, func_rows, slab_width), lambda b: (b, 0, 0)),
+            pl.BlockSpec((1, func_rows, total_points), lambda b: (b, 0, 0)),
+            pl.BlockSpec((1, 3, total_points), lambda b: (b, 0, 0)),
+            pl.BlockSpec((1, 1, total_points), lambda b: (b, 0, 0)),
+            pl.BlockSpec((aux, 3), lambda b: (0, 0)),
+            pl.BlockSpec((aux, slab_width), lambda b: (0, 0)),
+        ],
+        out_specs=pl.BlockSpec((1, func_rows, slab_width), lambda b: (b, 0, 0)),
+        out_shape=jax.ShapeDtypeStruct((batches, func_rows, slab_width), jnp.bfloat16),
+    )(dens_rows, colloc, grid_points, scale, sites, charge_proj)
 
 
 def on_device(
@@ -110,7 +141,7 @@
     terms = batch_terms(
         dens_rows, colloc, grid_points, grid_weights, charge_sites, charge_proj, point_counts
     )
-    terms = terms.astype(jnp.bfloat16).reshape(request_count, SH, slab_width)
+    terms = terms.reshape(request_count, SH, slab_width)
     tiles = terms[source_of]
     arrived = lax.all_to_all(
         tiles.reshape(owners, capacity * SH, slab_width),

time: 248 us -> 243 us (0.980)
  matrix products: 32.1 us -> 15.1 us
  Pallas kernels: 0 us -> 13 us
    dot_general x3 -> x0, matrix products: 17.1 us -> none  [the longest x1 7.6 us: batch_terms(): jnp.einsum('bfp,bps->bfs', colloc, spread_back, preferred_element_type=jn...]
    pallas_call x0 -> x1, Pallas kernels: none -> 13 us  [batch_terms(): pl.pallas_call(batch_kernel, grid=(batches,), in_specs=[pl.BlockSpec((1,...]
    convert_element_type x1 -> x0, local copies, waits for them, and re-layouts: 3.03 us -> none  [on_device(): terms = terms.astype(jnp.bfloat16).reshape(request_count, SH, slab_width)]
  transfers between devices with their start and end apart: 8 -> 8, of which waited for: 4 -> 4; matrix products, arithmetic and copies ran while one was open for 7% -> 8% of each run, Pallas kernels for 0% -> 0%
where the time goes in v7:
time: 243 us; the launch traced here: 242 us
  waiting for transfers between devices  146 us (60%)
  starting transfers between devices  42.9 us (18%)
  local copies, waits for them, and re-layouts  21 us (9%)
  matrix products  15.1 us (6%)
  Pallas kernels  13 us (5%)
  other arithmetic  4.23 us (2%)
    all_to_all x1, waiting for transfers between devices, on_device(): lax.all_to_all(tiles.reshape(owners, capacity * SH, slab_width), ('row',...  52.1 us
    all_to_all x1, waiting for transfers between devices, on_device(): lax.all_to_all(found.reshape(owners, capacity * SH, slab_width), ('row',...  49.7 us
    all_to_all x1, waiting for transfers between devices, on_device(): lax.all_to_all(partial.reshape(col_count, own_rows, slab_width), 'col', s...  39 us
    all_to_all x1, starting transfers between devices, on_device(): lax.all_to_all(found.reshape(owners, capacity * SH, slab_width), ('row',...  15.3 us
    pallas_call x1, Pallas kernels, batch_terms(): pl.pallas_call(batch_kernel, grid=(batches,), in_specs=[pl.BlockSpec((1,...  13 us
    all_to_all x1, starting transfers between devices, on_device(): lax.all_to_all(wanted.reshape(owners, capacity), ('row', 'col'), split_ax...  11.4 us
    dot_general x1, matrix products, on_device(): lax.dot_general(occ_coeffs, window, (((1,), (1,)), ((), ())), preferred_e...  10.6 us
    all_to_all x1, starting transfers between devices, on_device(): lax.all_to_all(partial.reshape(col_count, own_rows, slab_width), 'col', s...  7.1 us
  transfers between devices with their start and end apart: 8, of which 4 were waited for; matrix products, arithmetic and copies ran while one was open for 8% of the time, Pallas kernels for 0%

profile of v7, /device:TPU:1, one launch (start us, length us, event | category | flops | bytes accessed | tf_op | source)
XLA Modules:
  0.0 242.5 jit_solution(11447589750993952797)
XLA Ops:
  0.0 1.0 slice.3
  1.0 0.7 collective-permute-start
  1.7 0.7 collective-permute-start.1
  2.4 1.3 collective-permute-start.2
  3.7 0.7 broadcast_remainder_fusion
  4.4 0.7 compare_and_fusion
  5.1 0.1 div.28
  5.2 0.1 rem.34
  5.2 0.1 ne.65
  5.3 0.1 div.27
  5.4 0.1 and.29
  5.5 0.1 fusion.5
  5.6 0.2 reduce_window_sum.11
  5.8 0.0 collective-permute-done
  5.8 0.0 collective-permute-done.1
  5.8 5.4 %collective-permute-done.2 = bf16[128,1280]{1,0:T(8,128)(2,1)S(1)} collective-permute-done((bf16[128,1280]{1,0:T(8,128)(2,1)S(1)}, bf16[128,1280]{1,0:T(8,128)(2,1)S(1)}, u32[]{:S(2)}, u32[]{:S(2)}) %collective-permute-start.2) | collective-permute-done | bytes 327712 | tf_op jit(solution)/shard_map/ppermute | solution.py:25
  11.2 1.0 select_select_fusion
  12.2 1.3 collective-permute-start.3
  13.5 0.2 select_reduce_fusion.1
  13.7 1.0 scatter_custom_fusion
  14.7 0.8 all_to_all.15
  15.5 11.4 %all-to-all-start = ((s32[128,1,2]{2,1,0:T(1,128)}), s32[128,1,2]{2,1,0:T(1,128)S(1)}, u32[]{:S(2)}, u32[]{:S(2)}) async-start(s32[128,1,2]{2,1,0:T(1,128)} %bitcast.2), calls=%async_computation | async-start | bytes 131072 | tf_op jit(solution)/shard_map/all_to_all | solution.py:119
  26.9 10.6 %fusion.2 = f32[128,6144]{1,0:T(8,128)S(1)} fusion(bf16[6144,1280]{1,0:T(8,128)(2,1)} %param.8, bf16[128,1280]{1,0:T(8,128)(2,1)S(1)} %collective-permute-done.3, bf16[128,1280]{1,0:T(8,128)(2,1)S(1)} %select_select_fusion, pred[]{:T(512)S(6)} %or.11), kind=kOutput, calls=%fused_computation.7 | convolution fusion | flops 2013429760 | bytes 19529728 | tf_op jit(solution)/shard_map/dot_general | solution.py:123
  37.5 2.0 copy.43
  39.5 0.0 all-to-all-done
  39.5 7.1 %all-to-all-start.1 = ((f32[16,384,128]{1,2,0:T(8,128)}), f32[16,384,128]{1,2,0:T(8,128)S(1)}, u32[]{:S(2)}, u32[]{:S(2)}) async-start(f32[16,384,128]{1,2,0:T(8,128)} %bitcast.26), calls=%async_computation.1 | async-start | bytes 6291456 | tf_op jit(solution)/shard_map/all_to_all | solution.py:126
  46.6 0.5 broadcast.186
  47.1 1.0 fusion.15
  48.1 0.1 reshape.184
  48.3 39.0 %all-to-all-done.1 = f32[16,384,128]{1,2,0:T(8,128)S(1)} async-done(((f32[16,384,128]{1,2,0:T(8,128)}), f32[16,384,128]{1,2,0:T(8,128)S(1)}, u32[]{:S(2)}, u32[]{:S(2)}) %all-to-all-start.1) | async-done | bytes 3145760 | tf_op jit(solution)/shard_map/all_to_all | solution.py:126
  87.3 0.1 reduce_sum.33
  87.4 0.1 copy.33
  87.5 3.1 %gather_fusion = bf16[256,64,128]{2,1,0:T(8,128)(2,1)} fusion(bf16[6,64,128]{2,1,0:T(8,128)(2,1)S(1)} %bitcast.27, s32[1024]{0:T(1024)S(1)} %pad_clamp_fusion.2), kind=kCustom, calls=%fused_computation | custom fusion | bytes 8389632 | tf_op jit(solution)/shard_map/gather | solution.py:131
  90.6 15.3 %all-to-all-start.2 = ((bf16[128,128,128]{2,1,0:T(8,128)(2,1)}), bf16[128,128,128]{2,1,0:T(8,128)(2,1)}, u32[]{:S(2)}, u32[]{:S(2)}) async-start(bf16[128,128,128]{2,1,0:T(8,128)(2,1)} %bitcast.29), calls=%async_computation.2 | async-start | bytes 8388608 | tf_op jit(solution)/shard_map/all_to_all | solution.py:132
  105.9 0.9 copy.34
  106.8 0.7 copy.35.points_ref
  107.5 0.1 fusion.6
  107.6 0.6 reshape.177.scale_ref
  108.2 0.1 select_reduce_fusion
  108.3 49.7 %all-to-all-done.2 = bf16[128,128,128]{2,1,0:T(8,128)(2,1)} async-done(((bf16[128,128,128]{2,1,0:T(8,128)(2,1)}), bf16[128,128,128]{2,1,0:T(8,128)(2,1)}, u32[]{:S(2)}, u32[]{:S(2)}) %all-to-all-start.2) | async-done | bytes 4194336 | tf_op jit(solution)/shard_map/all_to_all | solution.py:132
  158.0 4.3 %gather_fusion.1 = bf16[128,64,128]{2,1,0:T(8,128)(2,1)} fusion(bf16[256,64,128]{2,1,0:T(8,128)(2,1)} %bitcast.7, s32[1024]{0:T(1024)S(1)} %pad_clamp_fusion.1), kind=kCustom, calls=%fused_computation.1 | custom fusion | bytes 4194816 | tf_op jit(solution)/shard_map/gather | solution.py:139
  162.3 13.0 %shard_map.82 = bf16[8,1024,128]{2,1,0:T(8,128)(2,1)} custom-call(bf16[8,1024,128]{2,1,0:T(8,128)(2,1)} %bitcast.32, bf16[8,1024,512]{2,1,0:T(8,128)(2,1)} %colloc_ref.1, f32[8,3,512]{2,1,0:T(4,128)} %copy.35.points_ref, f32[8,1,512]{2,1,0:T(1,128)} %reshape.177.scale_ref, f32[512,3]{1,0:T(8,128)} %bitcast.33, bf16[512,128]{1,0:T(8,128)(2,1)} %proj_ref.1), custom_call_target="tpu_custom_call" | custom-call | tf_op jit(solution)/shard_map/pallas_call | solution.py:70
  175.3 4.6 %gather_fusion.2 = bf16[256,64,128]{2,1,0:T(8,128)(2,1)} fusion(bf16[128,64,128]{2,1,0:T(8,128)(2,1)} %bitcast.28, s32[1024]{0:T(1024)S(1)} %pad_clamp_fusion), kind=kCustom, calls=%fused_computation.2 | custom fusion | bytes 8389632 | tf_op jit(solution)/shard_map/gather | solution.py:145
  179.9 5.1 %all-to-all-start.3 = ((bf16[128,128,128]{2,1,0:T(8,128)(2,1)}), bf16[128,128,128]{2,1,0:T(8,128)(2,1)}, u32[]{:S(2)}, u32[]{:S(2)}) async-start(bf16[128,128,128]{2,1,0:T(8,128)(2,1)} %bitcast.30), calls=%async_computation.3 | async-start | bytes 8388608 | tf_op jit(solution)/shard_map/all_to_all | solution.py:146
  185.1 0.1 eq.68
  185.2 52.1 %all-to-all-done.3 = bf16[128,128,128]{2,1,0:T(8,128)(2,1)} async-done(((bf16[128,128,128]{2,1,0:T(8,128)(2,1)}), bf16[128,128,128]{2,1,0:T(8,128)(2,1)}, u32[]{:S(2)}, u32[]{:S(2)}) %all-to-all-start.3) | async-done | bytes 4194336 | tf_op jit(solution)/shard_map/all_to_all | solution.py:146
  237.3 4.5 %fusion = f32[6,64,128]{2,0,1:T(8,128)S(1)} fusion(bf16[256,64,128]{2,1,0:T(8,128)(2,1)} %bitcast.14, s32[256]{0:T(256)S(1)} %eq.68), kind=kOutput, calls=%fused_computation.4 | convolution fusion | flops 25167360 | bytes 4391936 | tf_op jit(solution)/shard_map/js,sfc->jfc/dot_general | solution.py:154
  241.8 0.7 copy.37
  (16 shorter events, 0.1 us)
Async XLA Ops:
  1.0 4.8 %collective-permute-start = (bf16[128,1280]{1,0:T(8,128)(2,1)S(1)}, bf16[128,1280]{1,0:T(8,128)(2,1)S(1)}, u32[]{:S(2)}, u32[]{:S(2)}) collective-permute-start(bf16[128,1280]{1,0:T(8,128)(2,1)S(1)} %slice.3), channel_id=1, source_target_pairs={{0,96},{1,97},{2,98},{3,99},{4,100},{5,101},{6,102},{7,103},{8,104... | collective-permute-start | bytes 983048 | tf_op jit(solution)/shard_map/ppermute | solution.py:25
  1.7 4.1 %collective-permute-start.1 = (bf16[128,1280]{1,0:T(8,128)(2,1)S(1)}, bf16[128,1280]{1,0:T(8,128)(2,1)S(1)}, u32[]{:S(2)}, u32[]{:S(2)}) collective-permute-start(bf16[128,1280]{1,0:T(8,128)(2,1)S(1)} %slice.3), channel_id=1, source_target_pairs={{0,32},{1,33},{2,34},{3,35},{4,36},{5,37},{6,38},{7,39},{8,40},{9,... | collective-permute-start | bytes 983048 | tf_op jit(solution)/shard_map/ppermute | solution.py:25
  2.4 8.8 %collective-permute-start.2 = (bf16[128,1280]{1,0:T(8,128)(2,1)S(1)}, bf16[128,1280]{1,0:T(8,128)(2,1)S(1)}, u32[]{:S(2)}, u32[]{:S(2)}) collective-permute-start(bf16[128,1280]{1,0:T(8,128)(2,1)S(1)} %slice.3), channel_id=1, source_target_pairs={{0,16},{1,17},{2,18},{3,19},{4,20},{5,21},{6,22},{7,23},{8,24},{9,... | collective-permute-start | bytes 983048 | tf_op jit(solution)/shard_map/ppermute | solution.py:25
  12.2 14.7 %collective-permute-start.3 = (bf16[128,1280]{1,0:T(8,128)(2,1)S(1)}, bf16[128,1280]{1,0:T(8,128)(2,1)S(1)}, u32[]{:S(2)}, u32[]{:S(2)}) collective-permute-start(bf16[128,1280]{1,0:T(8,128)(2,1)S(1)} %select_select_fusion), channel_id=1, source_target_pairs={{16,48},{32,64},{96,112},{0,80},{17,49},{33,65},{97,113},{1,81},{1... | collective-permute-start | bytes 983048 | tf_op jit(solution)/shard_map/ppermute | solution.py:29
  15.5 24.1 %all-to-all-start = ((s32[128,1,2]{2,1,0:T(1,128)}), s32[128,1,2]{2,1,0:T(1,128)S(1)}, u32[]{:S(2)}, u32[]{:S(2)}) async-start(s32[128,1,2]{2,1,0:T(1,128)} %bitcast.2), calls=%async_computation | async-start | bytes 131072 | tf_op jit(solution)/shard_map/all_to_all | solution.py:119
  39.5 47.7 %all-to-all-start.1 = ((f32[16,384,128]{1,2,0:T(8,128)}), f32[16,384,128]{1,2,0:T(8,128)S(1)}, u32[]{:S(2)}, u32[]{:S(2)}) async-start(f32[16,384,128]{1,2,0:T(8,128)} %bitcast.26), calls=%async_computation.1 | async-start | bytes 6291456 | tf_op jit(solution)/shard_map/all_to_all | solution.py:126
  90.6 15.3 %copy-start.2 = (f32[3,512]{1,0:T(4,128)S(1)}, f32[3,512]{1,0:T(4,128)}, u32[]{:S(2)}) copy-start(f32[3,512]{1,0:T(4,128)} %param.12) | copy-start | bytes 18436
  90.6 16.2 %copy-start = (f32[8,3,512]{2,0,1:T(8,128)S(1)}, f32[8,3,512]{2,0,1:T(8,128)}, u32[]{:S(2)}) copy-start(f32[8,3,512]{2,0,1:T(8,128)} %param.10) | copy-start | bytes 147460
  90.6 16.9 %copy-start.1 = (f32[8,512]{1,0:T(8,128)S(1)}, f32[8,512]{1,0:T(8,128)}, u32[]{:S(2)}) copy-start(f32[8,512]{1,0:T(8,128)} %param.11) | copy-start | bytes 49156
  90.6 16.9 %copy-start.3 = (s32[8]{0:T(128)S(1)}, s32[8]{0:T(128)}, u32[]{:S(2)}) copy-start(s32[8]{0:T(128)} %param.15) | copy-start | bytes 100
  90.6 67.4 %all-to-all-start.2 = ((bf16[128,128,128]{2,1,0:T(8,128)(2,1)}), bf16[128,128,128]{2,1,0:T(8,128)(2,1)}, u32[]{:S(2)}, u32[]{:S(2)}) async-start(bf16[128,128,128]{2,1,0:T(8,128)(2,1)} %bitcast.29), calls=%async_computation.2 | async-start | bytes 8388608 | tf_op jit(solution)/shard_map/all_to_all | solution.py:132
  179.9 57.4 %all-to-all-start.3 = ((bf16[128,128,128]{2,1,0:T(8,128)(2,1)}), bf16[128,128,128]{2,1,0:T(8,128)(2,1)}, u32[]{:S(2)}, u32[]{:S(2)}) async-start(bf16[128,128,128]{2,1,0:T(8,128)(2,1)} %bitcast.30), calls=%async_computation.3 | async-start | bytes 8388608 | tf_op jit(solution)/shard_map/all_to_all | solution.py:146

commit v8 on v7

--- a/solution.py
+++ b/solution.py
@@ -83,6 +83,28 @@
     )(dens_rows, colloc, grid_points, scale, sites, charge_proj)
 
 
+def product_kernel(coeff_ref, window_ref, out_ref):
+    out_ref[...] = lax.dot_general(
+        coeff_ref[...], window_ref[...], (((1,), (1,)), ((), ())), preferred_element_type=jnp.float32
+    )
+
+
+def slab_product(occ_coeffs, window):
+    rows, depth = occ_coeffs.shape
+    width = window.shape[0]
+    block = 768 if rows % 768 == 0 else rows
+    return pl.pallas_call(
+        product_kernel,
+        grid=(rows // block,),
+        in_specs=[
+            pl.BlockSpec((block, depth), lambda i: (i, 0)),
+            pl.BlockSpec((width, depth), lambda i: (0, 0)),
+        ],
+        out_specs=pl.BlockSpec((block, width), lambda i: (i, 0)),
+        out_shape=jax.ShapeDtypeStruct((rows, width), jnp.float32),
+    )(occ_coeffs, window)
+
+
 def on_device(
     occ_coeffs,
     colloc,
@@ -120,9 +142,7 @@
         wanted.reshape(owners, capacity), ("row", "col"), split_axis=0, concat_axis=0, tiled=True
     ).reshape(-1)
 
-    partial = lax.dot_general(
-        occ_coeffs, window, (((1,), (1,)), ((), ())), preferred_element_type=jnp.float32
-    )
+    partial = slab_product(occ_coeffs, window)
     pieces = lax.all_to_all(
         partial.reshape(col_count, own_rows, slab_width), "col", split_axis=0, concat_axis=0, tiled=True
     )

time: 243 us -> 243 us (level)
  Pallas kernels: 13 us -> 24.2 us
  matrix products: 15.1 us -> 4.47 us
    pallas_call x0 -> x1, Pallas kernels: none -> 11.2 us  [slab_product(): pl.pallas_call(product_kernel, grid=(rows // block,), in_specs=[pl.BlockS...]
    dot_general x1 -> x0, matrix products: 10.6 us -> none  [on_device(): lax.dot_general(occ_coeffs, window, (((1,), (1,)), ((), ())), preferred_e...]
  transfers between devices with their start and end apart: 8 -> 8, of which waited for: 4 -> 4; matrix products, arithmetic and copies ran while one was open for 8% -> 3% of each run, Pallas kernels for 0% -> 5%
where the time goes in v8:
time: 243 us; the launch traced here: 242 us
  waiting for transfers between devices  146 us (60%)
  starting transfers between devices  42.9 us (18%)
  Pallas kernels  24.2 us (10%)
  local copies, waits for them, and re-layouts  18.8 us (8%)
  other arithmetic  4.99 us (2%)
  matrix products  4.47 us (2%)
    all_to_all x1, waiting for transfers between devices, on_device(): lax.all_to_all(tiles.reshape(owners, capacity * SH, slab_width), ('row',...  52.1 us
    all_to_all x1, waiting for transfers between devices, on_device(): lax.all_to_all(found.reshape(owners, capacity * SH, slab_width), ('row',...  49.7 us
    all_to_all x1, waiting for transfers between devices, on_device(): lax.all_to_all(partial.reshape(col_count, own_rows, slab_width), 'col', s...  39 us
    all_to_all x1, starting transfers between devices, on_device(): lax.all_to_all(found.reshape(owners, capacity * SH, slab_width), ('row',...  15.3 us
    pallas_call x1, Pallas kernels, batch_terms(): pl.pallas_call(batch_kernel, grid=(batches,), in_specs=[pl.BlockSpec((1,...  13 us
    all_to_all x1, starting transfers between devices, on_device(): lax.all_to_all(wanted.reshape(owners, capacity), ('row', 'col'), split_ax...  11.4 us
    pallas_call x1, Pallas kernels, slab_product(): pl.pallas_call(product_kernel, grid=(rows // block,), in_specs=[pl.BlockS...  11.2 us
    all_to_all x1, starting transfers between devices, on_device(): lax.all_to_all(partial.reshape(col_count, own_rows, slab_width), 'col', s...  7.1 us
  transfers between devices with their start and end apart: 8, of which 4 were waited for; matrix products, arithmetic and copies ran while one was open for 3% of the time, Pallas kernels for 5%

profile of v8, /device:TPU:1, one launch (start us, length us, event | category | flops | bytes accessed | tf_op | source)
XLA Modules:
  0.0 241.8 jit_solution(2175716316136795680)
XLA Ops:
  0.0 1.0 slice.3
  1.0 0.7 collective-permute-start
  1.7 0.7 collective-permute-start.1
  2.4 1.3 collective-permute-start.2
  3.7 0.7 broadcast_remainder_fusion
  4.4 0.7 compare_and_fusion
  5.1 0.1 div.28
  5.2 0.1 rem.34
  5.2 0.1 ne.65
  5.3 0.1 div.27
  5.4 0.1 and.29
  5.5 0.1 fusion.2
  5.6 0.2 reduce_window_sum.11
  5.8 0.0 collective-permute-done
  5.8 0.0 collective-permute-done.1
  5.8 5.4 %collective-permute-done.2 = bf16[128,1280]{1,0:T(8,128)(2,1)S(1)} collective-permute-done((bf16[128,1280]{1,0:T(8,128)(2,1)S(1)}, bf16[128,1280]{1,0:T(8,128)(2,1)S(1)}, u32[]{:S(2)}, u32[]{:S(2)}) %collective-permute-start.2) | collective-permute-done | bytes 327712 | tf_op jit(solution)/shard_map/ppermute | solution.py:25
  11.2 1.0 select_select_fusion
  12.2 1.3 collective-permute-start.3
  13.5 0.2 select_reduce_fusion.1
  13.7 1.0 scatter_custom_fusion
  14.7 0.8 all_to_all.15
  15.5 11.4 %all-to-all-start = ((s32[128,1,2]{2,1,0:T(1,128)}), s32[128,1,2]{2,1,0:T(1,128)S(1)}, u32[]{:S(2)}, u32[]{:S(2)}) async-start(s32[128,1,2]{2,1,0:T(1,128)} %bitcast.2), calls=%async_computation | async-start | bytes 131072 | tf_op jit(solution)/shard_map/all_to_all | solution.py:141
  26.9 0.0 collective-permute-done.3
  26.9 0.8 broadcast_select_fusion.window_ref
  27.7 11.2 %shard_map.82 = f32[6144,128]{1,0:T(8,128)} custom-call(bf16[6144,1280]{1,0:T(8,128)(2,1)} %coeff_ref.1, bf16[128,1280]{1,0:T(8,128)(2,1)} %broadcast_select_fusion.window_ref), custom_call_target="tpu_custom_call" | custom-call | tf_op jit(solution)/shard_map/pallas_call | solution.py:96
  38.9 0.0 all-to-all-done
  38.9 7.1 %all-to-all-start.1 = ((f32[16,384,128]{2,1,0:T(8,128)}), f32[16,384,128]{2,1,0:T(8,128)S(1)}, u32[]{:S(2)}, u32[]{:S(2)}) async-start(f32[16,384,128]{2,1,0:T(8,128)} %bitcast.26), calls=%async_computation.1 | async-start | bytes 6291456 | tf_op jit(solution)/shard_map/all_to_all | solution.py:146
  46.0 0.5 broadcast.186
  46.6 1.0 fusion.12
  47.6 0.1 reshape.184
  47.7 39.0 %all-to-all-done.1 = f32[16,384,128]{2,1,0:T(8,128)S(1)} async-done(((f32[16,384,128]{2,1,0:T(8,128)}), f32[16,384,128]{2,1,0:T(8,128)S(1)}, u32[]{:S(2)}, u32[]{:S(2)}) %all-to-all-start.1) | async-done | bytes 3145760 | tf_op jit(solution)/shard_map/all_to_all | solution.py:146
  86.7 0.1 reduce_sum.33
  86.8 3.1 %gather_fusion = bf16[256,64,128]{2,1,0:T(8,128)(2,1)} fusion(bf16[6,64,128]{2,1,0:T(8,128)(2,1)S(1)} %bitcast.22, s32[1024]{0:T(1024)S(1)} %pad_clamp_fusion.2), kind=kCustom, calls=%fused_computation | custom fusion | bytes 8389632 | tf_op jit(solution)/shard_map/gather | solution.py:151
  89.9 15.3 %all-to-all-start.2 = ((bf16[128,128,128]{2,1,0:T(8,128)(2,1)}), bf16[128,128,128]{2,1,0:T(8,128)(2,1)}, u32[]{:S(2)}, u32[]{:S(2)}) async-start(bf16[128,128,128]{2,1,0:T(8,128)(2,1)} %bitcast.24), calls=%async_computation.2 | async-start | bytes 8388608 | tf_op jit(solution)/shard_map/all_to_all | solution.py:152
  105.2 0.9 copy.21
  106.1 0.7 copy.22.points_ref
  106.8 0.1 fusion.3
  106.8 0.6 reshape.177.scale_ref
  107.5 0.1 select_reduce_fusion
  107.6 49.7 %all-to-all-done.2 = bf16[128,128,128]{2,1,0:T(8,128)(2,1)} async-done(((bf16[128,128,128]{2,1,0:T(8,128)(2,1)}), bf16[128,128,128]{2,1,0:T(8,128)(2,1)}, u32[]{:S(2)}, u32[]{:S(2)}) %all-to-all-start.2) | async-done | bytes 4194336 | tf_op jit(solution)/shard_map/all_to_all | solution.py:152
  157.3 4.3 %gather_fusion.1 = bf16[128,64,128]{2,1,0:T(8,128)(2,1)} fusion(bf16[256,64,128]{2,1,0:T(8,128)(2,1)} %bitcast.7, s32[1024]{0:T(1024)S(1)} %pad_clamp_fusion.1), kind=kCustom, calls=%fused_computation.1 | custom fusion | bytes 4194816 | tf_op jit(solution)/shard_map/gather | solution.py:159
  161.6 13.0 %shard_map.83 = bf16[8,1024,128]{2,1,0:T(8,128)(2,1)} custom-call(bf16[8,1024,128]{2,1,0:T(8,128)(2,1)} %bitcast.27, bf16[8,1024,512]{2,1,0:T(8,128)(2,1)} %colloc_ref.1, f32[8,3,512]{2,1,0:T(4,128)} %copy.22.points_ref, f32[8,1,512]{2,1,0:T(1,128)} %reshape.177.scale_ref, f32[512,3]{1,0:T(8,128)} %bitcast.28, bf16[512,128]{1,0:T(8,128)(2,1)} %proj_ref.1), custom_call_target="tpu_custom_call" | custom-call | tf_op jit(solution)/shard_map/pallas_call | solution.py:70
  174.6 4.6 %gather_fusion.2 = bf16[256,64,128]{2,1,0:T(8,128)(2,1)} fusion(bf16[128,64,128]{2,1,0:T(8,128)(2,1)} %bitcast.23, s32[1024]{0:T(1024)S(1)} %pad_clamp_fusion), kind=kCustom, calls=%fused_computation.2 | custom fusion | bytes 8389632 | tf_op jit(solution)/shard_map/gather | solution.py:165
  179.2 5.1 %all-to-all-start.3 = ((bf16[128,128,128]{2,1,0:T(8,128)(2,1)}), bf16[128,128,128]{2,1,0:T(8,128)(2,1)}, u32[]{:S(2)}, u32[]{:S(2)}) async-start(bf16[128,128,128]{2,1,0:T(8,128)(2,1)} %bitcast.25), calls=%async_computation.3 | async-start | bytes 8388608 | tf_op jit(solution)/shard_map/all_to_all | solution.py:166
  184.3 0.1 eq.68
  184.5 52.1 %all-to-all-done.3 = bf16[128,128,128]{2,1,0:T(8,128)(2,1)} async-done(((bf16[128,128,128]{2,1,0:T(8,128)(2,1)}), bf16[128,128,128]{2,1,0:T(8,128)(2,1)}, u32[]{:S(2)}, u32[]{:S(2)}) %all-to-all-start.3) | async-done | bytes 4194336 | tf_op jit(solution)/shard_map/all_to_all | solution.py:166
  236.6 4.5 %fusion = f32[6,64,128]{2,0,1:T(8,128)S(1)} fusion(bf16[256,64,128]{2,1,0:T(8,128)(2,1)} %bitcast.14, s32[256]{0:T(256)S(1)} %eq.68), kind=kOutput, calls=%fused_computation.4 | convolution fusion | flops 25167360 | bytes 4391936 | tf_op jit(solution)/shard_map/js,sfc->jfc/dot_general | solution.py:174
  241.1 0.7 copy.24
  (15 shorter events, 0.1 us)
Async XLA Ops:
  1.0 4.8 %collective-permute-start = (bf16[128,1280]{1,0:T(8,128)(2,1)S(1)}, bf16[128,1280]{1,0:T(8,128)(2,1)S(1)}, u32[]{:S(2)}, u32[]{:S(2)}) collective-permute-start(bf16[128,1280]{1,0:T(8,128)(2,1)S(1)} %slice.3), channel_id=1, source_target_pairs={{0,96},{1,97},{2,98},{3,99},{4,100},{5,101},{6,102},{7,103},{8,104... | collective-permute-start | bytes 983048 | tf_op jit(solution)/shard_map/ppermute | solution.py:25
  1.7 4.1 %collective-permute-start.1 = (bf16[128,1280]{1,0:T(8,128)(2,1)S(1)}, bf16[128,1280]{1,0:T(8,128)(2,1)S(1)}, u32[]{:S(2)}, u32[]{:S(2)}) collective-permute-start(bf16[128,1280]{1,0:T(8,128)(2,1)S(1)} %slice.3), channel_id=1, source_target_pairs={{0,32},{1,33},{2,34},{3,35},{4,36},{5,37},{6,38},{7,39},{8,40},{9,... | collective-permute-start | bytes 983048 | tf_op jit(solution)/shard_map/ppermute | solution.py:25
  2.4 8.8 %collective-permute-start.2 = (bf16[128,1280]{1,0:T(8,128)(2,1)S(1)}, bf16[128,1280]{1,0:T(8,128)(2,1)S(1)}, u32[]{:S(2)}, u32[]{:S(2)}) collective-permute-start(bf16[128,1280]{1,0:T(8,128)(2,1)S(1)} %slice.3), channel_id=1, source_target_pairs={{0,16},{1,17},{2,18},{3,19},{4,20},{5,21},{6,22},{7,23},{8,24},{9,... | collective-permute-start | bytes 983048 | tf_op jit(solution)/shard_map/ppermute | solution.py:25
  12.2 14.7 %collective-permute-start.3 = (bf16[128,1280]{1,0:T(8,128)(2,1)S(1)}, bf16[128,1280]{1,0:T(8,128)(2,1)S(1)}, u32[]{:S(2)}, u32[]{:S(2)}) collective-permute-start(bf16[128,1280]{1,0:T(8,128)(2,1)S(1)} %select_select_fusion), channel_id=1, source_target_pairs={{16,48},{32,64},{96,112},{0,80},{17,49},{33,65},{97,113},{1,81},{1... | collective-permute-start | bytes 983048 | tf_op jit(solution)/shard_map/ppermute | solution.py:29
  15.5 23.5 %all-to-all-start = ((s32[128,1,2]{2,1,0:T(1,128)}), s32[128,1,2]{2,1,0:T(1,128)S(1)}, u32[]{:S(2)}, u32[]{:S(2)}) async-start(s32[128,1,2]{2,1,0:T(1,128)} %bitcast.2), calls=%async_computation | async-start | bytes 131072 | tf_op jit(solution)/shard_map/all_to_all | solution.py:141
  38.9 47.7 %all-to-all-start.1 = ((f32[16,384,128]{2,1,0:T(8,128)}), f32[16,384,128]{2,1,0:T(8,128)S(1)}, u32[]{:S(2)}, u32[]{:S(2)}) async-start(f32[16,384,128]{2,1,0:T(8,128)} %bitcast.26), calls=%async_computation.1 | async-start | bytes 6291456 | tf_op jit(solution)/shard_map/all_to_all | solution.py:146
  89.9 15.3 %copy-start.2 = (f32[3,512]{1,0:T(4,128)S(1)}, f32[3,512]{1,0:T(4,128)}, u32[]{:S(2)}) copy-start(f32[3,512]{1,0:T(4,128)} %param.12) | copy-start | bytes 18436
  89.9 16.2 %copy-start = (f32[8,3,512]{2,0,1:T(8,128)S(1)}, f32[8,3,512]{2,0,1:T(8,128)}, u32[]{:S(2)}) copy-start(f32[8,3,512]{2,0,1:T(8,128)} %param.10) | copy-start | bytes 147460
  89.9 16.9 %copy-start.1 = (f32[8,512]{1,0:T(8,128)S(1)}, f32[8,512]{1,0:T(8,128)}, u32[]{:S(2)}) copy-start(f32[8,512]{1,0:T(8,128)} %param.11) | copy-start | bytes 49156
  89.9 16.9 %copy-start.3 = (s32[8]{0:T(128)S(1)}, s32[8]{0:T(128)}, u32[]{:S(2)}) copy-start(s32[8]{0:T(128)} %param.15) | copy-start | bytes 100
  89.9 67.4 %all-to-all-start.2 = ((bf16[128,128,128]{2,1,0:T(8,128)(2,1)}), bf16[128,128,128]{2,1,0:T(8,128)(2,1)}, u32[]{:S(2)}, u32[]{:S(2)}) async-start(bf16[128,128,128]{2,1,0:T(8,128)(2,1)} %bitcast.24), calls=%async_computation.2 | async-start | bytes 8388608 | tf_op jit(solution)/shard_map/all_to_all | solution.py:152
  179.2 57.4 %all-to-all-start.3 = ((bf16[128,128,128]{2,1,0:T(8,128)(2,1)}), bf16[128,128,128]{2,1,0:T(8,128)(2,1)}, u32[]{:S(2)}, u32[]{:S(2)}) async-start(bf16[128,128,128]{2,1,0:T(8,128)(2,1)} %bitcast.25), calls=%async_computation.3 | async-start | bytes 8388608 | tf_op jit(solution)/shard_map/all_to_all | solution.py:166

commit v9 on v8

--- a/solution.py
+++ b/solution.py
@@ -84,25 +84,23 @@
 
 
 def product_kernel(coeff_ref, window_ref, out_ref):
-    out_ref[...] = lax.dot_general(
-        coeff_ref[...], window_ref[...], (((1,), (1,)), ((), ())), preferred_element_type=jnp.float32
-    )
+    out_ref[...] = jnp.dot(coeff_ref[...], window_ref[...], preferred_element_type=jnp.float32)
 
 
 def slab_product(occ_coeffs, window):
     rows, depth = occ_coeffs.shape
     width = window.shape[0]
-    block = 768 if rows % 768 == 0 else rows
+    block = 1536 if rows % 1536 == 0 else rows
     return pl.pallas_call(
         product_kernel,
         grid=(rows // block,),
         in_specs=[
             pl.BlockSpec((block, depth), lambda i: (i, 0)),
-            pl.BlockSpec((width, depth), lambda i: (0, 0)),
+            pl.BlockSpec((depth, width), lambda i: (0, 0)),
         ],
         out_specs=pl.BlockSpec((block, width), lambda i: (i, 0)),
         out_shape=jax.ShapeDtypeStruct((rows, width), jnp.float32),
-    )(occ_coeffs, window)
+    )(occ_coeffs, jnp.transpose(window))
 
 
 def on_device(

time: 243 us -> 240 us (0.988)
  transfers between devices with their start and end apart: 8 -> 8, of which waited for: 4 -> 4; matrix products, arithmetic and copies ran while one was open for 3% -> 3% of each run, Pallas kernels for 5% -> 4%
where the time goes in v9:
time: 240 us; the launch traced here: 239 us
  waiting for transfers between devices  146 us (61%)
  starting transfers between devices  42.9 us (18%)
  Pallas kernels  22.4 us (9%)
  local copies, waits for them, and re-layouts  19 us (8%)
  matrix products  4.47 us (2%)
  other arithmetic  4.01 us (2%)
    all_to_all x1, waiting for transfers between devices, on_device(): lax.all_to_all(tiles.reshape(owners, capacity * SH, slab_width), ('row',...  52.1 us
    all_to_all x1, waiting for transfers between devices, on_device(): lax.all_to_all(found.reshape(owners, capacity * SH, slab_width), ('row',...  49.7 us
    all_to_all x1, waiting for transfers between devices, on_device(): lax.all_to_all(partial.reshape(col_count, own_rows, slab_width), 'col', s...  39 us
    all_to_all x1, starting transfers between devices, on_device(): lax.all_to_all(found.reshape(owners, capacity * SH, slab_width), ('row',...  15.3 us
    pallas_call x1, Pallas kernels, batch_terms(): pl.pallas_call(batch_kernel, grid=(batches,), in_specs=[pl.BlockSpec((1,...  13 us
    all_to_all x1, starting transfers between devices, on_device(): lax.all_to_all(wanted.reshape(owners, capacity), ('row', 'col'), split_ax...  11.4 us
    pallas_call x1, Pallas kernels, slab_product(): pl.pallas_call(product_kernel, grid=(rows // block,), in_specs=[pl.BlockS...  9.39 us
    all_to_all x1, starting transfers between devices, on_device(): lax.all_to_all(partial.reshape(col_count, own_rows, slab_width), 'col', s...  7.1 us
  transfers between devices with their start and end apart: 8, of which 4 were waited for; matrix products, arithmetic and copies ran while one was open for 3% of the time, Pallas kernels for 4%

profile of v9, /device:TPU:1, one launch (start us, length us, event | category | flops | bytes accessed | tf_op | source)
XLA Modules:
  0.0 239.2 jit_solution(11366610684091816055)
XLA Ops:
  0.0 1.0 slice.3
  1.0 0.2 copy.29
  1.2 0.7 collective-permute-start
  1.9 0.7 collective-permute-start.1
  2.6 1.3 collective-permute-start.2
  3.9 0.7 broadcast_remainder_fusion
  4.6 0.7 compare_and_fusion
  5.3 0.1 div.28
  5.4 0.1 rem.34
  5.4 0.1 ne.65
  5.5 0.1 div.27
  5.6 0.1 and.29
  5.7 0.1 fusion.2
  5.8 0.2 reduce_window_sum.11
  6.0 0.0 collective-permute-done
  6.0 0.0 collective-permute-done.1
  6.0 5.4 %collective-permute-done.2 = bf16[128,1280]{0,1:T(8,128)(2,1)S(1)} collective-permute-done((bf16[128,1280]{0,1:T(8,128)(2,1)S(1)}, bf16[128,1280]{0,1:T(8,128)(2,1)S(1)}, u32[]{:S(2)}, u32[]{:S(2)}) %collective-permute-start.2) | collective-permute-done | bytes 327712 | tf_op jit(solution)/shard_map/ppermute | solution.py:25
  11.4 0.1 select_select_fusion
  11.4 1.3 collective-permute-start.3
  12.8 0.2 select_reduce_fusion.1
  12.9 1.0 scatter_custom_fusion
  13.9 0.8 all_to_all.15
  14.7 11.4 %all-to-all-start = ((s32[128,1,2]{2,1,0:T(1,128)}), s32[128,1,2]{2,1,0:T(1,128)S(1)}, u32[]{:S(2)}, u32[]{:S(2)}) async-start(s32[128,1,2]{2,1,0:T(1,128)} %bitcast.2), calls=%async_computation | async-start | bytes 131072 | tf_op jit(solution)/shard_map/all_to_all | solution.py:139
  26.2 0.0 collective-permute-done.3
  26.2 0.8 select_bitcast_fusion.window_ref
  26.9 9.4 %shard_map.82 = f32[6144,128]{1,0:T(8,128)} custom-call(bf16[6144,1280]{1,0:T(8,128)(2,1)} %coeff_ref.1, bf16[1280,128]{1,0:T(8,128)(2,1)} %select_bitcast_fusion.window_ref), custom_call_target="tpu_custom_call" | custom-call | tf_op jit(solution)/shard_map/pallas_call | solution.py:94
  36.3 7.1 %all-to-all-start.1 = ((f32[16,384,128]{2,1,0:T(8,128)}), f32[16,384,128]{2,1,0:T(8,128)S(1)}, u32[]{:S(2)}, u32[]{:S(2)}) async-start(f32[16,384,128]{2,1,0:T(8,128)} %bitcast.28), calls=%async_computation.1 | async-start | bytes 6291456 | tf_op jit(solution)/shard_map/all_to_all | solution.py:144
  43.4 0.5 broadcast.186
  44.0 1.0 fusion.12
  44.9 0.1 reshape.184
  45.1 39.0 %all-to-all-done.1 = f32[16,384,128]{2,1,0:T(8,128)S(1)} async-done(((f32[16,384,128]{2,1,0:T(8,128)}), f32[16,384,128]{2,1,0:T(8,128)S(1)}, u32[]{:S(2)}, u32[]{:S(2)}) %all-to-all-start.1) | async-done | bytes 3145760 | tf_op jit(solution)/shard_map/all_to_all | solution.py:144
  84.1 0.1 reduce_sum.33
  84.2 3.1 %gather_fusion = bf16[256,64,128]{2,1,0:T(8,128)(2,1)} fusion(bf16[6,64,128]{2,1,0:T(8,128)(2,1)S(1)} %bitcast.24, s32[1024]{0:T(1024)S(1)} %pad_clamp_fusion.2), kind=kCustom, calls=%fused_computation | custom fusion | bytes 8389632 | tf_op jit(solution)/shard_map/gather | solution.py:149
  87.3 15.3 %all-to-all-start.2 = ((bf16[128,128,128]{2,1,0:T(8,128)(2,1)}), bf16[128,128,128]{2,1,0:T(8,128)(2,1)}, u32[]{:S(2)}, u32[]{:S(2)}) async-start(bf16[128,128,128]{2,1,0:T(8,128)(2,1)} %bitcast.26), calls=%async_computation.2 | async-start | bytes 8388608 | tf_op jit(solution)/shard_map/all_to_all | solution.py:150
  102.6 0.9 copy.25
  103.5 0.7 copy.26.points_ref
  104.2 0.1 fusion.3
  104.2 0.6 reshape.177.scale_ref
  104.9 0.1 select_reduce_fusion
  105.0 49.7 %all-to-all-done.2 = bf16[128,128,128]{2,1,0:T(8,128)(2,1)} async-done(((bf16[128,128,128]{2,1,0:T(8,128)(2,1)}), bf16[128,128,128]{2,1,0:T(8,128)(2,1)}, u32[]{:S(2)}, u32[]{:S(2)}) %all-to-all-start.2) | async-done | bytes 4194336 | tf_op jit(solution)/shard_map/all_to_all | solution.py:150
  154.7 4.3 %gather_fusion.1 = bf16[128,64,128]{2,1,0:T(8,128)(2,1)} fusion(bf16[256,64,128]{2,1,0:T(8,128)(2,1)} %bitcast.8, s32[1024]{0:T(1024)S(1)} %pad_clamp_fusion.1), kind=kCustom, calls=%fused_computation.1 | custom fusion | bytes 4194816 | tf_op jit(solution)/shard_map/gather | solution.py:157
  159.0 13.0 %shard_map.83 = bf16[8,1024,128]{2,1,0:T(8,128)(2,1)} custom-call(bf16[8,1024,128]{2,1,0:T(8,128)(2,1)} %bitcast.29, bf16[8,1024,512]{2,1,0:T(8,128)(2,1)} %colloc_ref.1, f32[8,3,512]{2,1,0:T(4,128)} %copy.26.points_ref, f32[8,1,512]{2,1,0:T(1,128)} %reshape.177.scale_ref, f32[512,3]{1,0:T(8,128)} %bitcast.30, bf16[512,128]{1,0:T(8,128)(2,1)} %proj_ref.1), custom_call_target="tpu_custom_call" | custom-call | tf_op jit(solution)/shard_map/pallas_call | solution.py:70
  172.0 4.6 %gather_fusion.2 = bf16[256,64,128]{2,1,0:T(8,128)(2,1)} fusion(bf16[128,64,128]{2,1,0:T(8,128)(2,1)} %bitcast.25, s32[1024]{0:T(1024)S(1)} %pad_clamp_fusion), kind=kCustom, calls=%fused_computation.2 | custom fusion | bytes 8389632 | tf_op jit(solution)/shard_map/gather | solution.py:163
  176.6 5.1 %all-to-all-start.3 = ((bf16[128,128,128]{2,1,0:T(8,128)(2,1)}), bf16[128,128,128]{2,1,0:T(8,128)(2,1)}, u32[]{:S(2)}, u32[]{:S(2)}) async-start(bf16[128,128,128]{2,1,0:T(8,128)(2,1)} %bitcast.27), calls=%async_computation.3 | async-start | bytes 8388608 | tf_op jit(solution)/shard_map/all_to_all | solution.py:164
  181.7 0.1 eq.68
  181.9 52.1 %all-to-all-done.3 = bf16[128,128,128]{2,1,0:T(8,128)(2,1)} async-done(((bf16[128,128,128]{2,1,0:T(8,128)(2,1)}), bf16[128,128,128]{2,1,0:T(8,128)(2,1)}, u32[]{:S(2)}, u32[]{:S(2)}) %all-to-all-start.3) | async-done | bytes 4194336 | tf_op jit(solution)/shard_map/all_to_all | solution.py:164
  234.0 4.5 %fusion = f32[6,64,128]{2,0,1:T(8,128)S(1)} fusion(bf16[256,64,128]{2,1,0:T(8,128)(2,1)} %bitcast.15, s32[256]{0:T(256)S(1)} %eq.68), kind=kOutput, calls=%fused_computation.4 | convolution fusion | flops 25167360 | bytes 4391936 | tf_op jit(solution)/shard_map/js,sfc->jfc/dot_general | solution.py:172
  238.4 0.7 copy.28
  (16 shorter events, 0.1 us)
Async XLA Ops:
  1.2 4.8 %collective-permute-start = (bf16[128,1280]{0,1:T(8,128)(2,1)S(1)}, bf16[128,1280]{0,1:T(8,128)(2,1)S(1)}, u32[]{:S(2)}, u32[]{:S(2)}) collective-permute-start(bf16[128,1280]{0,1:T(8,128)(2,1)S(1)} %copy.29), channel_id=1, source_target_pairs={{0,96},{1,97},{2,98},{3,99},{4,100},{5,101},{6,102},{7,103},{8,104... | collective-permute-start | bytes 983048 | tf_op jit(solution)/shard_map/ppermute | solution.py:25
  1.9 4.1 %collective-permute-start.1 = (bf16[128,1280]{0,1:T(8,128)(2,1)S(1)}, bf16[128,1280]{0,1:T(8,128)(2,1)S(1)}, u32[]{:S(2)}, u32[]{:S(2)}) collective-permute-start(bf16[128,1280]{0,1:T(8,128)(2,1)S(1)} %copy.29), channel_id=1, source_target_pairs={{0,32},{1,33},{2,34},{3,35},{4,36},{5,37},{6,38},{7,39},{8,40},{9,... | collective-permute-start | bytes 983048 | tf_op jit(solution)/shard_map/ppermute | solution.py:25
  2.6 8.8 %collective-permute-start.2 = (bf16[128,1280]{0,1:T(8,128)(2,1)S(1)}, bf16[128,1280]{0,1:T(8,128)(2,1)S(1)}, u32[]{:S(2)}, u32[]{:S(2)}) collective-permute-start(bf16[128,1280]{0,1:T(8,128)(2,1)S(1)} %copy.29), channel_id=1, source_target_pairs={{0,16},{1,17},{2,18},{3,19},{4,20},{5,21},{6,22},{7,23},{8,24},{9,... | collective-permute-start | bytes 983048 | tf_op jit(solution)/shard_map/ppermute | solution.py:25
  11.4 14.7 %collective-permute-start.3 = (bf16[128,1280]{0,1:T(8,128)(2,1)S(1)}, bf16[128,1280]{0,1:T(8,128)(2,1)S(1)}, u32[]{:S(2)}, u32[]{:S(2)}) collective-permute-start(bf16[128,1280]{0,1:T(8,128)(2,1)S(1)} %select_select_fusion), channel_id=1, source_target_pairs={{16,48},{32,64},{96,112},{0,80},{17,49},{33,65},{97,113},{1,81},{1... | collective-permute-start | bytes 983048 | tf_op jit(solution)/shard_map/ppermute | solution.py:29
  14.7 21.6 %all-to-all-start = ((s32[128,1,2]{2,1,0:T(1,128)}), s32[128,1,2]{2,1,0:T(1,128)S(1)}, u32[]{:S(2)}, u32[]{:S(2)}) async-start(s32[128,1,2]{2,1,0:T(1,128)} %bitcast.2), calls=%async_computation | async-start | bytes 131072 | tf_op jit(solution)/shard_map/all_to_all | solution.py:139
  36.3 47.7 %all-to-all-start.1 = ((f32[16,384,128]{2,1,0:T(8,128)}), f32[16,384,128]{2,1,0:T(8,128)S(1)}, u32[]{:S(2)}, u32[]{:S(2)}) async-start(f32[16,384,128]{2,1,0:T(8,128)} %bitcast.28), calls=%async_computation.1 | async-start | bytes 6291456 | tf_op jit(solution)/shard_map/all_to_all | solution.py:144
  87.3 15.3 %copy-start.2 = (f32[3,512]{1,0:T(4,128)S(1)}, f32[3,512]{1,0:T(4,128)}, u32[]{:S(2)}) copy-start(f32[3,512]{1,0:T(4,128)} %param.12) | copy-start | bytes 18436
  87.3 16.2 %copy-start = (f32[8,3,512]{2,0,1:T(8,128)S(1)}, f32[8,3,512]{2,0,1:T(8,128)}, u32[]{:S(2)}) copy-start(f32[8,3,512]{2,0,1:T(8,128)} %param.10) | copy-start | bytes 147460
  87.3 16.9 %copy-start.1 = (f32[8,512]{1,0:T(8,128)S(1)}, f32[8,512]{1,0:T(8,128)}, u32[]{:S(2)}) copy-start(f32[8,512]{1,0:T(8,128)} %param.11) | copy-start | bytes 49156
  87.3 16.9 %copy-start.3 = (s32[8]{0:T(128)S(1)}, s32[8]{0:T(128)}, u32[]{:S(2)}) copy-start(s32[8]{0:T(128)} %param.15) | copy-start | bytes 100
  87.3 67.4 %all-to-all-start.2 = ((bf16[128,128,128]{2,1,0:T(8,128)(2,1)}), bf16[128,128,128]{2,1,0:T(8,128)(2,1)}, u32[]{:S(2)}, u32[]{:S(2)}) async-start(bf16[128,128,128]{2,1,0:T(8,128)(2,1)} %bitcast.26), calls=%async_computation.2 | async-start | bytes 8388608 | tf_op jit(solution)/shard_map/all_to_all | solution.py:150
  176.6 57.4 %all-to-all-start.3 = ((bf16[128,128,128]{2,1,0:T(8,128)(2,1)}), bf16[128,128,128]{2,1,0:T(8,128)(2,1)}, u32[]{:S(2)}, u32[]{:S(2)}) async-start(bf16[128,128,128]{2,1,0:T(8,128)(2,1)} %bitcast.27), calls=%async_computation.3 | async-start | bytes 8388608 | tf_op jit(solution)/shard_map/all_to_all | solution.py:164

commit v10 on v9

--- a/solution.py
+++ b/solution.py
@@ -3,6 +3,7 @@
 from jax import lax
 from jax.sharding import PartitionSpec as P
 from jax.experimental import pallas as pl
+from jax.experimental.pallas import tpu as pltpu
 
 SH = 64
 NSIG = 16
@@ -37,12 +38,16 @@
     return lax.rsqrt(dist_sq + smear_sq)
 
 
-def batch_kernel(dens_ref, colloc_ref, points_ref, scale_ref, sites_ref, proj_ref, out_ref):
-    rows = dens_ref[0]
+def batch_kernel(slot_ref, *refs):
+    blocks = refs[:NSIG]
+    colloc_ref, points_ref, scale_ref, sites_ref, proj_ref, _, out_ref, rows_ref, term_ref, sems = refs[NSIG:]
+    b = pl.program_id(0)
+    for k in range(NSIG):
+        rows_ref[k * SH:(k + 1) * SH, :] = blocks[k][0]
     values = colloc_ref[0]
     weights = proj_ref[...]
     field = lax.dot_general(
-        rows, values, (((0,), (0,)), ((), ())), preferred_element_type=jnp.float32
+        rows_ref[...], values, (((0,), (0,)), ((), ())), preferred_element_type=jnp.float32
     ).astype(jnp.bfloat16)
     projected = jnp.dot(weights, field, preferred_element_type=jnp.float32)
     points = points_ref[0]
@@ -57,30 +62,56 @@
     term = lax.dot_general(
         values, spread_back, (((1,), (1,)), ((), ())), preferred_element_type=jnp.float32
     )
-    out_ref[0] = term.astype(out_ref.dtype)
-
-
-def batch_terms(dens_rows, colloc, grid_points, grid_weights, charge_sites, charge_proj, point_counts):
+    term_ref[...] = term.astype(term_ref.dtype)
+    copies = []
+    for k in range(NSIG):
+        copy = pltpu.make_async_copy(
+            term_ref.at[pl.ds(k * SH, SH)], out_ref.at[slot_ref[b * NSIG + k]], sems.at[k]
+        )
+        copy.start()
+        copies.append(copy)
+    for copy in copies:
+        copy.wait()
+
+
+def batch_terms(replies, slot, colloc, grid_points, grid_weights, charge_sites, charge_proj, point_counts):
     batches, func_rows, total_points = colloc.shape
+    slots = replies.shape[0]
     slab_width = charge_proj.shape[1]
     aux = charge_proj.shape[0]
     live = (jnp.arange(total_points)[None, :] < point_counts[:, None]).astype(jnp.float32)
     scale = (grid_weights * live).reshape(batches, 1, total_points)
     sites = jnp.transpose(charge_sites)
+
+    def block_spec(k):
+        return pl.BlockSpec((1, SH, slab_width), lambda b, slot_ref: (slot_ref[b * NSIG + k], 0, 0))
+
+    grid_spec = pltpu.PrefetchScalarGridSpec(
+        num_scalar_prefetch=1,
+        grid=(batches,),
+        in_specs=[block_spec(k) for k in range(NSIG)]
+        + [
+            pl.BlockSpec((1, func_rows, total_points), lambda b, slot_ref: (b, 0, 0)),
+            pl.BlockSpec((1, 3, total_points), lambda b, slot_ref: (b, 0, 0)),
+            pl.BlockSpec((1, 1, total_points), lambda b, slot_ref: (b, 0, 0)),
+            pl.BlockSpec((aux, 3), lambda b, slot_ref: (0, 0)),
+            pl.BlockSpec((aux, slab_width), lambda b, slot_ref: (0, 0)),
+            pl.BlockSpec(memory_space=pl.ANY),
+        ],
+        out_specs=pl.BlockSpec(memory_space=pl.ANY),
+        scratch_shapes=[
+            pltpu.VMEM((func_rows, slab_width), jnp.bfloat16),
+            pltpu.VMEM((func_rows, slab_width), jnp.bfloat16),
+            pltpu.SemaphoreType.DMA((NSIG,)),
+        ],
+    )
+    empty = jnp.zeros((slots, SH, slab_width), jnp.bfloat16)
     return pl.pallas_call(
         batch_kernel,
-        grid=(batches,),
-        in_specs=[
-            pl.BlockSpec((1, func_rows, slab_width), lambda b: (b, 0, 0)),
-            pl.BlockSpec((1, func_rows, total_points), lambda b: (b, 0, 0)),
-            pl.BlockSpec((1, 3, total_points), lambda b: (b, 0, 0)),
-            pl.BlockSpec((1, 1, total_points), lambda b: (b, 0, 0)),
-            pl.BlockSpec((aux, 3), lambda b: (0, 0)),
-            pl.BlockSpec((aux, slab_width), lambda b: (0, 0)),
-        ],
-        out_specs=pl.BlockSpec((1, func_rows, slab_width), lambda b: (b, 0, 0)),
-        out_shape=jax.ShapeDtypeStruct((batches, func_rows, slab_width), jnp.bfloat16),
-    )(dens_rows, colloc, grid_points, scale, sites, charge_proj)
+        grid_spec=grid_spec,
+        out_shape=jax.ShapeDtypeStruct((slots, SH, slab_width), jnp.bfloat16),
+        input_output_aliases={1 + NSIG + 5: 0},
+    )(slot, *([replies] * NSIG), colloc, grid_points, scale, sites, charge_proj, empty)
 
 
 def product_kernel(coeff_ref, window_ref, out_ref):
@@ -154,13 +185,16 @@
         concat_axis=0,
         tiled=True,
     )
-    fetched = replies.reshape(slots, SH, slab_width)[slot]
-    dens_rows = fetched.reshape(shell_lists.shape[0], NSIG * SH, slab_width)
-    terms = batch_terms(
-        dens_rows, colloc, grid_points, grid_weights, charge_sites, charge_proj, point_counts
-    )
-    terms = terms.reshape(request_count, SH, slab_width)
-    tiles = terms[source_of]
+    tiles = batch_terms(
+        replies.reshape(slots, SH, slab_width),
+        jnp.clip(slot, 0, slots - 1),
+        colloc,
+        grid_points,
+        grid_weights,
+        charge_sites,
+        charge_proj,
+        point_counts,
+    )
     arrived = lax.all_to_all(
         tiles.reshape(owners, capacity * SH, slab_width),
         ("row", "col"),

time: 240 us -> 243 us (1.012)
  Pallas kernels: 22.4 us -> 29.8 us
  starting transfers between devices: 42.9 us -> 49.5 us
  waiting for transfers between devices: 146 us -> 140 us
  local copies, waits for them, and re-layouts: 19 us -> 13.1 us
    gather x2 -> x0, local copies, waits for them, and re-layouts: 8.95 us -> none  [the longest x1 4.62 us: on_device(): tiles = terms[source_of]]
    pallas_call x1, Pallas kernels: 13 us -> 20.4 us  [batch_terms(): pl.pallas_call(batch_kernel, grid_spec=grid_spec, out_shape=jax.ShapeDtyp...]
    ppermute x3, waiting for transfers between devices: 5.39 us -> 0.01 us  [broadcast_from_first(): first = [lax.ppermute(value, axis, [(0, dst)]) for dst in (1, 2, 6)]]
    all_to_all x1, starting transfers between devices: 11.4 us -> 15.9 us  [on_device(): lax.all_to_all(wanted.reshape(owners, capacity), ('row', 'col'), split_ax...]
    broadcast_in_dim x0 -> x1, local copies, waits for them, and re-layouts: none -> 3.03 us  [batch_terms(): empty = jnp.zeros((slots, SH, slab_width), jnp.bfloat16)]
  transfers between devices with their start and end apart: 8 -> 8, of which waited for: 4 -> 3; matrix products, arithmetic and copies ran while one was open for 3% -> 4% of each run, Pallas kernels for 4% -> 4%
where the time goes in v10:
time: 243 us; the launch traced here: 242 us
  waiting for transfers between devices  140 us (58%)
  starting transfers between devices  49.5 us (20%)
  Pallas kernels  29.8 us (12%)
  local copies, waits for them, and re-layouts  13.1 us (5%)
  other arithmetic  4.47 us (2%)
  matrix products  4.47 us (2%)
    all_to_all x1, waiting for transfers between devices, on_device(): lax.all_to_all(tiles.reshape(owners, capacity * SH, slab_width), ('row',...  52.1 us
    all_to_all x1, waiting for transfers between devices, on_device(): lax.all_to_all(found.reshape(owners, capacity * SH, slab_width), ('row',...  49.3 us
    all_to_all x1, waiting for transfers between devices, on_device(): lax.all_to_all(partial.reshape(col_count, own_rows, slab_width), 'col', s...  39 us
    pallas_call x1, Pallas kernels, batch_terms(): pl.pallas_call(batch_kernel, grid_spec=grid_spec, out_shape=jax.ShapeDtyp...  20.4 us
    all_to_all x1, starting transfers between devices, on_device(): lax.all_to_all(wanted.reshape(owners, capacity), ('row', 'col'), split_ax...  15.9 us
    all_to_all x1, starting transfers between devices, on_device(): lax.all_to_all(found.reshape(owners, capacity * SH, slab_width), ('row',...  15.3 us
    pallas_call x1, Pallas kernels, slab_product(): pl.pallas_call(product_kernel, grid=(rows // block,), in_specs=[pl.BlockS...  9.39 us
    all_to_all x1, starting transfers between devices, on_device(): lax.all_to_all(partial.reshape(col_count, own_rows, slab_width), 'col', s...  7.1 us
  transfers between devices with their start and end apart: 8, of which 3 were waited for; matrix products, arithmetic and copies ran while one was open for 4% of the time, Pallas kernels for 4%

profile of v10, /device:TPU:1, one launch (start us, length us, event | category | flops | bytes accessed | tf_op | source)
XLA Modules:
  0.0 242.0 jit_solution(433763000647191796)
XLA Ops:
  0.0 1.0 slice.3
  1.0 0.2 copy.24
  1.2 1.3 collective-permute-start.2
  2.5 0.7 collective-permute-start.1
  3.2 0.7 collective-permute-start
  3.9 0.7 compare_and_fusion
  4.6 0.7 broadcast_remainder_fusion
  5.3 0.1 ne.57
  5.4 0.1 rem.30
  5.5 0.1 div.24
  5.6 0.1 div.23
  5.6 0.1 and.25
  5.7 0.1 fusion.2
  5.8 0.2 reduce_window_sum.11
  6.0 0.0 collective-permute-done.2
  6.0 0.0 collective-permute-done.1
  6.0 0.0 collective-permute-done
  6.0 0.1 select_select_fusion
  6.1 3.4 %collective-permute-start.3 = (bf16[128,1280]{0,1:T(8,128)(2,1)S(1)}, bf16[128,1280]{0,1:T(8,128)(2,1)S(1)}, u32[]{:S(2)}, u32[]{:S(2)}) collective-permute-start(bf16[128,1280]{0,1:T(8,128)(2,1)S(1)} %select_select_fusion), channel_id=1, source_target_pairs={{16,48},{32,64},{96,112},{0,80},{17,49},{33,65},{97,113},{1,81},{1... | collective-permute-start | bytes 983048 | tf_op jit(solution)/shard_map/ppermute | solution.py:30
  9.5 0.2 select_reduce_fusion
  9.7 1.0 scatter_custom_fusion
  10.7 0.8 all_to_all.15
  11.5 15.9 %all-to-all-start = ((s32[128,1,2]{2,1,0:T(1,128)}), s32[128,1,2]{2,1,0:T(1,128)S(1)}, u32[]{:S(2)}, u32[]{:S(2)}) async-start(s32[128,1,2]{2,1,0:T(1,128)} %bitcast.2), calls=%async_computation | async-start | bytes 131072 | tf_op jit(solution)/shard_map/all_to_all | solution.py:170
  27.4 0.0 collective-permute-done.3
  27.4 0.8 select_bitcast_fusion.window_ref
  28.2 9.4 %shard_map.82 = f32[6144,128]{1,0:T(8,128)} custom-call(bf16[6144,1280]{1,0:T(8,128)(2,1)} %coeff_ref.1, bf16[1280,128]{1,0:T(8,128)(2,1)} %select_bitcast_fusion.window_ref), custom_call_target="tpu_custom_call" | custom-call | tf_op jit(solution)/shard_map/pallas_call | solution.py:125
  37.6 0.0 all-to-all-done
  37.6 7.1 %all-to-all-start.1 = ((f32[16,384,128]{2,1,0:T(8,128)}), f32[16,384,128]{2,1,0:T(8,128)S(1)}, u32[]{:S(2)}, u32[]{:S(2)}) async-start(f32[16,384,128]{2,1,0:T(8,128)} %bitcast.24), calls=%async_computation.1 | async-start | bytes 6291456 | tf_op jit(solution)/shard_map/all_to_all | solution.py:175
  44.7 0.5 broadcast.130
  45.2 1.0 fusion.12
  46.2 0.1 reshape.141
  46.4 39.0 %all-to-all-done.1 = f32[16,384,128]{2,1,0:T(8,128)S(1)} async-done(((f32[16,384,128]{2,1,0:T(8,128)}), f32[16,384,128]{2,1,0:T(8,128)S(1)}, u32[]{:S(2)}, u32[]{:S(2)}) %all-to-all-start.1) | async-done | bytes 3145760 | tf_op jit(solution)/shard_map/all_to_all | solution.py:175
  85.3 0.1 reduce_sum.22
  85.5 3.1 %gather_fusion = bf16[256,64,128]{2,1,0:T(8,128)(2,1)} fusion(bf16[6,64,128]{2,1,0:T(8,128)(2,1)S(1)} %bitcast.21, s32[1024]{0:T(1024)S(1)} %pad_clamp_fusion), kind=kCustom, calls=%fused_computation | custom fusion | bytes 8389632 | tf_op jit(solution)/shard_map/gather | solution.py:180
  88.5 15.3 %all-to-all-start.2 = ((bf16[128,128,128]{2,1,0:T(8,128)(2,1)}), bf16[128,128,128]{2,1,0:T(8,128)(2,1)}, u32[]{:S(2)}, u32[]{:S(2)}) async-start(bf16[128,128,128]{2,1,0:T(8,128)(2,1)} %bitcast.23), calls=%async_computation.2 | async-start | bytes 8388608 | tf_op jit(solution)/shard_map/all_to_all | solution.py:181
  103.9 0.1 fusion.3
  103.9 0.6 reshape.135.refs_18_
  104.6 0.7 copy.21.refs_17_
  105.2 0.9 copy.20
  106.1 0.6 add_clamp_fusion.slot_ref
  106.7 49.3 %all-to-all-done.2 = bf16[128,128,128]{2,1,0:T(8,128)(2,1)} async-done(((bf16[128,128,128]{2,1,0:T(8,128)(2,1)}), bf16[128,128,128]{2,1,0:T(8,128)(2,1)}, u32[]{:S(2)}, u32[]{:S(2)}) %all-to-all-start.2) | async-done | bytes 4194336 | tf_op jit(solution)/shard_map/all_to_all | solution.py:181
  156.0 3.0 %broadcast_in_dim.5.refs_21_ = bf16[256,64,128]{2,1,0:T(8,128)(2,1)} broadcast(bf16[]{:T(256)} %constant.56.clone.1), dimensions={} | broadcast | bytes 4194306 | tf_op jit(solution)/shard_map/broadcast_in_dim | solution.py:108
  159.0 20.4 %shard_map.83 = bf16[256,64,128]{2,1,0:T(8,128)(2,1)} custom-call(s32[128]{0:T(128)} %add_clamp_fusion.slot_ref, bf16[256,64,128]{2,1,0:T(8,128)(2,1)} %bitcast.8.refs_0_.refs_1_.refs_2_.refs_3_.refs_4_.refs_5_.refs_6_.refs_7_.refs_8_.refs_9_.refs_10_.refs_11_.refs_12_.refs_13_.refs_14_.refs_15_, ...), custom_call_target="tpu_custom_call", output_to_operand_aliasing={{}: (22, {})} | custom-call | tf_op jit(solution)/shard_map/pallas_call | solution.py:109
  179.4 5.1 %all-to-all-start.3 = ((bf16[128,128,128]{2,1,0:T(8,128)(2,1)}), bf16[128,128,128]{2,1,0:T(8,128)(2,1)}, u32[]{:S(2)}, u32[]{:S(2)}) async-start(bf16[128,128,128]{2,1,0:T(8,128)(2,1)} %bitcast.22), calls=%async_computation.3 | async-start | bytes 8388608 | tf_op jit(solution)/shard_map/all_to_all | solution.py:198
  184.5 0.1 eq.55
  184.7 52.1 %all-to-all-done.3 = bf16[128,128,128]{2,1,0:T(8,128)(2,1)} async-done(((bf16[128,128,128]{2,1,0:T(8,128)(2,1)}), bf16[128,128,128]{2,1,0:T(8,128)(2,1)}, u32[]{:S(2)}, u32[]{:S(2)}) %all-to-all-start.3) | async-done | bytes 4194336 | tf_op jit(solution)/shard_map/all_to_all | solution.py:198
  236.8 4.5 %fusion = f32[6,64,128]{2,0,1:T(8,128)S(1)} fusion(bf16[256,64,128]{2,1,0:T(8,128)(2,1)} %bitcast.11, s32[256]{0:T(256)S(1)} %eq.55), kind=kOutput, calls=%fused_computation.2 | convolution fusion | flops 25167360 | bytes 4391936 | tf_op jit(solution)/shard_map/js,sfc->jfc/dot_general | solution.py:206
  241.2 0.7 copy.23
  (11 shorter events, 0.0 us)
Async XLA Ops:
  1.2 4.8 %collective-permute-start.2 = (bf16[128,1280]{0,1:T(8,128)(2,1)S(1)}, bf16[128,1280]{0,1:T(8,128)(2,1)S(1)}, u32[]{:S(2)}, u32[]{:S(2)}) collective-permute-start(bf16[128,1280]{0,1:T(8,128)(2,1)S(1)} %copy.24), channel_id=1, source_target_pairs={{0,16},{1,17},{2,18},{3,19},{4,20},{5,21},{6,22},{7,23},{8,24},{9,... | collective-permute-start | bytes 983048 | tf_op jit(solution)/shard_map/ppermute | solution.py:26
  2.5 3.5 %collective-permute-start.1 = (bf16[128,1280]{0,1:T(8,128)(2,1)S(1)}, bf16[128,1280]{0,1:T(8,128)(2,1)S(1)}, u32[]{:S(2)}, u32[]{:S(2)}) collective-permute-start(bf16[128,1280]{0,1:T(8,128)(2,1)S(1)} %copy.24), channel_id=1, source_target_pairs={{0,32},{1,33},{2,34},{3,35},{4,36},{5,37},{6,38},{7,39},{8,40},{9,... | collective-permute-start | bytes 983048 | tf_op jit(solution)/shard_map/ppermute | solution.py:26
  3.2 2.8 %collective-permute-start = (bf16[128,1280]{0,1:T(8,128)(2,1)S(1)}, bf16[128,1280]{0,1:T(8,128)(2,1)S(1)}, u32[]{:S(2)}, u32[]{:S(2)}) collective-permute-start(bf16[128,1280]{0,1:T(8,128)(2,1)S(1)} %copy.24), channel_id=1, source_target_pairs={{0,96},{1,97},{2,98},{3,99},{4,100},{5,101},{6,102},{7,103},{8,104... | collective-permute-start | bytes 983048 | tf_op jit(solution)/shard_map/ppermute | solution.py:26
  6.1 21.4 %collective-permute-start.3 = (bf16[128,1280]{0,1:T(8,128)(2,1)S(1)}, bf16[128,1280]{0,1:T(8,128)(2,1)S(1)}, u32[]{:S(2)}, u32[]{:S(2)}) collective-permute-start(bf16[128,1280]{0,1:T(8,128)(2,1)S(1)} %select_select_fusion), channel_id=1, source_target_pairs={{16,48},{32,64},{96,112},{0,80},{17,49},{33,65},{97,113},{1,81},{1... | collective-permute-start | bytes 983048 | tf_op jit(solution)/shard_map/ppermute | solution.py:30
  11.5 26.1 %all-to-all-start = ((s32[128,1,2]{2,1,0:T(1,128)}), s32[128,1,2]{2,1,0:T(1,128)S(1)}, u32[]{:S(2)}, u32[]{:S(2)}) async-start(s32[128,1,2]{2,1,0:T(1,128)} %bitcast.2), calls=%async_computation | async-start | bytes 131072 | tf_op jit(solution)/shard_map/all_to_all | solution.py:170
  37.6 47.7 %all-to-all-start.1 = ((f32[16,384,128]{2,1,0:T(8,128)}), f32[16,384,128]{2,1,0:T(8,128)S(1)}, u32[]{:S(2)}, u32[]{:S(2)}) async-start(f32[16,384,128]{2,1,0:T(8,128)} %bitcast.24), calls=%async_computation.1 | async-start | bytes 6291456 | tf_op jit(solution)/shard_map/all_to_all | solution.py:175
  88.5 15.3 %copy-start.1 = (f32[8,512]{1,0:T(8,128)S(1)}, f32[8,512]{1,0:T(8,128)}, u32[]{:S(2)}) copy-start(f32[8,512]{1,0:T(8,128)} %param.11) | copy-start | bytes 49156
  88.5 15.3 %copy-start.3 = (s32[8]{0:T(128)S(1)}, s32[8]{0:T(128)}, u32[]{:S(2)}) copy-start(s32[8]{0:T(128)} %param.15) | copy-start | bytes 100
  88.5 16.0 %copy-start = (f32[8,3,512]{2,0,1:T(8,128)S(1)}, f32[8,3,512]{2,0,1:T(8,128)}, u32[]{:S(2)}) copy-start(f32[8,3,512]{2,0,1:T(8,128)} %param.10) | copy-start | bytes 147460
  88.5 16.7 %copy-start.2 = (f32[3,512]{1,0:T(4,128)S(1)}, f32[3,512]{1,0:T(4,128)}, u32[]{:S(2)}) copy-start(f32[3,512]{1,0:T(4,128)} %param.12) | copy-start | bytes 18436
  88.5 67.4 %all-to-all-start.2 = ((bf16[128,128,128]{2,1,0:T(8,128)(2,1)}), bf16[128,128,128]{2,1,0:T(8,128)(2,1)}, u32[]{:S(2)}, u32[]{:S(2)}) async-start(bf16[128,128,128]{2,1,0:T(8,128)(2,1)} %bitcast.23), calls=%async_computation.2 | async-start | bytes 8388608 | tf_op jit(solution)/shard_map/all_to_all | solution.py:181
  179.4 57.3 %all-to-all-start.3 = ((bf16[128,128,128]{2,1,0:T(8,128)(2,1)}), bf16[128,128,128]{2,1,0:T(8,128)(2,1)}, u32[]{:S(2)}, u32[]{:S(2)}) async-start(bf16[128,128,128]{2,1,0:T(8,128)(2,1)} %bitcast.22), calls=%async_computation.3 | async-start | bytes 8388608 | tf_op jit(solution)/shard_map/all_to_all | solution.py:198

commit v11 on v10

--- a/solution.py
+++ b/solution.py
@@ -40,8 +40,7 @@
 
 def batch_kernel(slot_ref, *refs):
     blocks = refs[:NSIG]
-    colloc_ref, points_ref, scale_ref, sites_ref, proj_ref, _, out_ref, rows_ref, term_ref, sems = refs[NSIG:]
-    b = pl.program_id(0)
+    colloc_ref, points_ref, scale_ref, sites_ref, proj_ref, out_ref, rows_ref = refs[NSIG:]
     for k in range(NSIG):
         rows_ref[k * SH:(k + 1) * SH, :] = blocks[k][0]
     values = colloc_ref[0]
@@ -62,21 +61,11 @@
     term = lax.dot_general(
         values, spread_back, (((1,), (1,)), ((), ())), preferred_element_type=jnp.float32
     )
-    term_ref[...] = term.astype(term_ref.dtype)
-    copies = []
-    for k in range(NSIG):
-        copy = pltpu.make_async_copy(
-            term_ref.at[pl.ds(k * SH, SH)], out_ref.at[slot_ref[b * NSIG + k]], sems.at[k]
-        )
-        copy.start()
-        copies.append(copy)
-    for copy in copies:
-        copy.wait()
+    out_ref[0] = term.astype(out_ref.dtype)
 
 
 def batch_terms(replies, slot, colloc, grid_points, grid_weights, charge_sites, charge_proj, point_counts):
     batches, func_rows, total_points = colloc.shape
-    slots = replies.shape[0]
     slab_width = charge_proj.shape[1]
     aux = charge_proj.shape[0]
     live = (jnp.arange(total_points)[None, :] < point_counts[:, None]).astype(jnp.float32)
@@ -96,22 +85,15 @@
             pl.BlockSpec((1, 1, total_points), lambda b, slot_ref: (b, 0, 0)),
             pl.BlockSpec((aux, 3), lambda b, slot_ref: (0, 0)),
             pl.BlockSpec((aux, slab_width), lambda b, slot_ref: (0, 0)),
-            pl.BlockSpec(memory_space=pl.ANY),
         ],
-        out_specs=pl.BlockSpec(memory_space=pl.ANY),
-        scratch_shapes=[
-            pltpu.VMEM((func_rows, slab_width), jnp.bfloat16),
-            pltpu.VMEM((func_rows, slab_width), jnp.bfloat16),
-            pltpu.SemaphoreType.DMA((NSIG,)),
-        ],
-    )
-    empty = jnp.zeros((slots, SH, slab_width), jnp.bfloat16)
+        out_specs=pl.BlockSpec((1, func_rows, slab_width), lambda b, slot_ref: (b, 0, 0)),
+        scratch_shapes=[pltpu.VMEM((func_rows, slab_width), jnp.bfloat16)],
+    )
     return pl.pallas_call(
         batch_kernel,
         grid_spec=grid_spec,
-        out_shape=jax.ShapeDtypeStruct((slots, SH, slab_width), jnp.bfloat16),
-        input_output_aliases={1 + NSIG + 5: 0},
-    )(slot, *([replies] * NSIG), colloc, grid_points, scale, sites, charge_proj, empty)
+        out_shape=jax.ShapeDtypeStruct((batches, func_rows, slab_width), jnp.bfloat16),
+    )(slot, *([replies] * NSIG), colloc, grid_points, scale, sites, charge_proj)
 
 
 def product_kernel(coeff_ref, window_ref, out_ref):
@@ -185,7 +167,7 @@
         concat_axis=0,
         tiled=True,
     )
-    tiles = batch_terms(
+    terms = batch_terms(
         replies.reshape(slots, SH, slab_width),
         jnp.clip(slot, 0, slots - 1),
         colloc,
@@ -195,6 +177,7 @@
         charge_proj,
         point_counts,
     )
+    tiles = terms.reshape(request_count, SH, slab_width)[source_of]
     arrived = lax.all_to_all(
         tiles.reshape(owners, capacity * SH, slab_width),
         ("row", "col"),

time: 243 us -> 238 us (0.979)
  starting transfers between devices: 49.5 us -> 42.9 us
  waiting for transfers between devices: 140 us -> 146 us
  Pallas kernels: 29.8 us -> 25 us
    ppermute x3, waiting for transfers between devices: 0.01 us -> 5.39 us  [broadcast_from_first(): first = [lax.ppermute(value, axis, [(0, dst)]) for dst in (1, 2, 6)]]
    pallas_call x1, Pallas kernels: 20.4 us -> 15.7 us  [batch_terms(): pl.pallas_call(batch_kernel, grid_spec=grid_spec, out_shape=jax.ShapeDtyp...]
    gather x0 -> x1, local copies, waits for them, and re-layouts: none -> 4.62 us  [on_device(): tiles = terms.reshape(request_count, SH, slab_width)[source_of]]
    all_to_all x1, starting transfers between devices: 15.9 us -> 11.4 us  [on_device(): lax.all_to_all(wanted.reshape(owners, capacity), ('row', 'col'), split_ax...]
    broadcast_in_dim x1 -> x0, local copies, waits for them, and re-layouts: 3.03 us -> none  [batch_terms(): empty = jnp.zeros((slots, SH, slab_width), jnp.bfloat16)]
  transfers between devices with their start and end apart: 8 -> 8, of which waited for: 3 -> 4; matrix products, arithmetic and copies ran while one was open for 4% -> 4% of each run, Pallas kernels for 4% -> 4%
where the time goes in v11:
time: 238 us
  waiting for transfers between devices  146 us (61%)
  starting transfers between devices  42.9 us (18%)
  Pallas kernels  25 us (11%)
  local copies, waits for them, and re-layouts  14.7 us (6%)
  other arithmetic  4.51 us (2%)
  matrix products  4.47 us (2%)
    all_to_all x1, waiting for transfers between devices, on_device(): lax.all_to_all(tiles.reshape(owners, capacity * SH, slab_width), ('row',...  52.1 us
    all_to_all x1, waiting for transfers between devices, on_device(): lax.all_to_all(found.reshape(owners, capacity * SH, slab_width), ('row',...  49.2 us
    all_to_all x1, waiting for transfers between devices, on_device(): lax.all_to_all(partial.reshape(col_count, own_rows, slab_width), 'col', s...  39 us
    pallas_call x1, Pallas kernels, batch_terms(): pl.pallas_call(batch_kernel, grid_spec=grid_spec, out_shape=jax.ShapeDtyp...  15.7 us
    all_to_all x1, starting transfers between devices, on_device(): lax.all_to_all(found.reshape(owners, capacity * SH, slab_width), ('row',...  15.3 us
    all_to_all x1, starting transfers between devices, on_device(): lax.all_to_all(wanted.reshape(owners, capacity), ('row', 'col'), split_ax...  11.4 us
    pallas_call x1, Pallas kernels, slab_product(): pl.pallas_call(product_kernel, grid=(rows // block,), in_specs=[pl.BlockS...  9.38 us
    all_to_all x1, starting transfers between devices, on_device(): lax.all_to_all(partial.reshape(col_count, own_rows, slab_width), 'col', s...  7.1 us
  transfers between devices with their start and end apart: 8, of which 4 were waited for; matrix products, arithmetic and copies ran while one was open for 4% of the time, Pallas kernels for 4%

profile of v11, /device:TPU:1, one launch (start us, length us, event | category | flops | bytes accessed | tf_op | source)
XLA Modules:
  0.0 237.5 jit_solution(3850758607387005630)
XLA Ops:
  0.0 1.0 slice.3
  1.0 0.2 copy.29
  1.2 0.7 collective-permute-start
  1.9 0.7 collective-permute-start.1
  2.6 1.3 collective-permute-start.2
  3.9 0.7 broadcast_remainder_fusion
  4.6 0.7 compare_and_fusion
  5.3 0.1 div.28
  5.4 0.1 rem.34
  5.4 0.1 ne.65
  5.5 0.1 div.27
  5.6 0.1 and.29
  5.7 0.1 fusion.2
  5.8 0.2 reduce_window_sum.11
  6.0 0.0 collective-permute-done
  6.0 0.0 collective-permute-done.1
  6.0 5.4 %collective-permute-done.2 = bf16[128,1280]{0,1:T(8,128)(2,1)S(1)} collective-permute-done((bf16[128,1280]{0,1:T(8,128)(2,1)S(1)}, bf16[128,1280]{0,1:T(8,128)(2,1)S(1)}, u32[]{:S(2)}, u32[]{:S(2)}) %collective-permute-start.2) | collective-permute-done | bytes 327712 | tf_op jit(solution)/shard_map/ppermute | solution.py:26
  11.4 0.1 select_select_fusion
  11.4 1.3 collective-permute-start.3
  12.8 0.2 select_reduce_fusion.1
  12.9 1.0 scatter_custom_fusion
  13.9 0.8 all_to_all.15
  14.7 11.4 %all-to-all-start = ((s32[128,1,2]{2,1,0:T(1,128)}), s32[128,1,2]{2,1,0:T(1,128)S(1)}, u32[]{:S(2)}, u32[]{:S(2)}) async-start(s32[128,1,2]{2,1,0:T(1,128)} %bitcast.2), calls=%async_computation | async-start | bytes 131072 | tf_op jit(solution)/shard_map/all_to_all | solution.py:152
  26.2 0.0 collective-permute-done.3
  26.2 0.8 select_bitcast_fusion.window_ref
  26.9 9.4 %shard_map.82 = f32[6144,128]{1,0:T(8,128)} custom-call(bf16[6144,1280]{1,0:T(8,128)(2,1)} %coeff_ref.1, bf16[1280,128]{1,0:T(8,128)(2,1)} %select_bitcast_fusion.window_ref), custom_call_target="tpu_custom_call" | custom-call | tf_op jit(solution)/shard_map/pallas_call | solution.py:107
  36.3 7.1 %all-to-all-start.1 = ((f32[16,384,128]{2,1,0:T(8,128)}), f32[16,384,128]{2,1,0:T(8,128)S(1)}, u32[]{:S(2)}, u32[]{:S(2)}) async-start(f32[16,384,128]{2,1,0:T(8,128)} %bitcast.27), calls=%async_computation.1 | async-start | bytes 6291456 | tf_op jit(solution)/shard_map/all_to_all | solution.py:157
  43.4 0.5 broadcast.176
  44.0 1.0 fusion.12
  45.0 0.1 reshape.180
  45.1 39.0 %all-to-all-done.1 = f32[16,384,128]{2,1,0:T(8,128)S(1)} async-done(((f32[16,384,128]{2,1,0:T(8,128)}), f32[16,384,128]{2,1,0:T(8,128)S(1)}, u32[]{:S(2)}, u32[]{:S(2)}) %all-to-all-start.1) | async-done | bytes 3145760 | tf_op jit(solution)/shard_map/all_to_all | solution.py:157
  84.1 0.1 reduce_sum.33
  84.2 3.1 %gather_fusion = bf16[256,64,128]{2,1,0:T(8,128)(2,1)} fusion(bf16[6,64,128]{2,1,0:T(8,128)(2,1)S(1)} %bitcast.23, s32[1024]{0:T(1024)S(1)} %pad_clamp_fusion.1), kind=kCustom, calls=%fused_computation | custom fusion | bytes 8389632 | tf_op jit(solution)/shard_map/gather | solution.py:162
  87.3 15.3 %all-to-all-start.2 = ((bf16[128,128,128]{2,1,0:T(8,128)(2,1)}), bf16[128,128,128]{2,1,0:T(8,128)(2,1)}, u32[]{:S(2)}, u32[]{:S(2)}) async-start(bf16[128,128,128]{2,1,0:T(8,128)(2,1)} %bitcast.25), calls=%async_computation.2 | async-start | bytes 8388608 | tf_op jit(solution)/shard_map/all_to_all | solution.py:163
  102.6 0.9 copy.25
  103.5 0.7 copy.26.refs_17_
  104.2 0.1 fusion.3
  104.2 0.6 reshape.173.refs_18_
  104.9 0.5 broadcast_clamp_fusion
  105.3 0.1 select_reduce_fusion
  105.5 49.2 %all-to-all-done.2 = bf16[128,128,128]{2,1,0:T(8,128)(2,1)} async-done(((bf16[128,128,128]{2,1,0:T(8,128)(2,1)}), bf16[128,128,128]{2,1,0:T(8,128)(2,1)}, u32[]{:S(2)}, u32[]{:S(2)}) %all-to-all-start.2) | async-done | bytes 4194336 | tf_op jit(solution)/shard_map/all_to_all | solution.py:163
  154.7 15.7 %shard_map.83 = bf16[8,1024,128]{2,1,0:T(8,128)(2,1)} custom-call(s32[128]{0:T(128)} %get-tuple-element.9.slot_ref, bf16[256,64,128]{2,1,0:T(8,128)(2,1)} %bitcast.8.refs_0_.refs_1_.refs_2_.refs_3_.refs_4_.refs_5_.refs_6_.refs_7_.refs_8_.refs_9_.refs_10_.refs_11_.refs_12_.refs_13_.refs_14_.refs_15_, ...), custom_call_target="tpu_custom_call" | custom-call | tf_op jit(solution)/shard_map/pallas_call | solution.py:92
  170.4 4.6 %gather_fusion.1 = bf16[256,64,128]{2,1,0:T(8,128)(2,1)} fusion(bf16[128,64,128]{2,1,0:T(8,128)(2,1)} %bitcast.24, s32[1024]{0:T(1024)S(1)} %pad_clamp_fusion), kind=kCustom, calls=%fused_computation.1 | custom fusion | bytes 8389632 | tf_op jit(solution)/shard_map/gather | solution.py:180
  175.0 5.1 %all-to-all-start.3 = ((bf16[128,128,128]{2,1,0:T(8,128)(2,1)}), bf16[128,128,128]{2,1,0:T(8,128)(2,1)}, u32[]{:S(2)}, u32[]{:S(2)}) async-start(bf16[128,128,128]{2,1,0:T(8,128)(2,1)} %bitcast.26), calls=%async_computation.3 | async-start | bytes 8388608 | tf_op jit(solution)/shard_map/all_to_all | solution.py:181
  180.1 0.1 eq.68
  180.2 52.1 %all-to-all-done.3 = bf16[128,128,128]{2,1,0:T(8,128)(2,1)} async-done(((bf16[128,128,128]{2,1,0:T(8,128)(2,1)}), bf16[128,128,128]{2,1,0:T(8,128)(2,1)}, u32[]{:S(2)}, u32[]{:S(2)}) %all-to-all-start.3) | async-done | bytes 4194336 | tf_op jit(solution)/shard_map/all_to_all | solution.py:181
  232.3 4.5 %fusion = f32[6,64,128]{2,0,1:T(8,128)S(1)} fusion(bf16[256,64,128]{2,1,0:T(8,128)(2,1)} %bitcast.14, s32[256]{0:T(256)S(1)} %eq.68), kind=kOutput, calls=%fused_computation.3 | convolution fusion | flops 25167360 | bytes 4391936 | tf_op jit(solution)/shard_map/js,sfc->jfc/dot_general | solution.py:189
  236.8 0.7 copy.28
  (14 shorter events, 0.1 us)
Async XLA Ops:
  1.2 4.8 %collective-permute-start = (bf16[128,1280]{0,1:T(8,128)(2,1)S(1)}, bf16[128,1280]{0,1:T(8,128)(2,1)S(1)}, u32[]{:S(2)}, u32[]{:S(2)}) collective-permute-start(bf16[128,1280]{0,1:T(8,128)(2,1)S(1)} %copy.29), channel_id=1, source_target_pairs={{0,96},{1,97},{2,98},{3,99},{4,100},{5,101},{6,102},{7,103},{8,104... | collective-permute-start | bytes 983048 | tf_op jit(solution)/shard_map/ppermute | solution.py:26
  1.9 4.1 %collective-permute-start.1 = (bf16[128,1280]{0,1:T(8,128)(2,1)S(1)}, bf16[128,1280]{0,1:T(8,128)(2,1)S(1)}, u32[]{:S(2)}, u32[]{:S(2)}) collective-permute-start(bf16[128,1280]{0,1:T(8,128)(2,1)S(1)} %copy.29), channel_id=1, source_target_pairs={{0,32},{1,33},{2,34},{3,35},{4,36},{5,37},{6,38},{7,39},{8,40},{9,... | collective-permute-start | bytes 983048 | tf_op jit(solution)/shard_map/ppermute | solution.py:26
  2.6 8.8 %collective-permute-start.2 = (bf16[128,1280]{0,1:T(8,128)(2,1)S(1)}, bf16[128,1280]{0,1:T(8,128)(2,1)S(1)}, u32[]{:S(2)}, u32[]{:S(2)}) collective-permute-start(bf16[128,1280]{0,1:T(8,128)(2,1)S(1)} %copy.29), channel_id=1, source_target_pairs={{0,16},{1,17},{2,18},{3,19},{4,20},{5,21},{6,22},{7,23},{8,24},{9,... | collective-permute-start | bytes 983048 | tf_op jit(solution)/shard_map/ppermute | solution.py:26
  11.4 14.7 %collective-permute-start.3 = (bf16[128,1280]{0,1:T(8,128)(2,1)S(1)}, bf16[128,1280]{0,1:T(8,128)(2,1)S(1)}, u32[]{:S(2)}, u32[]{:S(2)}) collective-permute-start(bf16[128,1280]{0,1:T(8,128)(2,1)S(1)} %select_select_fusion), channel_id=1, source_target_pairs={{16,48},{32,64},{96,112},{0,80},{17,49},{33,65},{97,113},{1,81},{1... | collective-permute-start | bytes 983048 | tf_op jit(solution)/shard_map/ppermute | solution.py:30
  14.7 21.6 %all-to-all-start = ((s32[128,1,2]{2,1,0:T(1,128)}), s32[128,1,2]{2,1,0:T(1,128)S(1)}, u32[]{:S(2)}, u32[]{:S(2)}) async-start(s32[128,1,2]{2,1,0:T(1,128)} %bitcast.2), calls=%async_computation | async-start | bytes 131072 | tf_op jit(solution)/shard_map/all_to_all | solution.py:152
  36.3 47.7 %all-to-all-start.1 = ((f32[16,384,128]{2,1,0:T(8,128)}), f32[16,384,128]{2,1,0:T(8,128)S(1)}, u32[]{:S(2)}, u32[]{:S(2)}) async-start(f32[16,384,128]{2,1,0:T(8,128)} %bitcast.27), calls=%async_computation.1 | async-start | bytes 6291456 | tf_op jit(solution)/shard_map/all_to_all | solution.py:157
  87.3 15.3 %copy-start.2 = (f32[3,512]{1,0:T(4,128)S(1)}, f32[3,512]{1,0:T(4,128)}, u32[]{:S(2)}) copy-start(f32[3,512]{1,0:T(4,128)} %param.12) | copy-start | bytes 18436
  87.3 16.2 %copy-start = (f32[8,3,512]{2,0,1:T(8,128)S(1)}, f32[8,3,512]{2,0,1:T(8,128)}, u32[]{:S(2)}) copy-start(f32[8,3,512]{2,0,1:T(8,128)} %param.10) | copy-start | bytes 147460
  87.3 16.9 %copy-start.1 = (f32[8,512]{1,0:T(8,128)S(1)}, f32[8,512]{1,0:T(8,128)}, u32[]{:S(2)}) copy-start(f32[8,512]{1,0:T(8,128)} %param.11) | copy-start | bytes 49156
  87.3 16.9 %copy-start.3 = (s32[8]{0:T(128)S(1)}, s32[8]{0:T(128)}, u32[]{:S(2)}) copy-start(s32[8]{0:T(128)} %param.15) | copy-start | bytes 100
  87.3 67.4 %all-to-all-start.2 = ((bf16[128,128,128]{2,1,0:T(8,128)(2,1)}), bf16[128,128,128]{2,1,0:T(8,128)(2,1)}, u32[]{:S(2)}, u32[]{:S(2)}) async-start(bf16[128,128,128]{2,1,0:T(8,128)(2,1)} %bitcast.25), calls=%async_computation.2 | async-start | bytes 8388608 | tf_op jit(solution)/shard_map/all_to_all | solution.py:163
  175.0 57.3 %all-to-all-start.3 = ((bf16[128,128,128]{2,1,0:T(8,128)(2,1)}), bf16[128,128,128]{2,1,0:T(8,128)(2,1)}, u32[]{:S(2)}, u32[]{:S(2)}) async-start(bf16[128,128,128]{2,1,0:T(8,128)(2,1)} %bitcast.26), calls=%async_computation.3 | async-start | bytes 8388608 | tf_op jit(solution)/shard_map/all_to_all | solution.py:181

commit v12 on v11

--- a/solution.py
+++ b/solution.py
@@ -23,12 +23,10 @@
             value = jnp.where(index >= have, moved, value)
             have *= 2
         return value
-    first = [lax.ppermute(value, axis, [(0, dst)]) for dst in (1, 2, 6)]
-    value = jnp.where(index == 1, first[0], value)
-    value = jnp.where(index == 2, first[1], value)
-    value = jnp.where(index == 6, first[2], value)
-    second = lax.ppermute(value, axis, [(1, 3), (2, 4), (6, 7), (0, 5)])
-    return jnp.where((index == 3) | (index == 4) | (index == 5) | (index == 7), second, value)
+    for dst in range(1, size):
+        moved = lax.ppermute(value, axis, [(0, dst)])
+        value = jnp.where(index == dst, moved, value)
+    return value
 
 
 def potential(points, charge_sites):

time: 238 us -> 260 us (1.092)
  starting transfers between devices: 42.9 us -> 69.1 us
  waiting for transfers between devices: 146 us -> 143 us
    all_to_all x1, starting transfers between devices: 11.4 us -> 36.2 us  [on_device(): lax.all_to_all(wanted.reshape(owners, capacity), ('row', 'col'), split_ax...]
    ppermute x4 -> x7, waiting for transfers between devices: 5.39 us -> 2.53 us  [broadcast_from_first(): moved = lax.ppermute(value, axis, [(0, dst)])]
    ppermute x4 -> x7, starting transfers between devices: 3.97 us -> 5.38 us  [broadcast_from_first(): moved = lax.ppermute(value, axis, [(0, dst)])]
  transfers between devices with their start and end apart: 8 -> 11, of which waited for: 4 -> 4; matrix products, arithmetic and copies ran while one was open for 4% -> 3% of each run, Pallas kernels for 4% -> 4%
where the time goes in v12:
time: 260 us
  waiting for transfers between devices  143 us (55%)
  starting transfers between devices  69.1 us (27%)
  Pallas kernels  25 us (10%)
  local copies, waits for them, and re-layouts  14.7 us (6%)
  matrix products  4.47 us (2%)
  other arithmetic  3.3 us (1%)
    all_to_all x1, waiting for transfers between devices, on_device(): lax.all_to_all(tiles.reshape(owners, capacity * SH, slab_width), ('row',...  52.1 us
    all_to_all x1, waiting for transfers between devices, on_device(): lax.all_to_all(found.reshape(owners, capacity * SH, slab_width), ('row',...  49.2 us
    all_to_all x1, waiting for transfers between devices, on_device(): lax.all_to_all(partial.reshape(col_count, own_rows, slab_width), 'col', s...  39 us
    all_to_all x1, starting transfers between devices, on_device(): lax.all_to_all(wanted.reshape(owners, capacity), ('row', 'col'), split_ax...  36.2 us
    pallas_call x1, Pallas kernels, batch_terms(): pl.pallas_call(batch_kernel, grid_spec=grid_spec, out_shape=jax.ShapeDtyp...  15.6 us
    all_to_all x1, starting transfers between devices, on_device(): lax.all_to_all(found.reshape(owners, capacity * SH, slab_width), ('row',...  15.3 us
    pallas_call x1, Pallas kernels, slab_product(): pl.pallas_call(product_kernel, grid=(rows // block,), in_specs=[pl.BlockS...  9.38 us
    all_to_all x1, starting transfers between devices, on_device(): lax.all_to_all(partial.reshape(col_count, own_rows, slab_width), 'col', s...  7.1 us
  transfers between devices with their start and end apart: 11, of which 4 were waited for; matrix products, arithmetic and copies ran while one was open for 3% of the time, Pallas kernels for 4%

profile of v12, /device:TPU:1, one launch (start us, length us, event | category | flops | bytes accessed | tf_op | source)
XLA Modules:
  0.0 259.7 jit_solution(4305298181710178343)
XLA Ops:
  0.0 1.0 slice.3
  1.0 0.2 copy.29
  1.2 1.3 collective-permute-start
  2.5 2.5 collective-permute-done
  5.1 0.7 collective-permute-start.1
  5.8 0.7 collective-permute-start.2
  6.5 0.0 collective-permute-done.2
  6.6 0.7 collective-permute-start.3
  7.3 0.0 collective-permute-done.3
  7.3 0.7 collective-permute-start.4
  8.1 0.1 div.28
  8.1 0.1 rem.34
  8.2 0.1 ne.65
  8.3 0.0 collective-permute-done.4
  8.4 0.7 collective-permute-start.5
  9.1 0.1 div.27
  9.2 0.1 and.29
  9.2 0.1 fusion.2
  9.3 0.2 reduce_window_sum.11
  9.6 0.7 collective-permute-start.6
  10.2 0.2 select_reduce_fusion.1
  10.4 1.0 scatter_custom_fusion
  11.4 0.8 all_to_all.15
  12.2 36.2 %all-to-all-start = ((s32[128,1,2]{2,1,0:T(1,128)}), s32[128,1,2]{2,1,0:T(1,128)S(1)}, u32[]{:S(2)}, u32[]{:S(2)}) async-start(s32[128,1,2]{2,1,0:T(1,128)} %bitcast.2), calls=%async_computation | async-start | bytes 131072 | tf_op jit(solution)/shard_map/all_to_all | solution.py:150
  48.5 0.8 select_bitcast_fusion.window_ref
  49.2 9.4 %shard_map.82 = f32[6144,128]{1,0:T(8,128)} custom-call(bf16[6144,1280]{1,0:T(8,128)(2,1)} %coeff_ref.1, bf16[1280,128]{1,0:T(8,128)(2,1)} %select_bitcast_fusion.window_ref), custom_call_target="tpu_custom_call" | custom-call | tf_op jit(solution)/shard_map/pallas_call | solution.py:105
  58.6 7.1 %all-to-all-start.1 = ((f32[16,384,128]{2,1,0:T(8,128)}), f32[16,384,128]{2,1,0:T(8,128)S(1)}, u32[]{:S(2)}, u32[]{:S(2)}) async-start(f32[16,384,128]{2,1,0:T(8,128)} %bitcast.27), calls=%async_computation.1 | async-start | bytes 6291456 | tf_op jit(solution)/shard_map/all_to_all | solution.py:155
  65.7 0.5 broadcast.176
  66.2 1.0 fusion.12
  67.2 0.1 reshape.180
  67.4 39.0 %all-to-all-done.1 = f32[16,384,128]{2,1,0:T(8,128)S(1)} async-done(((f32[16,384,128]{2,1,0:T(8,128)}), f32[16,384,128]{2,1,0:T(8,128)S(1)}, u32[]{:S(2)}, u32[]{:S(2)}) %all-to-all-start.1) | async-done | bytes 3145760 | tf_op jit(solution)/shard_map/all_to_all | solution.py:155
  106.3 0.1 reduce_sum.33
  106.5 3.1 %gather_fusion = bf16[256,64,128]{2,1,0:T(8,128)(2,1)} fusion(bf16[6,64,128]{2,1,0:T(8,128)(2,1)S(1)} %bitcast.23, s32[1024]{0:T(1024)S(1)} %pad_clamp_fusion.1), kind=kCustom, calls=%fused_computation | custom fusion | bytes 8389632 | tf_op jit(solution)/shard_map/gather | solution.py:160
  109.6 15.3 %all-to-all-start.2 = ((bf16[128,128,128]{2,1,0:T(8,128)(2,1)}), bf16[128,128,128]{2,1,0:T(8,128)(2,1)}, u32[]{:S(2)}, u32[]{:S(2)}) async-start(bf16[128,128,128]{2,1,0:T(8,128)(2,1)} %bitcast.25), calls=%async_computation.2 | async-start | bytes 8388608 | tf_op jit(solution)/shard_map/all_to_all | solution.py:161
  124.9 0.9 copy.25
  125.7 0.7 copy.26.refs_17_
  126.4 0.1 fusion.3
  126.5 0.6 reshape.173.refs_18_
  127.1 0.5 broadcast_clamp_fusion
  127.6 0.1 select_reduce_fusion
  127.7 49.2 %all-to-all-done.2 = bf16[128,128,128]{2,1,0:T(8,128)(2,1)} async-done(((bf16[128,128,128]{2,1,0:T(8,128)(2,1)}), bf16[128,128,128]{2,1,0:T(8,128)(2,1)}, u32[]{:S(2)}, u32[]{:S(2)}) %all-to-all-start.2) | async-done | bytes 4194336 | tf_op jit(solution)/shard_map/all_to_all | solution.py:161
  177.0 15.6 %shard_map.83 = bf16[8,1024,128]{2,1,0:T(8,128)(2,1)} custom-call(s32[128]{0:T(128)} %get-tuple-element.9.slot_ref, bf16[256,64,128]{2,1,0:T(8,128)(2,1)} %bitcast.8.refs_0_.refs_1_.refs_2_.refs_3_.refs_4_.refs_5_.refs_6_.refs_7_.refs_8_.refs_9_.refs_10_.refs_11_.refs_12_.refs_13_.refs_14_.refs_15_, ...), custom_call_target="tpu_custom_call" | custom-call | tf_op jit(solution)/shard_map/pallas_call | solution.py:90
  192.6 4.6 %gather_fusion.1 = bf16[256,64,128]{2,1,0:T(8,128)(2,1)} fusion(bf16[128,64,128]{2,1,0:T(8,128)(2,1)} %bitcast.24, s32[1024]{0:T(1024)S(1)} %pad_clamp_fusion), kind=kCustom, calls=%fused_computation.1 | custom fusion | bytes 8389632 | tf_op jit(solution)/shard_map/gather | solution.py:178
  197.2 5.1 %all-to-all-start.3 = ((bf16[128,128,128]{2,1,0:T(8,128)(2,1)}), bf16[128,128,128]{2,1,0:T(8,128)(2,1)}, u32[]{:S(2)}, u32[]{:S(2)}) async-start(bf16[128,128,128]{2,1,0:T(8,128)(2,1)} %bitcast.26), calls=%async_computation.3 | async-start | bytes 8388608 | tf_op jit(solution)/shard_map/all_to_all | solution.py:179
  202.3 0.1 eq.68
  202.4 52.1 %all-to-all-done.3 = bf16[128,128,128]{2,1,0:T(8,128)(2,1)} async-done(((bf16[128,128,128]{2,1,0:T(8,128)(2,1)}), bf16[128,128,128]{2,1,0:T(8,128)(2,1)}, u32[]{:S(2)}, u32[]{:S(2)}) %all-to-all-start.3) | async-done | bytes 4194336 | tf_op jit(solution)/shard_map/all_to_all | solution.py:179
  254.5 4.5 %fusion = f32[6,64,128]{2,0,1:T(8,128)S(1)} fusion(bf16[256,64,128]{2,1,0:T(8,128)(2,1)} %bitcast.14, s32[256]{0:T(256)S(1)} %eq.68), kind=kOutput, calls=%fused_computation.3 | convolution fusion | flops 25167360 | bytes 4391936 | tf_op jit(solution)/shard_map/js,sfc->jfc/dot_general | solution.py:187
  259.0 0.7 copy.28
  (27 shorter events, 0.3 us)
Async XLA Ops:
  0.0 8.0 %copy-start.1 = (s32[8,16]{1,0:T(8,128)S(1)}, s32[8,16]{1,0:T(8,128)}, u32[]{:S(2)}) copy-start(s32[8,16]{1,0:T(8,128)} %param.14) | copy-start | bytes 1540
  1.2 3.8 %collective-permute-start = (bf16[128,1280]{0,1:T(8,128)(2,1)S(1)}, bf16[128,1280]{0,1:T(8,128)(2,1)S(1)}, u32[]{:S(2)}, u32[]{:S(2)}) collective-permute-start(bf16[128,1280]{0,1:T(8,128)(2,1)S(1)} %copy.29), channel_id=1, source_target_pairs={{0,16},{1,17},{2,18},{3,19},{4,20},{5,21},{6,22},{7,23},{8,24},{9,... | collective-permute-start | bytes 983048 | tf_op jit(solution)/shard_map/ppermute | solution.py:27
  5.1 0.7 collective-permute-start.1
  5.8 0.7 collective-permute-start.2
  6.6 0.7 collective-permute-start.3
  7.3 1.0 collective-permute-start.4
  8.4 1.1 collective-permute-start.5
  9.6 38.9 %collective-permute-start.6 = (bf16[128,1280]{0,1:T(8,128)(2,1)S(1)}, bf16[128,1280]{0,1:T(8,128)(2,1)S(1)}, u32[]{:S(2)}, u32[]{:S(2)}) collective-permute-start(bf16[128,1280]{0,1:T(8,128)(2,1)S(1)} %broadcast_select_fusion.5), channel_id=1, source_target_pairs={{0,112},{1,113},{2,114},{3,115},{4,116},{5,117},{6,118},{7,119},{8... | collective-permute-start | bytes 983048 | tf_op jit(solution)/shard_map/ppermute | solution.py:27
  12.2 46.4 %all-to-all-start = ((s32[128,1,2]{2,1,0:T(1,128)}), s32[128,1,2]{2,1,0:T(1,128)S(1)}, u32[]{:S(2)}, u32[]{:S(2)}) async-start(s32[128,1,2]{2,1,0:T(1,128)} %bitcast.2), calls=%async_computation | async-start | bytes 131072 | tf_op jit(solution)/shard_map/all_to_all | solution.py:150
  58.6 47.7 %all-to-all-start.1 = ((f32[16,384,128]{2,1,0:T(8,128)}), f32[16,384,128]{2,1,0:T(8,128)S(1)}, u32[]{:S(2)}, u32[]{:S(2)}) async-start(f32[16,384,128]{2,1,0:T(8,128)} %bitcast.27), calls=%async_computation.1 | async-start | bytes 6291456 | tf_op jit(solution)/shard_map/all_to_all | solution.py:155
  109.6 15.3 %copy-start.3 = (f32[3,512]{1,0:T(4,128)S(1)}, f32[3,512]{1,0:T(4,128)}, u32[]{:S(2)}) copy-start(f32[3,512]{1,0:T(4,128)} %param.12) | copy-start | bytes 18436
  109.6 16.2 %copy-start = (f32[8,3,512]{2,0,1:T(8,128)S(1)}, f32[8,3,512]{2,0,1:T(8,128)}, u32[]{:S(2)}) copy-start(f32[8,3,512]{2,0,1:T(8,128)} %param.10) | copy-start | bytes 147460
  109.6 16.9 %copy-start.2 = (f32[8,512]{1,0:T(8,128)S(1)}, f32[8,512]{1,0:T(8,128)}, u32[]{:S(2)}) copy-start(f32[8,512]{1,0:T(8,128)} %param.11) | copy-start | bytes 49156
  109.6 16.9 %copy-start.4 = (s32[8]{0:T(128)S(1)}, s32[8]{0:T(128)}, u32[]{:S(2)}) copy-start(s32[8]{0:T(128)} %param.15) | copy-start | bytes 100
  109.6 67.4 %all-to-all-start.2 = ((bf16[128,128,128]{2,1,0:T(8,128)(2,1)}), bf16[128,128,128]{2,1,0:T(8,128)(2,1)}, u32[]{:S(2)}, u32[]{:S(2)}) async-start(bf16[128,128,128]{2,1,0:T(8,128)(2,1)} %bitcast.25), calls=%async_computation.2 | async-start | bytes 8388608 | tf_op jit(solution)/shard_map/all_to_all | solution.py:161
  197.2 57.3 %all-to-all-start.3 = ((bf16[128,128,128]{2,1,0:T(8,128)(2,1)}), bf16[128,128,128]{2,1,0:T(8,128)(2,1)}, u32[]{:S(2)}, u32[]{:S(2)}) async-start(bf16[128,128,128]{2,1,0:T(8,128)(2,1)} %bitcast.26), calls=%async_computation.3 | async-start | bytes 8388608 | tf_op jit(solution)/shard_map/all_to_all | solution.py:179

commit v13 on v11

--- a/solution.py
+++ b/solution.py
@@ -103,7 +103,7 @@
 def slab_product(occ_coeffs, window):
     rows, depth = occ_coeffs.shape
     width = window.shape[0]
-    block = 1536 if rows % 1536 == 0 else rows
+    block = 768 if rows % 768 == 0 else rows
     return pl.pallas_call(
         product_kernel,
         grid=(rows // block,),

time: 238 us -> 240 us (level)
  transfers between devices with their start and end apart: 8 -> 8, of which waited for: 4 -> 4; matrix products, arithmetic and copies ran while one was open for 4% -> 4% of each run, Pallas kernels for 4% -> 5%
where the time goes in v13:
time: 240 us; the launch traced here: 239 us
  waiting for transfers between devices  146 us (61%)
  starting transfers between devices  42.9 us (18%)
  Pallas kernels  26.9 us (11%)
  local copies, waits for them, and re-layouts  14.7 us (6%)
  other arithmetic  4.51 us (2%)
  matrix products  4.47 us (2%)
    all_to_all x1, waiting for transfers between devices, on_device(): lax.all_to_all(tiles.reshape(owners, capacity * SH, slab_width), ('row',...  52.1 us
    all_to_all x1, waiting for transfers between devices, on_device(): lax.all_to_all(found.reshape(owners, capacity * SH, slab_width), ('row',...  49.2 us
    all_to_all x1, waiting for transfers between devices, on_device(): lax.all_to_all(partial.reshape(col_count, own_rows, slab_width), 'col', s...  39 us
    pallas_call x1, Pallas kernels, batch_terms(): pl.pallas_call(batch_kernel, grid_spec=grid_spec, out_shape=jax.ShapeDtyp...  15.7 us
    all_to_all x1, starting transfers between devices, on_device(): lax.all_to_all(found.reshape(owners, capacity * SH, slab_width), ('row',...  15.3 us
    all_to_all x1, starting transfers between devices, on_device(): lax.all_to_all(wanted.reshape(owners, capacity), ('row', 'col'), split_ax...  11.4 us
    pallas_call x1, Pallas kernels, slab_product(): pl.pallas_call(product_kernel, grid=(rows // block,), in_specs=[pl.BlockS...  11.3 us
    all_to_all x1, starting transfers between devices, on_device(): lax.all_to_all(partial.reshape(col_count, own_rows, slab_width), 'col', s...  7.1 us
  transfers between devices with their start and end apart: 8, of which 4 were waited for; matrix products, arithmetic and copies ran while one was open for 4% of the time, Pallas kernels for 5%

profile of v13, /device:TPU:1, one launch (start us, length us, event | category | flops | bytes accessed | tf_op | source)
XLA Modules:
  0.0 239.4 jit_solution(4601379953055021864)
XLA Ops:
  0.0 1.0 slice.3
  1.0 0.2 copy.29
  1.2 0.7 collective-permute-start
  1.9 0.7 collective-permute-start.1
  2.6 1.3 collective-permute-start.2
  3.9 0.7 broadcast_remainder_fusion
  4.6 0.7 compare_and_fusion
  5.3 0.1 div.28
  5.4 0.1 rem.34
  5.4 0.1 ne.65
  5.5 0.1 div.27
  5.6 0.1 and.29
  5.7 0.1 fusion.2
  5.8 0.2 reduce_window_sum.11
  6.0 0.0 collective-permute-done
  6.0 0.0 collective-permute-done.1
  6.0 5.4 %collective-permute-done.2 = bf16[128,1280]{0,1:T(8,128)(2,1)S(1)} collective-permute-done((bf16[128,1280]{0,1:T(8,128)(2,1)S(1)}, bf16[128,1280]{0,1:T(8,128)(2,1)S(1)}, u32[]{:S(2)}, u32[]{:S(2)}) %collective-permute-start.2) | collective-permute-done | bytes 327712 | tf_op jit(solution)/shard_map/ppermute | solution.py:26
  11.4 0.1 select_select_fusion
  11.4 1.3 collective-permute-start.3
  12.8 0.2 select_reduce_fusion.1
  12.9 1.0 scatter_custom_fusion
  13.9 0.8 all_to_all.15
  14.7 11.4 %all-to-all-start = ((s32[128,1,2]{2,1,0:T(1,128)}), s32[128,1,2]{2,1,0:T(1,128)S(1)}, u32[]{:S(2)}, u32[]{:S(2)}) async-start(s32[128,1,2]{2,1,0:T(1,128)} %bitcast.2), calls=%async_computation | async-start | bytes 131072 | tf_op jit(solution)/shard_map/all_to_all | solution.py:152
  26.2 0.8 select_bitcast_fusion.window_ref
  26.9 11.3 %shard_map.82 = f32[6144,128]{1,0:T(8,128)} custom-call(bf16[6144,1280]{1,0:T(8,128)(2,1)} %coeff_ref.1, bf16[1280,128]{1,0:T(8,128)(2,1)} %select_bitcast_fusion.window_ref), custom_call_target="tpu_custom_call" | custom-call | tf_op jit(solution)/shard_map/pallas_call | solution.py:107
  38.2 0.0 all-to-all-done
  38.2 7.1 %all-to-all-start.1 = ((f32[16,384,128]{2,1,0:T(8,128)}), f32[16,384,128]{2,1,0:T(8,128)S(1)}, u32[]{:S(2)}, u32[]{:S(2)}) async-start(f32[16,384,128]{2,1,0:T(8,128)} %bitcast.27), calls=%async_computation.1 | async-start | bytes 6291456 | tf_op jit(solution)/shard_map/all_to_all | solution.py:157
  45.3 0.5 broadcast.176
  45.8 1.0 fusion.12
  46.8 0.1 reshape.180
  47.0 39.0 %all-to-all-done.1 = f32[16,384,128]{2,1,0:T(8,128)S(1)} async-done(((f32[16,384,128]{2,1,0:T(8,128)}), f32[16,384,128]{2,1,0:T(8,128)S(1)}, u32[]{:S(2)}, u32[]{:S(2)}) %all-to-all-start.1) | async-done | bytes 3145760 | tf_op jit(solution)/shard_map/all_to_all | solution.py:157
  85.9 0.1 reduce_sum.33
  86.1 3.1 %gather_fusion = bf16[256,64,128]{2,1,0:T(8,128)(2,1)} fusion(bf16[6,64,128]{2,1,0:T(8,128)(2,1)S(1)} %bitcast.23, s32[1024]{0:T(1024)S(1)} %pad_clamp_fusion.1), kind=kCustom, calls=%fused_computation | custom fusion | bytes 8389632 | tf_op jit(solution)/shard_map/gather | solution.py:162
  89.2 15.3 %all-to-all-start.2 = ((bf16[128,128,128]{2,1,0:T(8,128)(2,1)}), bf16[128,128,128]{2,1,0:T(8,128)(2,1)}, u32[]{:S(2)}, u32[]{:S(2)}) async-start(bf16[128,128,128]{2,1,0:T(8,128)(2,1)} %bitcast.25), calls=%async_computation.2 | async-start | bytes 8388608 | tf_op jit(solution)/shard_map/all_to_all | solution.py:163
  104.5 0.9 copy.25
  105.4 0.7 copy.26.refs_17_
  106.0 0.1 fusion.3
  106.1 0.6 reshape.173.refs_18_
  106.7 0.5 broadcast_clamp_fusion
  107.2 0.1 select_reduce_fusion
  107.3 49.2 %all-to-all-done.2 = bf16[128,128,128]{2,1,0:T(8,128)(2,1)} async-done(((bf16[128,128,128]{2,1,0:T(8,128)(2,1)}), bf16[128,128,128]{2,1,0:T(8,128)(2,1)}, u32[]{:S(2)}, u32[]{:S(2)}) %all-to-all-start.2) | async-done | bytes 4194336 | tf_op jit(solution)/shard_map/all_to_all | solution.py:163
  156.6 15.7 %shard_map.83 = bf16[8,1024,128]{2,1,0:T(8,128)(2,1)} custom-call(s32[128]{0:T(128)} %get-tuple-element.9.slot_ref, bf16[256,64,128]{2,1,0:T(8,128)(2,1)} %bitcast.8.refs_0_.refs_1_.refs_2_.refs_3_.refs_4_.refs_5_.refs_6_.refs_7_.refs_8_.refs_9_.refs_10_.refs_11_.refs_12_.refs_13_.refs_14_.refs_15_, ...), custom_call_target="tpu_custom_call" | custom-call | tf_op jit(solution)/shard_map/pallas_call | solution.py:92
  172.2 4.6 %gather_fusion.1 = bf16[256,64,128]{2,1,0:T(8,128)(2,1)} fusion(bf16[128,64,128]{2,1,0:T(8,128)(2,1)} %bitcast.24, s32[1024]{0:T(1024)S(1)} %pad_clamp_fusion), kind=kCustom, calls=%fused_computation.1 | custom fusion | bytes 8389632 | tf_op jit(solution)/shard_map/gather | solution.py:180
  176.8 5.1 %all-to-all-start.3 = ((bf16[128,128,128]{2,1,0:T(8,128)(2,1)}), bf16[128,128,128]{2,1,0:T(8,128)(2,1)}, u32[]{:S(2)}, u32[]{:S(2)}) async-start(bf16[128,128,128]{2,1,0:T(8,128)(2,1)} %bitcast.26), calls=%async_computation.3 | async-start | bytes 8388608 | tf_op jit(solution)/shard_map/all_to_all | solution.py:181
  181.9 0.1 eq.68
  182.1 52.1 %all-to-all-done.3 = bf16[128,128,128]{2,1,0:T(8,128)(2,1)} async-done(((bf16[128,128,128]{2,1,0:T(8,128)(2,1)}), bf16[128,128,128]{2,1,0:T(8,128)(2,1)}, u32[]{:S(2)}, u32[]{:S(2)}) %all-to-all-start.3) | async-done | bytes 4194336 | tf_op jit(solution)/shard_map/all_to_all | solution.py:181
  234.2 4.5 %fusion = f32[6,64,128]{2,0,1:T(8,128)S(1)} fusion(bf16[256,64,128]{2,1,0:T(8,128)(2,1)} %bitcast.14, s32[256]{0:T(256)S(1)} %eq.68), kind=kOutput, calls=%fused_computation.3 | convolution fusion | flops 25167360 | bytes 4391936 | tf_op jit(solution)/shard_map/js,sfc->jfc/dot_general | solution.py:189
  238.7 0.7 copy.28
  (14 shorter events, 0.1 us)
Async XLA Ops:
  1.2 4.8 %collective-permute-start = (bf16[128,1280]{0,1:T(8,128)(2,1)S(1)}, bf16[128,1280]{0,1:T(8,128)(2,1)S(1)}, u32[]{:S(2)}, u32[]{:S(2)}) collective-permute-start(bf16[128,1280]{0,1:T(8,128)(2,1)S(1)} %copy.29), channel_id=1, source_target_pairs={{0,96},{1,97},{2,98},{3,99},{4,100},{5,101},{6,102},{7,103},{8,104... | collective-permute-start | bytes 983048 | tf_op jit(solution)/shard_map/ppermute | solution.py:26
  1.9 4.1 %collective-permute-start.1 = (bf16[128,1280]{0,1:T(8,128)(2,1)S(1)}, bf16[128,1280]{0,1:T(8,128)(2,1)S(1)}, u32[]{:S(2)}, u32[]{:S(2)}) collective-permute-start(bf16[128,1280]{0,1:T(8,128)(2,1)S(1)} %copy.29), channel_id=1, source_target_pairs={{0,32},{1,33},{2,34},{3,35},{4,36},{5,37},{6,38},{7,39},{8,40},{9,... | collective-permute-start | bytes 983048 | tf_op jit(solution)/shard_map/ppermute | solution.py:26
  2.6 8.8 %collective-permute-start.2 = (bf16[128,1280]{0,1:T(8,128)(2,1)S(1)}, bf16[128,1280]{0,1:T(8,128)(2,1)S(1)}, u32[]{:S(2)}, u32[]{:S(2)}) collective-permute-start(bf16[128,1280]{0,1:T(8,128)(2,1)S(1)} %copy.29), channel_id=1, source_target_pairs={{0,16},{1,17},{2,18},{3,19},{4,20},{5,21},{6,22},{7,23},{8,24},{9,... | collective-permute-start | bytes 983048 | tf_op jit(solution)/shard_map/ppermute | solution.py:26
  11.4 14.7 %collective-permute-start.3 = (bf16[128,1280]{0,1:T(8,128)(2,1)S(1)}, bf16[128,1280]{0,1:T(8,128)(2,1)S(1)}, u32[]{:S(2)}, u32[]{:S(2)}) collective-permute-start(bf16[128,1280]{0,1:T(8,128)(2,1)S(1)} %select_select_fusion), channel_id=1, source_target_pairs={{16,48},{32,64},{96,112},{0,80},{17,49},{33,65},{97,113},{1,81},{1... | collective-permute-start | bytes 983048 | tf_op jit(solution)/shard_map/ppermute | solution.py:30
  14.7 23.5 %all-to-all-start = ((s32[128,1,2]{2,1,0:T(1,128)}), s32[128,1,2]{2,1,0:T(1,128)S(1)}, u32[]{:S(2)}, u32[]{:S(2)}) async-start(s32[128,1,2]{2,1,0:T(1,128)} %bitcast.2), calls=%async_computation | async-start | bytes 131072 | tf_op jit(solution)/shard_map/all_to_all | solution.py:152
  38.2 47.7 %all-to-all-start.1 = ((f32[16,384,128]{2,1,0:T(8,128)}), f32[16,384,128]{2,1,0:T(8,128)S(1)}, u32[]{:S(2)}, u32[]{:S(2)}) async-start(f32[16,384,128]{2,1,0:T(8,128)} %bitcast.27), calls=%async_computation.1 | async-start | bytes 6291456 | tf_op jit(solution)/shard_map/all_to_all | solution.py:157
  89.1 15.3 %copy-start.2 = (f32[3,512]{1,0:T(4,128)S(1)}, f32[3,512]{1,0:T(4,128)}, u32[]{:S(2)}) copy-start(f32[3,512]{1,0:T(4,128)} %param.12) | copy-start | bytes 18436
  89.2 16.2 %copy-start = (f32[8,3,512]{2,0,1:T(8,128)S(1)}, f32[8,3,512]{2,0,1:T(8,128)}, u32[]{:S(2)}) copy-start(f32[8,3,512]{2,0,1:T(8,128)} %param.10) | copy-start | bytes 147460
  89.2 16.9 %copy-start.1 = (f32[8,512]{1,0:T(8,128)S(1)}, f32[8,512]{1,0:T(8,128)}, u32[]{:S(2)}) copy-start(f32[8,512]{1,0:T(8,128)} %param.11) | copy-start | bytes 49156
  89.2 16.9 %copy-start.3 = (s32[8]{0:T(128)S(1)}, s32[8]{0:T(128)}, u32[]{:S(2)}) copy-start(s32[8]{0:T(128)} %param.15) | copy-start | bytes 100
  89.2 67.4 %all-to-all-start.2 = ((bf16[128,128,128]{2,1,0:T(8,128)(2,1)}), bf16[128,128,128]{2,1,0:T(8,128)(2,1)}, u32[]{:S(2)}, u32[]{:S(2)}) async-start(bf16[128,128,128]{2,1,0:T(8,128)(2,1)} %bitcast.25), calls=%async_computation.2 | async-start | bytes 8388608 | tf_op jit(solution)/shard_map/all_to_all | solution.py:163
  176.8 57.3 %all-to-all-start.3 = ((bf16[128,128,128]{2,1,0:T(8,128)(2,1)}), bf16[128,128,128]{2,1,0:T(8,128)(2,1)}, u32[]{:S(2)}, u32[]{:S(2)}) async-start(bf16[128,128,128]{2,1,0:T(8,128)(2,1)} %bitcast.26), calls=%async_computation.3 | async-start | bytes 8388608 | tf_op jit(solution)/shard_map/all_to_all | solution.py:181

commit v14 on v13

--- a/solution.py
+++ b/solution.py
@@ -103,7 +103,7 @@
 def slab_product(occ_coeffs, window):
     rows, depth = occ_coeffs.shape
     width = window.shape[0]
-    block = 768 if rows % 768 == 0 else rows
+    block = 3072 if rows % 3072 == 0 else rows
     return pl.pallas_call(
         product_kernel,
         grid=(rows // block,),

time: 240 us -> 238 us (level)
  transfers between devices with their start and end apart: 8 -> 8, of which waited for: 4 -> 4; matrix products, arithmetic and copies ran while one was open for 4% -> 4% of each run, Pallas kernels for 5% -> 4%
where the time goes in v14:
time: 238 us; the launch traced here: 237 us
  waiting for transfers between devices  146 us (61%)
  starting transfers between devices  42.9 us (18%)
  Pallas kernels  24.6 us (10%)
  local copies, waits for them, and re-layouts  14.7 us (6%)
  other arithmetic  4.51 us (2%)
  matrix products  4.47 us (2%)
    all_to_all x1, waiting for transfers between devices, on_device(): lax.all_to_all(tiles.reshape(owners, capacity * SH, slab_width), ('row',...  52.1 us
    all_to_all x1, waiting for transfers between devices, on_device(): lax.all_to_all(found.reshape(owners, capacity * SH, slab_width), ('row',...  49.2 us
    all_to_all x1, waiting for transfers between devices, on_device(): lax.all_to_all(partial.reshape(col_count, own_rows, slab_width), 'col', s...  39 us
    pallas_call x1, Pallas kernels, batch_terms(): pl.pallas_call(batch_kernel, grid_spec=grid_spec, out_shape=jax.ShapeDtyp...  15.7 us
    all_to_all x1, starting transfers between devices, on_device(): lax.all_to_all(found.reshape(owners, capacity * SH, slab_width), ('row',...  15.3 us
    all_to_all x1, starting transfers between devices, on_device(): lax.all_to_all(wanted.reshape(owners, capacity), ('row', 'col'), split_ax...  11.4 us
    pallas_call x1, Pallas kernels, slab_product(): pl.pallas_call(product_kernel, grid=(rows // block,), in_specs=[pl.BlockS...  8.93 us
    all_to_all x1, starting transfers between devices, on_device(): lax.all_to_all(partial.reshape(col_count, own_rows, slab_width), 'col', s...  7.1 us
  transfers between devices with their start and end apart: 8, of which 4 were waited for; matrix products, arithmetic and copies ran while one was open for 4% of the time, Pallas kernels for 4%

profile of v14, /device:TPU:1, one launch (start us, length us, event | category | flops | bytes accessed | tf_op | source)
XLA Modules:
  0.0 237.0 jit_solution(1593650389735038180)
XLA Ops:
  0.0 1.0 slice.3
  1.0 0.2 copy.29
  1.2 0.7 collective-permute-start
  1.9 0.7 collective-permute-start.1
  2.6 1.3 collective-permute-start.2
  3.9 0.7 broadcast_remainder_fusion
  4.6 0.7 compare_and_fusion
  5.3 0.1 div.28
  5.4 0.1 rem.34
  5.4 0.1 ne.65
  5.5 0.1 div.27
  5.6 0.1 and.29
  5.7 0.1 fusion.2
  5.8 0.2 reduce_window_sum.11
  6.0 0.0 collective-permute-done
  6.0 0.0 collective-permute-done.1
  6.0 5.4 %collective-permute-done.2 = bf16[128,1280]{0,1:T(8,128)(2,1)S(1)} collective-permute-done((bf16[128,1280]{0,1:T(8,128)(2,1)S(1)}, bf16[128,1280]{0,1:T(8,128)(2,1)S(1)}, u32[]{:S(2)}, u32[]{:S(2)}) %collective-permute-start.2) | collective-permute-done | bytes 327712 | tf_op jit(solution)/shard_map/ppermute | solution.py:26
  11.4 0.1 select_select_fusion
  11.4 1.3 collective-permute-start.3
  12.8 0.2 select_reduce_fusion.1
  12.9 1.0 scatter_custom_fusion
  13.9 0.8 all_to_all.15
  14.7 11.4 %all-to-all-start = ((s32[128,1,2]{2,1,0:T(1,128)}), s32[128,1,2]{2,1,0:T(1,128)S(1)}, u32[]{:S(2)}, u32[]{:S(2)}) async-start(s32[128,1,2]{2,1,0:T(1,128)} %bitcast.2), calls=%async_computation | async-start | bytes 131072 | tf_op jit(solution)/shard_map/all_to_all | solution.py:152
  26.2 0.0 collective-permute-done.3
  26.2 0.8 select_bitcast_fusion.window_ref
  26.9 8.9 %shard_map.82 = f32[6144,128]{1,0:T(8,128)} custom-call(bf16[6144,1280]{1,0:T(8,128)(2,1)} %coeff_ref.1, bf16[1280,128]{1,0:T(8,128)(2,1)} %select_bitcast_fusion.window_ref), custom_call_target="tpu_custom_call" | custom-call | tf_op jit(solution)/shard_map/pallas_call | solution.py:107
  35.9 7.1 %all-to-all-start.1 = ((f32[16,384,128]{2,1,0:T(8,128)}), f32[16,384,128]{2,1,0:T(8,128)S(1)}, u32[]{:S(2)}, u32[]{:S(2)}) async-start(f32[16,384,128]{2,1,0:T(8,128)} %bitcast.27), calls=%async_computation.1 | async-start | bytes 6291456 | tf_op jit(solution)/shard_map/all_to_all | solution.py:157
  43.0 0.5 broadcast.176
  43.5 1.0 fusion.12
  44.5 0.1 reshape.180
  44.7 39.0 %all-to-all-done.1 = f32[16,384,128]{2,1,0:T(8,128)S(1)} async-done(((f32[16,384,128]{2,1,0:T(8,128)}), f32[16,384,128]{2,1,0:T(8,128)S(1)}, u32[]{:S(2)}, u32[]{:S(2)}) %all-to-all-start.1) | async-done | bytes 3145760 | tf_op jit(solution)/shard_map/all_to_all | solution.py:157
  83.6 0.1 reduce_sum.33
  83.8 3.1 %gather_fusion = bf16[256,64,128]{2,1,0:T(8,128)(2,1)} fusion(bf16[6,64,128]{2,1,0:T(8,128)(2,1)S(1)} %bitcast.23, s32[1024]{0:T(1024)S(1)} %pad_clamp_fusion.1), kind=kCustom, calls=%fused_computation | custom fusion | bytes 8389632 | tf_op jit(solution)/shard_map/gather | solution.py:162
  86.8 15.3 %all-to-all-start.2 = ((bf16[128,128,128]{2,1,0:T(8,128)(2,1)}), bf16[128,128,128]{2,1,0:T(8,128)(2,1)}, u32[]{:S(2)}, u32[]{:S(2)}) async-start(bf16[128,128,128]{2,1,0:T(8,128)(2,1)} %bitcast.25), calls=%async_computation.2 | async-start | bytes 8388608 | tf_op jit(solution)/shard_map/all_to_all | solution.py:163
  102.1 0.9 copy.25
  103.0 0.7 copy.26.refs_17_
  103.7 0.1 fusion.3
  103.8 0.6 reshape.173.refs_18_
  104.4 0.5 broadcast_clamp_fusion
  104.9 0.1 select_reduce_fusion
  105.0 49.2 %all-to-all-done.2 = bf16[128,128,128]{2,1,0:T(8,128)(2,1)} async-done(((bf16[128,128,128]{2,1,0:T(8,128)(2,1)}), bf16[128,128,128]{2,1,0:T(8,128)(2,1)}, u32[]{:S(2)}, u32[]{:S(2)}) %all-to-all-start.2) | async-done | bytes 4194336 | tf_op jit(solution)/shard_map/all_to_all | solution.py:163
  154.2 15.7 %shard_map.83 = bf16[8,1024,128]{2,1,0:T(8,128)(2,1)} custom-call(s32[128]{0:T(128)} %get-tuple-element.9.slot_ref, bf16[256,64,128]{2,1,0:T(8,128)(2,1)} %bitcast.8.refs_0_.refs_1_.refs_2_.refs_3_.refs_4_.refs_5_.refs_6_.refs_7_.refs_8_.refs_9_.refs_10_.refs_11_.refs_12_.refs_13_.refs_14_.refs_15_, ...), custom_call_target="tpu_custom_call" | custom-call | tf_op jit(solution)/shard_map/pallas_call | solution.py:92
  169.9 4.6 %gather_fusion.1 = bf16[256,64,128]{2,1,0:T(8,128)(2,1)} fusion(bf16[128,64,128]{2,1,0:T(8,128)(2,1)} %bitcast.24, s32[1024]{0:T(1024)S(1)} %pad_clamp_fusion), kind=kCustom, calls=%fused_computation.1 | custom fusion | bytes 8389632 | tf_op jit(solution)/shard_map/gather | solution.py:180
  174.5 5.1 %all-to-all-start.3 = ((bf16[128,128,128]{2,1,0:T(8,128)(2,1)}), bf16[128,128,128]{2,1,0:T(8,128)(2,1)}, u32[]{:S(2)}, u32[]{:S(2)}) async-start(bf16[128,128,128]{2,1,0:T(8,128)(2,1)} %bitcast.26), calls=%async_computation.3 | async-start | bytes 8388608 | tf_op jit(solution)/shard_map/all_to_all | solution.py:181
  179.6 0.1 eq.68
  179.7 52.1 %all-to-all-done.3 = bf16[128,128,128]{2,1,0:T(8,128)(2,1)} async-done(((bf16[128,128,128]{2,1,0:T(8,128)(2,1)}), bf16[128,128,128]{2,1,0:T(8,128)(2,1)}, u32[]{:S(2)}, u32[]{:S(2)}) %all-to-all-start.3) | async-done | bytes 4194336 | tf_op jit(solution)/shard_map/all_to_all | solution.py:181
  231.8 4.5 %fusion = f32[6,64,128]{2,0,1:T(8,128)S(1)} fusion(bf16[256,64,128]{2,1,0:T(8,128)(2,1)} %bitcast.14, s32[256]{0:T(256)S(1)} %eq.68), kind=kOutput, calls=%fused_computation.3 | convolution fusion | flops 25167360 | bytes 4391936 | tf_op jit(solution)/shard_map/js,sfc->jfc/dot_general | solution.py:189
  236.3 0.7 copy.28
  (14 shorter events, 0.1 us)
Async XLA Ops:
  1.2 4.8 %collective-permute-start = (bf16[128,1280]{0,1:T(8,128)(2,1)S(1)}, bf16[128,1280]{0,1:T(8,128)(2,1)S(1)}, u32[]{:S(2)}, u32[]{:S(2)}) collective-permute-start(bf16[128,1280]{0,1:T(8,128)(2,1)S(1)} %copy.29), channel_id=1, source_target_pairs={{0,96},{1,97},{2,98},{3,99},{4,100},{5,101},{6,102},{7,103},{8,104... | collective-permute-start | bytes 983048 | tf_op jit(solution)/shard_map/ppermute | solution.py:26
  1.9 4.1 %collective-permute-start.1 = (bf16[128,1280]{0,1:T(8,128)(2,1)S(1)}, bf16[128,1280]{0,1:T(8,128)(2,1)S(1)}, u32[]{:S(2)}, u32[]{:S(2)}) collective-permute-start(bf16[128,1280]{0,1:T(8,128)(2,1)S(1)} %copy.29), channel_id=1, source_target_pairs={{0,32},{1,33},{2,34},{3,35},{4,36},{5,37},{6,38},{7,39},{8,40},{9,... | collective-permute-start | bytes 983048 | tf_op jit(solution)/shard_map/ppermute | solution.py:26
  2.6 8.8 %collective-permute-start.2 = (bf16[128,1280]{0,1:T(8,128)(2,1)S(1)}, bf16[128,1280]{0,1:T(8,128)(2,1)S(1)}, u32[]{:S(2)}, u32[]{:S(2)}) collective-permute-start(bf16[128,1280]{0,1:T(8,128)(2,1)S(1)} %copy.29), channel_id=1, source_target_pairs={{0,16},{1,17},{2,18},{3,19},{4,20},{5,21},{6,22},{7,23},{8,24},{9,... | collective-permute-start | bytes 983048 | tf_op jit(solution)/shard_map/ppermute | solution.py:26
  11.4 14.7 %collective-permute-start.3 = (bf16[128,1280]{0,1:T(8,128)(2,1)S(1)}, bf16[128,1280]{0,1:T(8,128)(2,1)S(1)}, u32[]{:S(2)}, u32[]{:S(2)}) collective-permute-start(bf16[128,1280]{0,1:T(8,128)(2,1)S(1)} %select_select_fusion), channel_id=1, source_target_pairs={{16,48},{32,64},{96,112},{0,80},{17,49},{33,65},{97,113},{1,81},{1... | collective-permute-start | bytes 983048 | tf_op jit(solution)/shard_map/ppermute | solution.py:30
  14.7 21.2 %all-to-all-start = ((s32[128,1,2]{2,1,0:T(1,128)}), s32[128,1,2]{2,1,0:T(1,128)S(1)}, u32[]{:S(2)}, u32[]{:S(2)}) async-start(s32[128,1,2]{2,1,0:T(1,128)} %bitcast.2), calls=%async_computation | async-start | bytes 131072 | tf_op jit(solution)/shard_map/all_to_all | solution.py:152
  35.9 47.7 %all-to-all-start.1 = ((f32[16,384,128]{2,1,0:T(8,128)}), f32[16,384,128]{2,1,0:T(8,128)S(1)}, u32[]{:S(2)}, u32[]{:S(2)}) async-start(f32[16,384,128]{2,1,0:T(8,128)} %bitcast.27), calls=%async_computation.1 | async-start | bytes 6291456 | tf_op jit(solution)/shard_map/all_to_all | solution.py:157
  86.8 15.3 %copy-start.2 = (f32[3,512]{1,0:T(4,128)S(1)}, f32[3,512]{1,0:T(4,128)}, u32[]{:S(2)}) copy-start(f32[3,512]{1,0:T(4,128)} %param.12) | copy-start | bytes 18436
  86.8 16.2 %copy-start = (f32[8,3,512]{2,0,1:T(8,128)S(1)}, f32[8,3,512]{2,0,1:T(8,128)}, u32[]{:S(2)}) copy-start(f32[8,3,512]{2,0,1:T(8,128)} %param.10) | copy-start | bytes 147460
  86.8 16.9 %copy-start.1 = (f32[8,512]{1,0:T(8,128)S(1)}, f32[8,512]{1,0:T(8,128)}, u32[]{:S(2)}) copy-start(f32[8,512]{1,0:T(8,128)} %param.11) | copy-start | bytes 49156
  86.8 16.9 %copy-start.3 = (s32[8]{0:T(128)S(1)}, s32[8]{0:T(128)}, u32[]{:S(2)}) copy-start(s32[8]{0:T(128)} %param.15) | copy-start | bytes 100
  86.8 67.4 %all-to-all-start.2 = ((bf16[128,128,128]{2,1,0:T(8,128)(2,1)}), bf16[128,128,128]{2,1,0:T(8,128)(2,1)}, u32[]{:S(2)}, u32[]{:S(2)}) async-start(bf16[128,128,128]{2,1,0:T(8,128)(2,1)} %bitcast.25), calls=%async_computation.2 | async-start | bytes 8388608 | tf_op jit(solution)/shard_map/all_to_all | solution.py:163
  174.5 57.3 %all-to-all-start.3 = ((bf16[128,128,128]{2,1,0:T(8,128)(2,1)}), bf16[128,128,128]{2,1,0:T(8,128)(2,1)}, u32[]{:S(2)}, u32[]{:S(2)}) async-start(bf16[128,128,128]{2,1,0:T(8,128)(2,1)} %bitcast.26), calls=%async_computation.3 | async-start | bytes 8388608 | tf_op jit(solution)/shard_map/all_to_all | solution.py:181

commit v15 on v14

--- a/solution.py
+++ b/solution.py
@@ -39,29 +39,31 @@
 
 
 def batch_kernel(slot_ref, *refs):
-    blocks = refs[:NSIG]
-    colloc_ref, points_ref, scale_ref, sites_ref, proj_ref, out_ref, rows_ref = refs[NSIG:]
-    for k in range(NSIG):
-        rows_ref[k * SH:(k + 1) * SH, :] = blocks[k][0]
-    values = colloc_ref[0]
+    per_step = (len(refs) - 7) // NSIG
+    blocks = refs[:NSIG * per_step]
+    colloc_ref, points_ref, scale_ref, sites_ref, proj_ref, out_ref, rows_ref = refs[NSIG * per_step:]
     weights = proj_ref[...]
-    field = lax.dot_general(
-        rows_ref[...], values, (((0,), (0,)), ((), ())), preferred_element_type=jnp.float32
-    ).astype(jnp.bfloat16)
-    projected = jnp.dot(weights, field, preferred_element_type=jnp.float32)
-    points = points_ref[0]
     sites = sites_ref[...]
-    dist_sq = (points[0:1, :] - sites[:, 0:1]) ** 2
-    dist_sq = dist_sq + (points[1:2, :] - sites[:, 1:2]) ** 2
-    dist_sq = dist_sq + (points[2:3, :] - sites[:, 2:3]) ** 2
-    charges = (projected * lax.rsqrt(dist_sq + smear_sq) * scale_ref[0]).astype(jnp.bfloat16)
-    spread_back = lax.dot_general(
-        weights, charges, (((0,), (0,)), ((), ())), preferred_element_type=jnp.float32
-    ).astype(jnp.bfloat16)
-    term = lax.dot_general(
-        values, spread_back, (((1,), (1,)), ((), ())), preferred_element_type=jnp.float32
-    )
-    out_ref[0] = term.astype(out_ref.dtype)
+    for t in range(per_step):
+        for k in range(NSIG):
+            rows_ref[k * SH:(k + 1) * SH, :] = blocks[t * NSIG + k][0]
+        values = colloc_ref[t]
+        field = lax.dot_general(
+            rows_ref[...], values, (((0,), (0,)), ((), ())), preferred_element_type=jnp.float32
+        ).astype(jnp.bfloat16)
+        projected = jnp.dot(weights, field, preferred_element_type=jnp.float32)
+        points = points_ref[t]
+        dist_sq = (points[0:1, :] - sites[:, 0:1]) ** 2
+        dist_sq = dist_sq + (points[1:2, :] - sites[:, 1:2]) ** 2
+        dist_sq = dist_sq + (points[2:3, :] - sites[:, 2:3]) ** 2
+        charges = (projected * lax.rsqrt(dist_sq + smear_sq) * scale_ref[t]).astype(jnp.bfloat16)
+        spread_back = lax.dot_general(
+            weights, charges, (((0,), (0,)), ((), ())), preferred_element_type=jnp.float32
+        ).astype(jnp.bfloat16)
+        term = lax.dot_general(
+            values, spread_back, (((1,), (1,)), ((), ())), preferred_element_type=jnp.float32
+        )
+        out_ref[t] = term.astype(out_ref.dtype)
 
 
 def batch_terms(replies, slot, colloc, grid_points, grid_weights, charge_sites, charge_proj, point_counts):
@@ -72,28 +74,32 @@
     scale = (grid_weights * live).reshape(batches, 1, total_points)
     sites = jnp.transpose(charge_sites)
 
-    def block_spec(k):
-        return pl.BlockSpec((1, SH, slab_width), lambda b, slot_ref: (slot_ref[b * NSIG + k], 0, 0))
+    per_step = 2 if batches % 2 == 0 else 1
+
+    def block_spec(i):
+        return pl.BlockSpec(
+            (1, SH, slab_width), lambda b, slot_ref: (slot_ref[b * per_step * NSIG + i], 0, 0)
+        )
 
     grid_spec = pltpu.PrefetchScalarGridSpec(
         num_scalar_prefetch=1,
-        grid=(batches,),
-        in_specs=[block_spec(k) for k in range(NSIG)]
+        grid=(batches // per_step,),
+        in_specs=[block_spec(i) for i in range(NSIG * per_step)]
         + [
-            pl.BlockSpec((1, func_rows, total_points), lambda b, slot_ref: (b, 0, 0)),
-            pl.BlockSpec((1, 3, total_points), lambda b, slot_ref: (b, 0, 0)),
-            pl.BlockSpec((1, 1, total_points), lambda b, slot_ref: (b, 0, 0)),
+            pl.BlockSpec((per_step, func_rows, total_points), lambda b, slot_ref: (b, 0, 0)),
+            pl.BlockSpec((per_step, 3, total_points), lambda b, slot_ref: (b, 0, 0)),
+            pl.BlockSpec((per_step, 1, total_points), lambda b, slot_ref: (b, 0, 0)),
             pl.BlockSpec((aux, 3), lambda b, slot_ref: (0, 0)),
             pl.BlockSpec((aux, slab_width), lambda b, slot_ref: (0, 0)),
         ],
-        out_specs=pl.BlockSpec((1, func_rows, slab_width), lambda b, slot_ref: (b, 0, 0)),
+        out_specs=pl.BlockSpec((per_step, func_rows, slab_width), lambda b, slot_ref: (b, 0, 0)),
         scratch_shapes=[pltpu.VMEM((func_rows, slab_width), jnp.bfloat16)],
     )
     return pl.pallas_call(
         batch_kernel,
         grid_spec=grid_spec,
         out_shape=jax.ShapeDtypeStruct((batches, func_rows, slab_width), jnp.bfloat16),
-    )(slot, *([replies] * NSIG), colloc, grid_points, scale, sites, charge_proj)
+    )(slot, *([replies] * (NSIG * per_step)), colloc, grid_points, scale, sites, charge_proj)
 
 
 def product_kernel(coeff_ref, window_ref, out_ref):

time: 238 us -> 238 us (level)
  no operation moved by 1% of the time
where the time goes in v15:
time: 238 us; the launch traced here: 237 us
  waiting for transfers between devices  146 us (61%)
  starting transfers between devices  42.9 us (18%)
  Pallas kernels  24.7 us (10%)
  local copies, waits for them, and re-layouts  14.7 us (6%)
  other arithmetic  4.51 us (2%)
  matrix products  4.47 us (2%)
    all_to_all x1, waiting for transfers between devices, on_device(): lax.all_to_all(tiles.reshape(owners, capacity * SH, slab_width), ('row',...  52.1 us
    all_to_all x1, waiting for transfers between devices, on_device(): lax.all_to_all(found.reshape(owners, capacity * SH, slab_width), ('row',...  49.2 us
    all_to_all x1, waiting for transfers between devices, on_device(): lax.all_to_all(partial.reshape(col_count, own_rows, slab_width), 'col', s...  39 us
    pallas_call x1, Pallas kernels, batch_terms(): pl.pallas_call(batch_kernel, grid_spec=grid_spec, out_shape=jax.ShapeDtyp...  15.7 us
    all_to_all x1, starting transfers between devices, on_device(): lax.all_to_all(found.reshape(owners, capacity * SH, slab_width), ('row',...  15.3 us
    all_to_all x1, starting transfers between devices, on_device(): lax.all_to_all(wanted.reshape(owners, capacity), ('row', 'col'), split_ax...  11.4 us
    pallas_call x1, Pallas kernels, slab_product(): pl.pallas_call(product_kernel, grid=(rows // block,), in_specs=[pl.BlockS...  8.92 us
    all_to_all x1, starting transfers between devices, on_device(): lax.all_to_all(partial.reshape(col_count, own_rows, slab_width), 'col', s...  7.1 us
  transfers between devices with their start and end apart: 8, of which 4 were waited for; matrix products, arithmetic and copies ran while one was open for 4% of the time, Pallas kernels for 4%

profile of v15, /device:TPU:1, one launch (start us, length us, event | category | flops | bytes accessed | tf_op | source)
XLA Modules:
  0.0 237.1 jit_solution(5854638597089160249)
XLA Ops:
  0.0 1.0 slice.3
  1.0 0.2 copy.29
  1.2 0.7 collective-permute-start
  1.9 0.7 collective-permute-start.1
  2.6 1.3 collective-permute-start.2
  3.9 0.7 broadcast_remainder_fusion
  4.6 0.7 compare_and_fusion
  5.3 0.1 div.28
  5.4 0.1 rem.34
  5.4 0.1 ne.65
  5.5 0.1 div.27
  5.6 0.1 and.29
  5.7 0.1 fusion.2
  5.8 0.2 reduce_window_sum.11
  6.0 0.0 collective-permute-done
  6.0 0.0 collective-permute-done.1
  6.0 5.4 %collective-permute-done.2 = bf16[128,1280]{0,1:T(8,128)(2,1)S(1)} collective-permute-done((bf16[128,1280]{0,1:T(8,128)(2,1)S(1)}, bf16[128,1280]{0,1:T(8,128)(2,1)S(1)}, u32[]{:S(2)}, u32[]{:S(2)}) %collective-permute-start.2) | collective-permute-done | bytes 327712 | tf_op jit(solution)/shard_map/ppermute | solution.py:26
  11.4 0.1 select_select_fusion
  11.4 1.3 collective-permute-start.3
  12.8 0.2 select_reduce_fusion.1
  12.9 1.0 scatter_custom_fusion
  13.9 0.8 all_to_all.15
  14.7 11.4 %all-to-all-start = ((s32[128,1,2]{2,1,0:T(1,128)}), s32[128,1,2]{2,1,0:T(1,128)S(1)}, u32[]{:S(2)}, u32[]{:S(2)}) async-start(s32[128,1,2]{2,1,0:T(1,128)} %bitcast.2), calls=%async_computation | async-start | bytes 131072 | tf_op jit(solution)/shard_map/all_to_all | solution.py:158
  26.2 0.0 collective-permute-done.3
  26.2 0.8 select_bitcast_fusion.window_ref
  26.9 8.9 %shard_map.82 = f32[6144,128]{1,0:T(8,128)} custom-call(bf16[6144,1280]{1,0:T(8,128)(2,1)} %coeff_ref.1, bf16[1280,128]{1,0:T(8,128)(2,1)} %select_bitcast_fusion.window_ref), custom_call_target="tpu_custom_call" | custom-call | tf_op jit(solution)/shard_map/pallas_call | solution.py:113
  35.9 7.1 %all-to-all-start.1 = ((f32[16,384,128]{2,1,0:T(8,128)}), f32[16,384,128]{2,1,0:T(8,128)S(1)}, u32[]{:S(2)}, u32[]{:S(2)}) async-start(f32[16,384,128]{2,1,0:T(8,128)} %bitcast.27), calls=%async_computation.1 | async-start | bytes 6291456 | tf_op jit(solution)/shard_map/all_to_all | solution.py:163
  43.0 0.5 broadcast.176
  43.5 1.0 fusion.12
  44.5 0.1 reshape.180
  44.6 39.0 %all-to-all-done.1 = f32[16,384,128]{2,1,0:T(8,128)S(1)} async-done(((f32[16,384,128]{2,1,0:T(8,128)}), f32[16,384,128]{2,1,0:T(8,128)S(1)}, u32[]{:S(2)}, u32[]{:S(2)}) %all-to-all-start.1) | async-done | bytes 3145760 | tf_op jit(solution)/shard_map/all_to_all | solution.py:163
  83.6 0.1 reduce_sum.33
  83.8 3.1 %gather_fusion = bf16[256,64,128]{2,1,0:T(8,128)(2,1)} fusion(bf16[6,64,128]{2,1,0:T(8,128)(2,1)S(1)} %bitcast.23, s32[1024]{0:T(1024)S(1)} %pad_clamp_fusion.1), kind=kCustom, calls=%fused_computation | custom fusion | bytes 8389632 | tf_op jit(solution)/shard_map/gather | solution.py:168
  86.8 15.3 %all-to-all-start.2 = ((bf16[128,128,128]{2,1,0:T(8,128)(2,1)}), bf16[128,128,128]{2,1,0:T(8,128)(2,1)}, u32[]{:S(2)}, u32[]{:S(2)}) async-start(bf16[128,128,128]{2,1,0:T(8,128)(2,1)} %bitcast.25), calls=%async_computation.2 | async-start | bytes 8388608 | tf_op jit(solution)/shard_map/all_to_all | solution.py:169
  102.1 0.9 copy.25
  103.0 0.7 copy.26.refs_33_
  103.7 0.1 fusion.3
  103.8 0.6 reshape.173.refs_34_
  104.4 0.5 broadcast_clamp_fusion
  104.9 0.1 select_reduce_fusion
  105.0 49.2 %all-to-all-done.2 = bf16[128,128,128]{2,1,0:T(8,128)(2,1)} async-done(((bf16[128,128,128]{2,1,0:T(8,128)(2,1)}), bf16[128,128,128]{2,1,0:T(8,128)(2,1)}, u32[]{:S(2)}, u32[]{:S(2)}) %all-to-all-start.2) | async-done | bytes 4194336 | tf_op jit(solution)/shard_map/all_to_all | solution.py:169
  154.2 15.7 %shard_map.83 = bf16[8,1024,128]{2,1,0:T(8,128)(2,1)} custom-call(s32[128]{0:T(128)} %get-tuple-element.9.slot_ref, ...), custom_call_target="tpu_custom_call" | custom-call | tf_op jit(solution)/shard_map/pallas_call | solution.py:98
  170.0 4.6 %gather_fusion.1 = bf16[256,64,128]{2,1,0:T(8,128)(2,1)} fusion(bf16[128,64,128]{2,1,0:T(8,128)(2,1)} %bitcast.24, s32[1024]{0:T(1024)S(1)} %pad_clamp_fusion), kind=kCustom, calls=%fused_computation.1 | custom fusion | bytes 8389632 | tf_op jit(solution)/shard_map/gather | solution.py:186
  174.6 5.1 %all-to-all-start.3 = ((bf16[128,128,128]{2,1,0:T(8,128)(2,1)}), bf16[128,128,128]{2,1,0:T(8,128)(2,1)}, u32[]{:S(2)}, u32[]{:S(2)}) async-start(bf16[128,128,128]{2,1,0:T(8,128)(2,1)} %bitcast.26), calls=%async_computation.3 | async-start | bytes 8388608 | tf_op jit(solution)/shard_map/all_to_all | solution.py:187
  179.7 0.1 eq.68
  179.8 52.1 %all-to-all-done.3 = bf16[128,128,128]{2,1,0:T(8,128)(2,1)} async-done(((bf16[128,128,128]{2,1,0:T(8,128)(2,1)}), bf16[128,128,128]{2,1,0:T(8,128)(2,1)}, u32[]{:S(2)}, u32[]{:S(2)}) %all-to-all-start.3) | async-done | bytes 4194336 | tf_op jit(solution)/shard_map/all_to_all | solution.py:187
  231.9 4.5 %fusion = f32[6,64,128]{2,0,1:T(8,128)S(1)} fusion(bf16[256,64,128]{2,1,0:T(8,128)(2,1)} %bitcast.14, s32[256]{0:T(256)S(1)} %eq.68), kind=kOutput, calls=%fused_computation.3 | convolution fusion | flops 25167360 | bytes 4391936 | tf_op jit(solution)/shard_map/js,sfc->jfc/dot_general | solution.py:195
  236.4 0.7 copy.28
  (14 shorter events, 0.1 us)
Async XLA Ops:
  1.2 4.8 %collective-permute-start = (bf16[128,1280]{0,1:T(8,128)(2,1)S(1)}, bf16[128,1280]{0,1:T(8,128)(2,1)S(1)}, u32[]{:S(2)}, u32[]{:S(2)}) collective-permute-start(bf16[128,1280]{0,1:T(8,128)(2,1)S(1)} %copy.29), channel_id=1, source_target_pairs={{0,96},{1,97},{2,98},{3,99},{4,100},{5,101},{6,102},{7,103},{8,104... | collective-permute-start | bytes 983048 | tf_op jit(solution)/shard_map/ppermute | solution.py:26
  1.9 4.1 %collective-permute-start.1 = (bf16[128,1280]{0,1:T(8,128)(2,1)S(1)}, bf16[128,1280]{0,1:T(8,128)(2,1)S(1)}, u32[]{:S(2)}, u32[]{:S(2)}) collective-permute-start(bf16[128,1280]{0,1:T(8,128)(2,1)S(1)} %copy.29), channel_id=1, source_target_pairs={{0,32},{1,33},{2,34},{3,35},{4,36},{5,37},{6,38},{7,39},{8,40},{9,... | collective-permute-start | bytes 983048 | tf_op jit(solution)/shard_map/ppermute | solution.py:26
  2.6 8.8 %collective-permute-start.2 = (bf16[128,1280]{0,1:T(8,128)(2,1)S(1)}, bf16[128,1280]{0,1:T(8,128)(2,1)S(1)}, u32[]{:S(2)}, u32[]{:S(2)}) collective-permute-start(bf16[128,1280]{0,1:T(8,128)(2,1)S(1)} %copy.29), channel_id=1, source_target_pairs={{0,16},{1,17},{2,18},{3,19},{4,20},{5,21},{6,22},{7,23},{8,24},{9,... | collective-permute-start | bytes 983048 | tf_op jit(solution)/shard_map/ppermute | solution.py:26
  11.4 14.7 %collective-permute-start.3 = (bf16[128,1280]{0,1:T(8,128)(2,1)S(1)}, bf16[128,1280]{0,1:T(8,128)(2,1)S(1)}, u32[]{:S(2)}, u32[]{:S(2)}) collective-permute-start(bf16[128,1280]{0,1:T(8,128)(2,1)S(1)} %select_select_fusion), channel_id=1, source_target_pairs={{16,48},{32,64},{96,112},{0,80},{17,49},{33,65},{97,113},{1,81},{1... | collective-permute-start | bytes 983048 | tf_op jit(solution)/shard_map/ppermute | solution.py:30
  14.7 21.2 %all-to-all-start = ((s32[128,1,2]{2,1,0:T(1,128)}), s32[128,1,2]{2,1,0:T(1,128)S(1)}, u32[]{:S(2)}, u32[]{:S(2)}) async-start(s32[128,1,2]{2,1,0:T(1,128)} %bitcast.2), calls=%async_computation | async-start | bytes 131072 | tf_op jit(solution)/shard_map/all_to_all | solution.py:158
  35.9 47.7 %all-to-all-start.1 = ((f32[16,384,128]{2,1,0:T(8,128)}), f32[16,384,128]{2,1,0:T(8,128)S(1)}, u32[]{:S(2)}, u32[]{:S(2)}) async-start(f32[16,384,128]{2,1,0:T(8,128)} %bitcast.27), calls=%async_computation.1 | async-start | bytes 6291456 | tf_op jit(solution)/shard_map/all_to_all | solution.py:163
  86.8 15.3 %copy-start.2 = (f32[3,512]{1,0:T(4,128)S(1)}, f32[3,512]{1,0:T(4,128)}, u32[]{:S(2)}) copy-start(f32[3,512]{1,0:T(4,128)} %param.12) | copy-start | bytes 18436
  86.8 16.2 %copy-start = (f32[8,3,512]{2,0,1:T(8,128)S(1)}, f32[8,3,512]{2,0,1:T(8,128)}, u32[]{:S(2)}) copy-start(f32[8,3,512]{2,0,1:T(8,128)} %param.10) | copy-start | bytes 147460
  86.8 16.9 %copy-start.1 = (f32[8,512]{1,0:T(8,128)S(1)}, f32[8,512]{1,0:T(8,128)}, u32[]{:S(2)}) copy-start(f32[8,512]{1,0:T(8,128)} %param.11) | copy-start | bytes 49156
  86.8 16.9 %copy-start.3 = (s32[8]{0:T(128)S(1)}, s32[8]{0:T(128)}, u32[]{:S(2)}) copy-start(s32[8]{0:T(128)} %param.15) | copy-start | bytes 100
  86.8 67.4 %all-to-all-start.2 = ((bf16[128,128,128]{2,1,0:T(8,128)(2,1)}), bf16[128,128,128]{2,1,0:T(8,128)(2,1)}, u32[]{:S(2)}, u32[]{:S(2)}) async-start(bf16[128,128,128]{2,1,0:T(8,128)(2,1)} %bitcast.25), calls=%async_computation.2 | async-start | bytes 8388608 | tf_op jit(solution)/shard_map/all_to_all | solution.py:169
  174.6 57.3 %all-to-all-start.3 = ((bf16[128,128,128]{2,1,0:T(8,128)(2,1)}), bf16[128,128,128]{2,1,0:T(8,128)(2,1)}, u32[]{:S(2)}, u32[]{:S(2)}) async-start(bf16[128,128,128]{2,1,0:T(8,128)(2,1)} %bitcast.26), calls=%async_computation.3 | async-start | bytes 8388608 | tf_op jit(solution)/shard_map/all_to_all | solution.py:187

commit v16 on v14

--- a/solution.py
+++ b/solution.py
@@ -103,7 +103,7 @@
 def slab_product(occ_coeffs, window):
     rows, depth = occ_coeffs.shape
     width = window.shape[0]
-    block = 3072 if rows % 3072 == 0 else rows
+    block = 2048 if rows % 2048 == 0 else rows
     return pl.pallas_call(
         product_kernel,
         grid=(rows // block,),

time: 238 us -> 239 us (level)
  no operation moved by 1% of the time
where the time goes in v16:
time: 239 us; the launch traced here: 238 us
  waiting for transfers between devices  146 us (61%)
  starting transfers between devices  42.9 us (18%)
  Pallas kernels  25.5 us (11%)
  local copies, waits for them, and re-layouts  14.7 us (6%)
  other arithmetic  4.51 us (2%)
  matrix products  4.47 us (2%)
    all_to_all x1, waiting for transfers between devices, on_device(): lax.all_to_all(tiles.reshape(owners, capacity * SH, slab_width), ('row',...  52.1 us
    all_to_all x1, waiting for transfers between devices, on_device(): lax.all_to_all(found.reshape(owners, capacity * SH, slab_width), ('row',...  49.2 us
    all_to_all x1, waiting for transfers between devices, on_device(): lax.all_to_all(partial.reshape(col_count, own_rows, slab_width), 'col', s...  39 us
    pallas_call x1, Pallas kernels, batch_terms(): pl.pallas_call(batch_kernel, grid_spec=grid_spec, out_shape=jax.ShapeDtyp...  15.7 us
    all_to_all x1, starting transfers between devices, on_device(): lax.all_to_all(found.reshape(owners, capacity * SH, slab_width), ('row',...  15.3 us
    all_to_all x1, starting transfers between devices, on_device(): lax.all_to_all(wanted.reshape(owners, capacity), ('row', 'col'), split_ax...  11.4 us
    pallas_call x1, Pallas kernels, slab_product(): pl.pallas_call(product_kernel, grid=(rows // block,), in_specs=[pl.BlockS...  9.84 us
    all_to_all x1, starting transfers between devices, on_device(): lax.all_to_all(partial.reshape(col_count, own_rows, slab_width), 'col', s...  7.1 us
  transfers between devices with their start and end apart: 8, of which 4 were waited for; matrix products, arithmetic and copies ran while one was open for 4% of the time, Pallas kernels for 4%

profile of v16, /device:TPU:1, one launch (start us, length us, event | category | flops | bytes accessed | tf_op | source)
XLA Modules:
  0.0 238.0 jit_solution(4402243700000574810)
XLA Ops:
  0.0 1.0 slice.3
  1.0 0.2 copy.29
  1.2 0.7 collective-permute-start
  1.9 0.7 collective-permute-start.1
  2.6 1.3 collective-permute-start.2
  3.9 0.7 broadcast_remainder_fusion
  4.6 0.7 compare_and_fusion
  5.3 0.1 div.28
  5.4 0.1 rem.34
  5.4 0.1 ne.65
  5.5 0.1 div.27
  5.6 0.1 and.29
  5.7 0.1 fusion.2
  5.8 0.2 reduce_window_sum.11
  6.0 0.0 collective-permute-done
  6.0 0.0 collective-permute-done.1
  6.0 5.4 %collective-permute-done.2 = bf16[128,1280]{0,1:T(8,128)(2,1)S(1)} collective-permute-done((bf16[128,1280]{0,1:T(8,128)(2,1)S(1)}, bf16[128,1280]{0,1:T(8,128)(2,1)S(1)}, u32[]{:S(2)}, u32[]{:S(2)}) %collective-permute-start.2) | collective-permute-done | bytes 327712 | tf_op jit(solution)/shard_map/ppermute | solution.py:26
  11.4 0.1 select_select_fusion
  11.4 1.3 collective-permute-start.3
  12.8 0.2 select_reduce_fusion.1
  12.9 1.0 scatter_custom_fusion
  13.9 0.8 all_to_all.15
  14.7 11.4 %all-to-all-start = ((s32[128,1,2]{2,1,0:T(1,128)}), s32[128,1,2]{2,1,0:T(1,128)S(1)}, u32[]{:S(2)}, u32[]{:S(2)}) async-start(s32[128,1,2]{2,1,0:T(1,128)} %bitcast.2), calls=%async_computation | async-start | bytes 131072 | tf_op jit(solution)/shard_map/all_to_all | solution.py:152
  26.2 0.8 select_bitcast_fusion.window_ref
  26.9 9.8 %shard_map.82 = f32[6144,128]{1,0:T(8,128)} custom-call(bf16[6144,1280]{1,0:T(8,128)(2,1)} %coeff_ref.1, bf16[1280,128]{1,0:T(8,128)(2,1)} %select_bitcast_fusion.window_ref), custom_call_target="tpu_custom_call" | custom-call | tf_op jit(solution)/shard_map/pallas_call | solution.py:107
  36.8 0.0 all-to-all-done
  36.8 7.1 %all-to-all-start.1 = ((f32[16,384,128]{2,1,0:T(8,128)}), f32[16,384,128]{2,1,0:T(8,128)S(1)}, u32[]{:S(2)}, u32[]{:S(2)}) async-start(f32[16,384,128]{2,1,0:T(8,128)} %bitcast.27), calls=%async_computation.1 | async-start | bytes 6291456 | tf_op jit(solution)/shard_map/all_to_all | solution.py:157
  43.9 0.5 broadcast.176
  44.4 1.0 fusion.12
  45.4 0.1 reshape.180
  45.6 39.0 %all-to-all-done.1 = f32[16,384,128]{2,1,0:T(8,128)S(1)} async-done(((f32[16,384,128]{2,1,0:T(8,128)}), f32[16,384,128]{2,1,0:T(8,128)S(1)}, u32[]{:S(2)}, u32[]{:S(2)}) %all-to-all-start.1) | async-done | bytes 3145760 | tf_op jit(solution)/shard_map/all_to_all | solution.py:157
  84.5 0.1 reduce_sum.33
  84.7 3.1 %gather_fusion = bf16[256,64,128]{2,1,0:T(8,128)(2,1)} fusion(bf16[6,64,128]{2,1,0:T(8,128)(2,1)S(1)} %bitcast.23, s32[1024]{0:T(1024)S(1)} %pad_clamp_fusion.1), kind=kCustom, calls=%fused_computation | custom fusion | bytes 8389632 | tf_op jit(solution)/shard_map/gather | solution.py:162
  87.7 15.3 %all-to-all-start.2 = ((bf16[128,128,128]{2,1,0:T(8,128)(2,1)}), bf16[128,128,128]{2,1,0:T(8,128)(2,1)}, u32[]{:S(2)}, u32[]{:S(2)}) async-start(bf16[128,128,128]{2,1,0:T(8,128)(2,1)} %bitcast.25), calls=%async_computation.2 | async-start | bytes 8388608 | tf_op jit(solution)/shard_map/all_to_all | solution.py:163
  103.1 0.9 copy.25
  103.9 0.7 copy.26.refs_17_
  104.6 0.1 fusion.3
  104.7 0.6 reshape.173.refs_18_
  105.3 0.5 broadcast_clamp_fusion
  105.8 0.1 select_reduce_fusion
  105.9 49.2 %all-to-all-done.2 = bf16[128,128,128]{2,1,0:T(8,128)(2,1)} async-done(((bf16[128,128,128]{2,1,0:T(8,128)(2,1)}), bf16[128,128,128]{2,1,0:T(8,128)(2,1)}, u32[]{:S(2)}, u32[]{:S(2)}) %all-to-all-start.2) | async-done | bytes 4194336 | tf_op jit(solution)/shard_map/all_to_all | solution.py:163
  155.1 15.7 %shard_map.83 = bf16[8,1024,128]{2,1,0:T(8,128)(2,1)} custom-call(s32[128]{0:T(128)} %get-tuple-element.9.slot_ref, bf16[256,64,128]{2,1,0:T(8,128)(2,1)} %bitcast.8.refs_0_.refs_1_.refs_2_.refs_3_.refs_4_.refs_5_.refs_6_.refs_7_.refs_8_.refs_9_.refs_10_.refs_11_.refs_12_.refs_13_.refs_14_.refs_15_, ...), custom_call_target="tpu_custom_call" | custom-call | tf_op jit(solution)/shard_map/pallas_call | solution.py:92
  170.8 4.6 %gather_fusion.1 = bf16[256,64,128]{2,1,0:T(8,128)(2,1)} fusion(bf16[128,64,128]{2,1,0:T(8,128)(2,1)} %bitcast.24, s32[1024]{0:T(1024)S(1)} %pad_clamp_fusion), kind=kCustom, calls=%fused_computation.1 | custom fusion | bytes 8389632 | tf_op jit(solution)/shard_map/gather | solution.py:180
  175.4 5.1 %all-to-all-start.3 = ((bf16[128,128,128]{2,1,0:T(8,128)(2,1)}), bf16[128,128,128]{2,1,0:T(8,128)(2,1)}, u32[]{:S(2)}, u32[]{:S(2)}) async-start(bf16[128,128,128]{2,1,0:T(8,128)(2,1)} %bitcast.26), calls=%async_computation.3 | async-start | bytes 8388608 | tf_op jit(solution)/shard_map/all_to_all | solution.py:181
  180.5 0.1 eq.68
  180.7 52.1 %all-to-all-done.3 = bf16[128,128,128]{2,1,0:T(8,128)(2,1)} async-done(((bf16[128,128,128]{2,1,0:T(8,128)(2,1)}), bf16[128,128,128]{2,1,0:T(8,128)(2,1)}, u32[]{:S(2)}, u32[]{:S(2)}) %all-to-all-start.3) | async-done | bytes 4194336 | tf_op jit(solution)/shard_map/all_to_all | solution.py:181
  232.8 4.5 %fusion = f32[6,64,128]{2,0,1:T(8,128)S(1)} fusion(bf16[256,64,128]{2,1,0:T(8,128)(2,1)} %bitcast.14, s32[256]{0:T(256)S(1)} %eq.68), kind=kOutput, calls=%fused_computation.3 | convolution fusion | flops 25167360 | bytes 4391936 | tf_op jit(solution)/shard_map/js,sfc->jfc/dot_general | solution.py:189
  237.2 0.7 copy.28
  (14 shorter events, 0.1 us)
Async XLA Ops:
  1.2 4.8 %collective-permute-start = (bf16[128,1280]{0,1:T(8,128)(2,1)S(1)}, bf16[128,1280]{0,1:T(8,128)(2,1)S(1)}, u32[]{:S(2)}, u32[]{:S(2)}) collective-permute-start(bf16[128,1280]{0,1:T(8,128)(2,1)S(1)} %copy.29), channel_id=1, source_target_pairs={{0,96},{1,97},{2,98},{3,99},{4,100},{5,101},{6,102},{7,103},{8,104... | collective-permute-start | bytes 983048 | tf_op jit(solution)/shard_map/ppermute | solution.py:26
  1.9 4.1 %collective-permute-start.1 = (bf16[128,1280]{0,1:T(8,128)(2,1)S(1)}, bf16[128,1280]{0,1:T(8,128)(2,1)S(1)}, u32[]{:S(2)}, u32[]{:S(2)}) collective-permute-start(bf16[128,1280]{0,1:T(8,128)(2,1)S(1)} %copy.29), channel_id=1, source_target_pairs={{0,32},{1,33},{2,34},{3,35},{4,36},{5,37},{6,38},{7,39},{8,40},{9,... | collective-permute-start | bytes 983048 | tf_op jit(solution)/shard_map/ppermute | solution.py:26
  2.6 8.8 %collective-permute-start.2 = (bf16[128,1280]{0,1:T(8,128)(2,1)S(1)}, bf16[128,1280]{0,1:T(8,128)(2,1)S(1)}, u32[]{:S(2)}, u32[]{:S(2)}) collective-permute-start(bf16[128,1280]{0,1:T(8,128)(2,1)S(1)} %copy.29), channel_id=1, source_target_pairs={{0,16},{1,17},{2,18},{3,19},{4,20},{5,21},{6,22},{7,23},{8,24},{9,... | collective-permute-start | bytes 983048 | tf_op jit(solution)/shard_map/ppermute | solution.py:26
  11.4 14.7 %collective-permute-start.3 = (bf16[128,1280]{0,1:T(8,128)(2,1)S(1)}, bf16[128,1280]{0,1:T(8,128)(2,1)S(1)}, u32[]{:S(2)}, u32[]{:S(2)}) collective-permute-start(bf16[128,1280]{0,1:T(8,128)(2,1)S(1)} %select_select_fusion), channel_id=1, source_target_pairs={{16,48},{32,64},{96,112},{0,80},{17,49},{33,65},{97,113},{1,81},{1... | collective-permute-start | bytes 983048 | tf_op jit(solution)/shard_map/ppermute | solution.py:30
  14.7 22.1 %all-to-all-start = ((s32[128,1,2]{2,1,0:T(1,128)}), s32[128,1,2]{2,1,0:T(1,128)S(1)}, u32[]{:S(2)}, u32[]{:S(2)}) async-start(s32[128,1,2]{2,1,0:T(1,128)} %bitcast.2), calls=%async_computation | async-start | bytes 131072 | tf_op jit(solution)/shard_map/all_to_all | solution.py:152
  36.8 47.7 %all-to-all-start.1 = ((f32[16,384,128]{2,1,0:T(8,128)}), f32[16,384,128]{2,1,0:T(8,128)S(1)}, u32[]{:S(2)}, u32[]{:S(2)}) async-start(f32[16,384,128]{2,1,0:T(8,128)} %bitcast.27), calls=%async_computation.1 | async-start | bytes 6291456 | tf_op jit(solution)/shard_map/all_to_all | solution.py:157
  87.7 15.3 %copy-start.2 = (f32[3,512]{1,0:T(4,128)S(1)}, f32[3,512]{1,0:T(4,128)}, u32[]{:S(2)}) copy-start(f32[3,512]{1,0:T(4,128)} %param.12) | copy-start | bytes 18436
  87.7 16.2 %copy-start = (f32[8,3,512]{2,0,1:T(8,128)S(1)}, f32[8,3,512]{2,0,1:T(8,128)}, u32[]{:S(2)}) copy-start(f32[8,3,512]{2,0,1:T(8,128)} %param.10) | copy-start | bytes 147460
  87.7 16.9 %copy-start.1 = (f32[8,512]{1,0:T(8,128)S(1)}, f32[8,512]{1,0:T(8,128)}, u32[]{:S(2)}) copy-start(f32[8,512]{1,0:T(8,128)} %param.11) | copy-start | bytes 49156
  87.7 16.9 %copy-start.3 = (s32[8]{0:T(128)S(1)}, s32[8]{0:T(128)}, u32[]{:S(2)}) copy-start(s32[8]{0:T(128)} %param.15) | copy-start | bytes 100
  87.7 67.4 %all-to-all-start.2 = ((bf16[128,128,128]{2,1,0:T(8,128)(2,1)}), bf16[128,128,128]{2,1,0:T(8,128)(2,1)}, u32[]{:S(2)}, u32[]{:S(2)}) async-start(bf16[128,128,128]{2,1,0:T(8,128)(2,1)} %bitcast.25), calls=%async_computation.2 | async-start | bytes 8388608 | tf_op jit(solution)/shard_map/all_to_all | solution.py:163
  175.4 57.3 %all-to-all-start.3 = ((bf16[128,128,128]{2,1,0:T(8,128)(2,1)}), bf16[128,128,128]{2,1,0:T(8,128)(2,1)}, u32[]{:S(2)}, u32[]{:S(2)}) async-start(bf16[128,128,128]{2,1,0:T(8,128)(2,1)} %bitcast.26), calls=%async_computation.3 | async-start | bytes 8388608 | tf_op jit(solution)/shard_map/all_to_all | solution.py:181
